TPU v7x, 512 devices: a whole 4x8x8 slice. The times are simulated.
512 devices in a mesh: freq: 8 (over x, core), geo: 64 (over z, y).
Axes of the slice: x: 4, y: 8, z: 8, core: 2. Of those that a mesh axis runs over, the one named last changes fastest.
Arguments:
- energy: float32 [256, 48, 36, 128], P('geo', 'freq'), may hold values from 0.1 to 1.5
- water_depth: float32 [256, 128], P('geo'), may hold values from 0.5 to 4
- wet_mask: int32 [256, 128], P('geo'), may hold values 0 or 1
- vegetation: int32 [256, 128], P('geo'), may hold values 0 or 1
- canopy: float32 [256, 128], P('geo'), may hold values from 0.004 to 0.04
- quad_offsets: int32 [4], replicated, may hold values from 1 to 3, as said below
- quad_weights: float32 [2], replicated, may hold values from 0.2 to 0.8
Outputs:
- energy_next: float32 [256, 48, 36, 128], P('geo', 'freq')
- orbital: float32 [256, 128], P('geo')
Inputs may be any that keep to these rules, and one draw needn't show every extreme that they name: `quad_offsets`: offsets a and the two direction turns lie in 1 .. 3; the lower frequency offset b equals 3 in every draw.
All inputs are finite; a program needn't handle non-finite values. No bound on the sum of `wet_mask` or of `vegetation` on one device may be relied on, other than what follows from the above.
Results may differ from a plain program's by a relative error of at most 0.00002.
Values sent between devices are 32-bit elements; how exact they have to be, the bound alone decides.
No kernel may reach another device: no remote copies, remote signals or barrier semaphores. Data moves between devices by JAX's collectives and lax.ppermute only.
A program may use at most 64 MiB of HBM per device.

v0:
```python
import math

import jax
import jax.numpy as jnp
from jax import lax
from jax.sharding import PartitionSpec as P

FH = 4
SUBSTEPS = 8


gravity = 9.81
base_freq = 0.03
freq_ratio = 1.05
cell_size = 20.0
sub_step = 2.0
coupling = 0.01
coef_plus = 0.4096
coef_minus = 3.1605
coef_both = 2.589


def padded(block, sides, width):
    for axis, dim in sides:
        count = lax.axis_size(axis)
        forward = [(i, i + 1) for i in range(count - 1)]
        backward = [(target, source) for source, target in forward]
        low = lax.ppermute(
            lax.slice_in_dim(block, block.shape[dim] - width, None, axis=dim), axis, forward
        )
        high = lax.ppermute(lax.slice_in_dim(block, 0, width, axis=dim), axis, backward)
        block = jnp.concatenate([low, block, high], axis=dim)
    return block


def physics(radian_freq, water_depth, dir_count):
    square = (radian_freq * radian_freq)[None, :, None]
    column = water_depth[:, None, :]
    depth_ratio = square * column / gravity
    depth_wave = depth_ratio / jnp.sqrt(jnp.tanh(depth_ratio))
    group_speed = (
        radian_freq[None, :, None]
        * column
        / depth_wave
        * (0.5 + depth_wave / jnp.sinh(2.0 * depth_wave))
    )
    orbit_weight = (
        square
        / jnp.sinh(depth_wave) ** 2
        * (radian_freq * (freq_ratio - 1.0))[None, :, None]
        * (2.0 * math.pi / dir_count)
    )
    return (group_speed, orbit_weight)


def angles_of(dir_count):
    angles = (jnp.arange(dir_count, dtype=jnp.float32) + 0.5) * (2.0 * math.pi / dir_count)
    return (jnp.cos(angles), jnp.sin(angles))


def shifted(doubled, freq_off, dir_off, count):
    dir_count = doubled.shape[2] // 2
    starts = (
        jnp.zeros((), jnp.int32),
        freq_off + FH,
        dir_off % dir_count,
        jnp.zeros((), jnp.int32),
    )
    return lax.dynamic_slice(
        doubled, starts, (doubled.shape[0], count, dir_count, doubled.shape[3])
    )


def interaction(extended, masked, quad_offsets, quad_weights):
    count = masked.shape[1]
    doubled = jnp.concatenate([extended, extended], axis=2)
    up_bins, down_bins, up_turn, down_turn = (
        quad_offsets[0],
        quad_offsets[1],
        quad_offsets[2],
        quad_offsets[3],
    )
    weight_up, weight_down = (quad_weights[0], quad_weights[1])
    upper = weight_up * shifted(doubled, up_bins, up_turn, count) + (1.0 - weight_up) * shifted(
        doubled, up_bins + 1, up_turn, count
    )
    lower = weight_down * shifted(doubled, -down_bins, -down_turn, count) + (
        1.0 - weight_down
    ) * shifted(doubled, -down_bins - 1, -down_turn, count)
    return coupling * (
        masked * masked * (coef_plus * upper + coef_minus * lower)
        - coef_both * masked * upper * lower
    )


def redistribute(extended, transfer, quad_offsets, quad_weights):
    count = transfer.shape[1]
    doubled = jnp.concatenate([extended, extended], axis=2)
    up_bins, down_bins, up_turn, down_turn = (
        quad_offsets[0],
        quad_offsets[1],
        quad_offsets[2],
        quad_offsets[3],
    )
    weight_up, weight_down = (quad_weights[0], quad_weights[1])
    gained = weight_up * shifted(doubled, -up_bins, -up_turn, count) + (1.0 - weight_up) * shifted(
        doubled, -up_bins - 1, -up_turn, count
    )
    gained = (
        gained
        + weight_down * shifted(doubled, down_bins, down_turn, count)
        + (1.0 - weight_down) * shifted(doubled, down_bins + 1, down_turn, count)
    )
    return gained - 2.0 * transfer


def east_west(east_flux, cosines):
    zeros = jnp.zeros_like(east_flux[..., :1])
    behind = jnp.concatenate([zeros, east_flux[..., :-1]], axis=-1)
    ahead = jnp.concatenate([east_flux[..., 1:], zeros], axis=-1)
    east_going = (cosines > 0.0).astype(jnp.float32)[None, None, :, None]
    return east_going * (east_flux - behind) + (1.0 - east_going) * (ahead - east_flux)


def body(energy, water_depth, wet_mask, vegetation, canopy, quad_offsets, quad_weights):
    tile_rows, freq_count, dir_count, tile_cols = energy.shape
    wet_field = wet_mask.astype(jnp.float32)
    veg_field = vegetation.astype(jnp.float32)
    wet_four = wet_field[:, None, None, :]
    masked = wet_four * energy
    first_bin = lax.axis_index("freq") * freq_count
    bin_index = (first_bin + jnp.arange(freq_count, dtype=jnp.int32)).astype(jnp.float32)
    radian_freq = 2.0 * math.pi * base_freq * jnp.power(freq_ratio, bin_index)
    group_speed, orbit_weight = physics(radian_freq, water_depth, dir_count)
    partial_value = jnp.sum(orbit_weight * jnp.sum(energy, axis=2), axis=1)
    orbital = jnp.sqrt(lax.psum(partial_value, "freq"))
    full_step = SUBSTEPS * sub_step
    damping = 1.0 + full_step * canopy * veg_field * orbital
    extended = padded(masked, (("freq", 1),), FH)
    transfer = interaction(extended, masked, quad_offsets, quad_weights)
    spread = padded(transfer, (("freq", 1),), FH)
    change = redistribute(spread, transfer, quad_offsets, quad_weights)
    increment = (masked + full_step * change) / damping[:, None, None, :] - masked
    cosines, sines = angles_of(dir_count)
    step_ratio = sub_step / cell_size
    east_speed = group_speed[:, :, None, :] * cosines[None, None, :, None]
    north_speed = group_speed[:, :, None, :] * sines[None, None, :, None]
    north_going = (sines > 0.0).astype(jnp.float32)[None, None, :, None]
    spectrum = masked
    for substep in range(SUBSTEPS):
        east_flux = east_speed * spectrum
        north_flux = north_speed * spectrum
        rimmed = padded(north_flux, (("geo", 0),), 1)
        below = rimmed[:-2]
        above = rimmed[2:]
        along = north_going * (north_flux - below) + (1.0 - north_going) * (above - north_flux)
        spectrum = wet_four * (spectrum - step_ratio * (east_west(east_flux, cosines) + along))
    return (wet_four * (spectrum + increment), orbital)


def solution(mesh):
    placed = (
        P("geo", "freq", None, None),
        P("geo", None),
        P("geo", None),
        P("geo", None),
        P("geo", None),
        P(),
        P(),
    )
    return jax.shard_map(
        body,
        mesh=mesh,
        in_specs=placed,
        out_specs=(P("geo", "freq", None, None), P("geo", None)),
        check_vma=False,
    )
```

profile of v0, /device:TPU:256, one launch (start us, length us, event | category | flops | bytes accessed | tf_op | source)
XLA Modules:
  0.0 154.1 jit_solution(6656783811822100877)
XLA Ops:
  0.8 0.7 convert_element_type.106
  1.5 0.8 add_multiply_fusion
  2.3 1.2 multiply_multiply_fusion.15
  3.5 1.3 collective-permute-start.17
  4.8 3.0 %collective-permute-start.16 = (f32[4,4,36,128]{3,0,2,1:T(4,128)S(1)}, f32[4,4,36,128]{3,0,2,1:T(4,128)S(1)}, u32[]{:S(2)}, u32[]{:S(2)}) collective-permute-start(f32[4,4,36,128]{3,0,2,1:T(4,128)S(1)} %get-tuple-element.58), channel_id=1, source_target_pairs={{0,64},{64,128},{128,192},{192,256},{256,320},{320,384},{384,448},... | collective-permute-start | bytes 884744 | tf_op jit(solution)/shard_map/ppermute | solution.py:28
  8.0 0.6 fusion.110
  8.6 0.6 fusion.109
  9.4 14.2 %psum.7 = f32[4,128]{1,0:T(4,128)S(1)} all-reduce(f32[4,128]{1,0:T(4,128)S(1)} %multiply_reduce_fusion), channel_id=1, replica_groups=mesh['freq'=8,'geo'=64] {'freq'}, use_global_device_ids=true, to_apply=%region_2.0 | all-reduce | flops 512 | bytes 4096 | tf_op jit(solution)/shard_map/psum | solution.py:136
  23.6 0.6 multiply_add_fusion
  34.6 3.9 %maximum_maximum_fusion = f32[4,14,72,128]{3,0,2,1:T(4,128)S(1)} fusion(f32[4,4,36,128]{3,0,2,1:T(4,128)S(1)} %collective-permute-done.17, f32[4,6,36,128]{3,0,2,1:T(4,128)S(1)} %get-tuple-element.19, f32[4,4,36,128]{3,0,2,1:T(4,128)S(1)} %collective-permute-done.16), kind=kLoop, calls=%fused_computation | loop fusion | flops 2580480 | bytes 3096576 | tf_op jit(solution)/shard_map/concatenate | solution.py:76
  38.5 1.8 %broadcast_multiply_fusion = (f32[4,6,36,128]{3,0,2,1:T(4,128)S(1)}, f32[4,6,36,128]{3,0,2,1:T(4,128)S(1)}, f32[4,6,36,128]{3,0,2,1:T(4,128)S(1)}) fusion(f32[4,6,36,128]{3,0,2,1:T(4,128)S(1)} %get-tuple-element.19, f32[4,14,72,128]{3,0,2,1:T(4,128)S(1)} %maximum_maximum_fusion, s32[]{:T(128)S(6)} %select_n.74, s32[]{:T(128)S(6)} %select_n.73, ...), kind=kLoop, calls=%fused_computation.110 | loop fusion | flops 1990656 | bytes 3551416 | tf_op jit(solution)/shard_map/mul | solution.py:90
  40.5 4.5 %collective-permute-start.1 = (f32[1,6,36,128]{3,0,2,1:T(1,128)S(1)}, f32[1,6,36,128]{3,0,2,1:T(1,128)S(1)}, u32[]{:S(2)}, u32[]{:S(2)}) collective-permute-start(f32[1,6,36,128]{3,0,2,1:T(1,128)S(1)} %get-tuple-element.54), channel_id=1, source_target_pairs={{1,0},{2,1},{3,2},{4,3},{5,4},{6,5},{7,6},{8,7},{9,8},{10,9},{11,1... | collective-permute-start | bytes 331784 | tf_op jit(solution)/shard_map/ppermute | solution.py:31
  45.0 1.9 %collective-permute-start = (f32[1,6,36,128]{3,0,2,1:T(1,128)S(1)}, f32[1,6,36,128]{3,0,2,1:T(1,128)S(1)}, u32[]{:S(2)}, u32[]{:S(2)}) collective-permute-start(f32[1,6,36,128]{3,0,2,1:T(1,128)S(1)} %get-tuple-element.53), channel_id=1, source_target_pairs={{0,1},{1,2},{2,3},{3,4},{4,5},{5,6},{6,7},{7,8},{8,9},{9,10},{10,1... | collective-permute-start | bytes 331784 | tf_op jit(solution)/shard_map/ppermute | solution.py:28
  47.0 1.3 collective-permute-start.19
  48.3 3.0 %collective-permute-start.18 = (f32[4,4,36,128]{3,0,2,1:T(4,128)S(1)}, f32[4,4,36,128]{3,0,2,1:T(4,128)S(1)}, u32[]{:S(2)}, u32[]{:S(2)}) collective-permute-start(f32[4,4,36,128]{3,0,2,1:T(4,128)S(1)} %get-tuple-element.56), channel_id=1, source_target_pairs={{0,64},{64,128},{128,192},{192,256},{256,320},{320,384},{384,448},... | collective-permute-start | bytes 884744 | tf_op jit(solution)/shard_map/ppermute | solution.py:28
  51.4 3.6 %collective-permute-done = f32[1,6,36,128]{3,0,2,1:T(1,128)S(1)} collective-permute-done((f32[1,6,36,128]{3,0,2,1:T(1,128)S(1)}, f32[1,6,36,128]{3,0,2,1:T(1,128)S(1)}, u32[]{:S(2)}, u32[]{:S(2)}) %collective-permute-start) | collective-permute-done | bytes 110624 | tf_op jit(solution)/shard_map/ppermute | solution.py:28
  55.0 1.0 multiply_multiply_fusion.14
  56.3 3.7 %collective-permute-start.3 = (f32[1,6,36,128]{3,0,2,1:T(1,128)S(1)}, f32[1,6,36,128]{3,0,2,1:T(1,128)S(1)}, u32[]{:S(2)}, u32[]{:S(2)}) collective-permute-start(f32[1,6,36,128]{3,0,2,1:T(1,128)S(1)} %get-tuple-element.50), channel_id=1, source_target_pairs={{1,0},{2,1},{3,2},{4,3},{5,4},{6,5},{7,6},{8,7},{9,8},{10,9},{11,1... | collective-permute-start | bytes 331784 | tf_op jit(solution)/shard_map/ppermute | solution.py:31
  59.9 2.2 %collective-permute-start.2 = (f32[1,6,36,128]{3,0,2,1:T(1,128)S(1)}, f32[1,6,36,128]{3,0,2,1:T(1,128)S(1)}, u32[]{:S(2)}, u32[]{:S(2)}) collective-permute-start(f32[1,6,36,128]{3,0,2,1:T(1,128)S(1)} %get-tuple-element.49), channel_id=1, source_target_pairs={{0,1},{1,2},{2,3},{3,4},{4,5},{5,6},{6,7},{7,8},{8,9},{9,10},{10,1... | collective-permute-start | bytes 331784 | tf_op jit(solution)/shard_map/ppermute | solution.py:28
  62.4 0.5 collective-permute-done.3
  62.9 7.0 %collective-permute-done.2 = f32[1,6,36,128]{3,0,2,1:T(1,128)S(1)} collective-permute-done((f32[1,6,36,128]{3,0,2,1:T(1,128)S(1)}, f32[1,6,36,128]{3,0,2,1:T(1,128)S(1)}, u32[]{:S(2)}, u32[]{:S(2)}) %collective-permute-start.2) | collective-permute-done | bytes 110624 | tf_op jit(solution)/shard_map/ppermute | solution.py:28
  69.9 1.0 multiply_multiply_fusion.13
  71.2 1.9 %collective-permute-start.5 = (f32[1,6,36,128]{3,0,2,1:T(1,128)S(1)}, f32[1,6,36,128]{3,0,2,1:T(1,128)S(1)}, u32[]{:S(2)}, u32[]{:S(2)}) collective-permute-start(f32[1,6,36,128]{3,0,2,1:T(1,128)S(1)} %get-tuple-element.46), channel_id=1, source_target_pairs={{1,0},{2,1},{3,2},{4,3},{5,4},{6,5},{7,6},{8,7},{9,8},{10,9},{11,1... | collective-permute-start | bytes 331784 | tf_op jit(solution)/shard_map/ppermute | solution.py:31
  73.1 3.9 %collective-permute-start.4 = (f32[1,6,36,128]{3,0,2,1:T(1,128)S(1)}, f32[1,6,36,128]{3,0,2,1:T(1,128)S(1)}, u32[]{:S(2)}, u32[]{:S(2)}) collective-permute-start(f32[1,6,36,128]{3,0,2,1:T(1,128)S(1)} %get-tuple-element.45), channel_id=1, source_target_pairs={{0,1},{1,2},{2,3},{3,4},{4,5},{5,6},{6,7},{7,8},{8,9},{9,10},{10,1... | collective-permute-start | bytes 331784 | tf_op jit(solution)/shard_map/ppermute | solution.py:28
  77.4 3.9 %maximum_maximum_fusion.1 = f32[4,14,72,128]{3,0,2,1:T(4,128)S(1)} fusion(f32[4,4,36,128]{3,0,2,1:T(4,128)S(1)} %collective-permute-done.19, f32[4,6,36,128]{3,0,2,1:T(4,128)S(1)} %get-tuple-element.20, f32[4,4,36,128]{3,0,2,1:T(4,128)S(1)} %collective-permute-done.18), kind=kLoop, calls=%fused_computation.1 | loop fusion | flops 2580480 | bytes 3096576 | tf_op jit(solution)/shard_map/concatenate | solution.py:98
  81.3 1.8 %collective-permute-done.4 = f32[1,6,36,128]{3,0,2,1:T(1,128)S(1)} collective-permute-done((f32[1,6,36,128]{3,0,2,1:T(1,128)S(1)}, f32[1,6,36,128]{3,0,2,1:T(1,128)S(1)}, u32[]{:S(2)}, u32[]{:S(2)}) %collective-permute-start.4) | collective-permute-done | bytes 110624 | tf_op jit(solution)/shard_map/ppermute | solution.py:28
  83.1 1.0 multiply_multiply_fusion.12
  84.4 3.5 %collective-permute-start.7 = (f32[1,6,36,128]{3,0,2,1:T(1,128)S(1)}, f32[1,6,36,128]{3,0,2,1:T(1,128)S(1)}, u32[]{:S(2)}, u32[]{:S(2)}) collective-permute-start(f32[1,6,36,128]{3,0,2,1:T(1,128)S(1)} %get-tuple-element.42), channel_id=1, source_target_pairs={{1,0},{2,1},{3,2},{4,3},{5,4},{6,5},{7,6},{8,7},{9,8},{10,9},{11,1... | collective-permute-start | bytes 331784 | tf_op jit(solution)/shard_map/ppermute | solution.py:31
  87.9 2.5 %collective-permute-start.6 = (f32[1,6,36,128]{3,0,2,1:T(1,128)S(1)}, f32[1,6,36,128]{3,0,2,1:T(1,128)S(1)}, u32[]{:S(2)}, u32[]{:S(2)}) collective-permute-start(f32[1,6,36,128]{3,0,2,1:T(1,128)S(1)} %get-tuple-element.41), channel_id=1, source_target_pairs={{0,1},{1,2},{2,3},{3,4},{4,5},{5,6},{6,7},{7,8},{8,9},{9,10},{10,1... | collective-permute-start | bytes 331784 | tf_op jit(solution)/shard_map/ppermute | solution.py:28
  91.0 6.8 %collective-permute-done.6 = f32[1,6,36,128]{3,0,2,1:T(1,128)S(1)} collective-permute-done((f32[1,6,36,128]{3,0,2,1:T(1,128)S(1)}, f32[1,6,36,128]{3,0,2,1:T(1,128)S(1)}, u32[]{:S(2)}, u32[]{:S(2)}) %collective-permute-start.6) | collective-permute-done | bytes 110624 | tf_op jit(solution)/shard_map/ppermute | solution.py:28
  97.8 1.0 multiply_multiply_fusion.11
  99.1 1.9 %collective-permute-start.9 = (f32[1,6,36,128]{3,0,2,1:T(1,128)S(1)}, f32[1,6,36,128]{3,0,2,1:T(1,128)S(1)}, u32[]{:S(2)}, u32[]{:S(2)}) collective-permute-start(f32[1,6,36,128]{3,0,2,1:T(1,128)S(1)} %get-tuple-element.38), channel_id=1, source_target_pairs={{1,0},{2,1},{3,2},{4,3},{5,4},{6,5},{7,6},{8,7},{9,8},{10,9},{11,1... | collective-permute-start | bytes 331784 | tf_op jit(solution)/shard_map/ppermute | solution.py:31
  101.1 3.9 %collective-permute-start.8 = (f32[1,6,36,128]{3,0,2,1:T(1,128)S(1)}, f32[1,6,36,128]{3,0,2,1:T(1,128)S(1)}, u32[]{:S(2)}, u32[]{:S(2)}) collective-permute-start(f32[1,6,36,128]{3,0,2,1:T(1,128)S(1)} %get-tuple-element.37), channel_id=1, source_target_pairs={{0,1},{1,2},{2,3},{3,4},{4,5},{5,6},{6,7},{7,8},{8,9},{9,10},{10,1... | collective-permute-start | bytes 331784 | tf_op jit(solution)/shard_map/ppermute | solution.py:28
  105.3 0.5 collective-permute-done.9
  105.8 5.2 %collective-permute-done.8 = f32[1,6,36,128]{3,0,2,1:T(1,128)S(1)} collective-permute-done((f32[1,6,36,128]{3,0,2,1:T(1,128)S(1)}, f32[1,6,36,128]{3,0,2,1:T(1,128)S(1)}, u32[]{:S(2)}, u32[]{:S(2)}) %collective-permute-start.8) | collective-permute-done | bytes 110624 | tf_op jit(solution)/shard_map/ppermute | solution.py:28
  111.0 1.0 multiply_multiply_fusion.10
  112.3 1.9 %collective-permute-start.11 = (f32[1,6,36,128]{3,0,2,1:T(1,128)S(1)}, f32[1,6,36,128]{3,0,2,1:T(1,128)S(1)}, u32[]{:S(2)}, u32[]{:S(2)}) collective-permute-start(f32[1,6,36,128]{3,0,2,1:T(1,128)S(1)} %get-tuple-element.34), channel_id=1, source_target_pairs={{1,0},{2,1},{3,2},{4,3},{5,4},{6,5},{7,6},{8,7},{9,8},{10,9},{11,1... | collective-permute-start | bytes 331784 | tf_op jit(solution)/shard_map/ppermute | solution.py:31
  114.3 3.9 %collective-permute-start.10 = (f32[1,6,36,128]{3,0,2,1:T(1,128)S(1)}, f32[1,6,36,128]{3,0,2,1:T(1,128)S(1)}, u32[]{:S(2)}, u32[]{:S(2)}) collective-permute-start(f32[1,6,36,128]{3,0,2,1:T(1,128)S(1)} %get-tuple-element.33), channel_id=1, source_target_pairs={{0,1},{1,2},{2,3},{3,4},{4,5},{5,6},{6,7},{7,8},{8,9},{9,10},{10,1... | collective-permute-start | bytes 331784 | tf_op jit(solution)/shard_map/ppermute | solution.py:28
  119.0 5.2 %collective-permute-done.10 = f32[1,6,36,128]{3,0,2,1:T(1,128)S(1)} collective-permute-done((f32[1,6,36,128]{3,0,2,1:T(1,128)S(1)}, f32[1,6,36,128]{3,0,2,1:T(1,128)S(1)}, u32[]{:S(2)}, u32[]{:S(2)}) %collective-permute-start.10) | collective-permute-done | bytes 110624 | tf_op jit(solution)/shard_map/ppermute | solution.py:28
  124.2 1.0 multiply_multiply_fusion.9
  125.5 1.9 %collective-permute-start.13 = (f32[1,6,36,128]{3,0,2,1:T(1,128)S(1)}, f32[1,6,36,128]{3,0,2,1:T(1,128)S(1)}, u32[]{:S(2)}, u32[]{:S(2)}) collective-permute-start(f32[1,6,36,128]{3,0,2,1:T(1,128)S(1)} %get-tuple-element.30), channel_id=1, source_target_pairs={{1,0},{2,1},{3,2},{4,3},{5,4},{6,5},{7,6},{8,7},{9,8},{10,9},{11,1... | collective-permute-start | bytes 331784 | tf_op jit(solution)/shard_map/ppermute | solution.py:31
  127.5 3.9 %collective-permute-start.12 = (f32[1,6,36,128]{3,0,2,1:T(1,128)S(1)}, f32[1,6,36,128]{3,0,2,1:T(1,128)S(1)}, u32[]{:S(2)}, u32[]{:S(2)}) collective-permute-start(f32[1,6,36,128]{3,0,2,1:T(1,128)S(1)} %get-tuple-element.29), channel_id=1, source_target_pairs={{0,1},{1,2},{2,3},{3,4},{4,5},{5,6},{6,7},{7,8},{8,9},{9,10},{10,1... | collective-permute-start | bytes 331784 | tf_op jit(solution)/shard_map/ppermute | solution.py:28
  132.2 5.2 %collective-permute-done.12 = f32[1,6,36,128]{3,0,2,1:T(1,128)S(1)} collective-permute-done((f32[1,6,36,128]{3,0,2,1:T(1,128)S(1)}, f32[1,6,36,128]{3,0,2,1:T(1,128)S(1)}, u32[]{:S(2)}, u32[]{:S(2)}) %collective-permute-start.12) | collective-permute-done | bytes 110624 | tf_op jit(solution)/shard_map/ppermute | solution.py:28
  137.4 1.0 multiply_multiply_fusion.8
  138.7 1.9 %collective-permute-start.15 = (f32[1,6,36,128]{3,0,2,1:T(1,128)S(1)}, f32[1,6,36,128]{3,0,2,1:T(1,128)S(1)}, u32[]{:S(2)}, u32[]{:S(2)}) collective-permute-start(f32[1,6,36,128]{3,0,2,1:T(1,128)S(1)} %get-tuple-element.26), channel_id=1, source_target_pairs={{1,0},{2,1},{3,2},{4,3},{5,4},{6,5},{7,6},{8,7},{9,8},{10,9},{11,1... | collective-permute-start | bytes 331784 | tf_op jit(solution)/shard_map/ppermute | solution.py:31
  140.6 3.9 %collective-permute-start.14 = (f32[1,6,36,128]{3,0,2,1:T(1,128)S(1)}, f32[1,6,36,128]{3,0,2,1:T(1,128)S(1)}, u32[]{:S(2)}, u32[]{:S(2)}) collective-permute-start(f32[1,6,36,128]{3,0,2,1:T(1,128)S(1)} %get-tuple-element.25), channel_id=1, source_target_pairs={{0,1},{1,2},{2,3},{3,4},{4,5},{5,6},{6,7},{7,8},{8,9},{9,10},{10,1... | collective-permute-start | bytes 331784 | tf_op jit(solution)/shard_map/ppermute | solution.py:28
  145.4 5.2 %collective-permute-done.14 = f32[1,6,36,128]{3,0,2,1:T(1,128)S(1)} collective-permute-done((f32[1,6,36,128]{3,0,2,1:T(1,128)S(1)}, f32[1,6,36,128]{3,0,2,1:T(1,128)S(1)}, u32[]{:S(2)}, u32[]{:S(2)}) %collective-permute-start.14) | collective-permute-done | bytes 110624 | tf_op jit(solution)/shard_map/ppermute | solution.py:28
  150.6 3.5 %fusion.73 = f32[4,6,36,128]{3,0,2,1:T(4,128)} fusion(f32[4,6,36,128]{3,0,2,1:T(4,128)S(1)} %get-tuple-element.19, f32[4,6,36,128]{3,0,2,1:T(4,128)S(1)} %get-tuple-element.21, f32[4,14,72,128]{3,0,2,1:T(4,128)S(1)} %maximum_maximum_fusion.1, s32[]{:T(128)S(6)} %select_n.82, s32[]{:T(128)S(6)} %select_n.81, s32[]{:T(128)S(6)} %select_n.79, ...), kind=kLoop, calls=%fused_computation.109 | loop fusion | flops 3649536 | bytes 5097464 | tf_op jit(solution)/shard_map/mul | solution.py:158
  (52 shorter events, 7.0 us)
Async XLA Ops:
  0.6 8.6 %copy-start.4 = (f32[4,128]{1,0:T(4,128)S(1)}, f32[4,128]{1,0:T(4,128)}, u32[]{:S(2)}) copy-start(f32[4,128]{1,0:T(4,128)} %param.8) | copy-start | bytes 6148
  0.6 7.4 %copy-start = (s32[4]{0:T(128)S(1)}, s32[4]{0:T(128)}, u32[]{:S(2)}) copy-start(s32[4]{0:T(128)} %param.12) | copy-start | bytes 52
  0.7 8.0 %copy-start.3 = (f32[2]{0:T(128)S(1)}, f32[2]{0:T(128)}, u32[]{:S(2)}) copy-start(f32[2]{0:T(128)} %param.13) | copy-start | bytes 28
  0.7 22.9 %copy-start.1 = (s32[4,128]{1,0:T(4,128)S(1)}, s32[4,128]{1,0:T(4,128)}, u32[]{:S(2)}) copy-start(s32[4,128]{1,0:T(4,128)} %param.10) | copy-start | bytes 6148
  0.7 22.9 %copy-start.2 = (f32[4,128]{1,0:T(4,128)S(1)}, f32[4,128]{1,0:T(4,128)}, u32[]{:S(2)}) copy-start(f32[4,128]{1,0:T(4,128)} %param.11) | copy-start | bytes 6148
  3.5 31.0 %collective-permute-start.17 = (f32[4,4,36,128]{3,0,2,1:T(4,128)S(1)}, f32[4,4,36,128]{3,0,2,1:T(4,128)S(1)}, u32[]{:S(2)}, u32[]{:S(2)}) collective-permute-start(f32[4,4,36,128]{3,0,2,1:T(4,128)S(1)} %get-tuple-element.59), channel_id=1, source_target_pairs={{64,0},{128,64},{192,128},{256,192},{320,256},{384,320},{448,384},... | collective-permute-start | bytes 884744 | tf_op jit(solution)/shard_map/ppermute | solution.py:31
  4.8 29.7 %collective-permute-start.16 = (f32[4,4,36,128]{3,0,2,1:T(4,128)S(1)}, f32[4,4,36,128]{3,0,2,1:T(4,128)S(1)}, u32[]{:S(2)}, u32[]{:S(2)}) collective-permute-start(f32[4,4,36,128]{3,0,2,1:T(4,128)S(1)} %get-tuple-element.58), channel_id=1, source_target_pairs={{0,64},{64,128},{128,192},{192,256},{256,320},{320,384},{384,448},... | collective-permute-start | bytes 884744 | tf_op jit(solution)/shard_map/ppermute | solution.py:28
  40.5 10.8 %collective-permute-start.1 = (f32[1,6,36,128]{3,0,2,1:T(1,128)S(1)}, f32[1,6,36,128]{3,0,2,1:T(1,128)S(1)}, u32[]{:S(2)}, u32[]{:S(2)}) collective-permute-start(f32[1,6,36,128]{3,0,2,1:T(1,128)S(1)} %get-tuple-element.54), channel_id=1, source_target_pairs={{1,0},{2,1},{3,2},{4,3},{5,4},{6,5},{7,6},{8,7},{9,8},{10,9},{11,1... | collective-permute-start | bytes 331784 | tf_op jit(solution)/shard_map/ppermute | solution.py:31
  45.0 10.0 %collective-permute-start = (f32[1,6,36,128]{3,0,2,1:T(1,128)S(1)}, f32[1,6,36,128]{3,0,2,1:T(1,128)S(1)}, u32[]{:S(2)}, u32[]{:S(2)}) collective-permute-start(f32[1,6,36,128]{3,0,2,1:T(1,128)S(1)} %get-tuple-element.53), channel_id=1, source_target_pairs={{0,1},{1,2},{2,3},{3,4},{4,5},{5,6},{6,7},{7,8},{8,9},{9,10},{10,1... | collective-permute-start | bytes 331784 | tf_op jit(solution)/shard_map/ppermute | solution.py:28
  47.0 30.3 %collective-permute-start.19 = (f32[4,4,36,128]{3,0,2,1:T(4,128)S(1)}, f32[4,4,36,128]{3,0,2,1:T(4,128)S(1)}, u32[]{:S(2)}, u32[]{:S(2)}) collective-permute-start(f32[4,4,36,128]{3,0,2,1:T(4,128)S(1)} %get-tuple-element.57), channel_id=1, source_target_pairs={{64,0},{128,64},{192,128},{256,192},{320,256},{384,320},{448,384},... | collective-permute-start | bytes 884744 | tf_op jit(solution)/shard_map/ppermute | solution.py:31
  48.3 29.1 %collective-permute-start.18 = (f32[4,4,36,128]{3,0,2,1:T(4,128)S(1)}, f32[4,4,36,128]{3,0,2,1:T(4,128)S(1)}, u32[]{:S(2)}, u32[]{:S(2)}) collective-permute-start(f32[4,4,36,128]{3,0,2,1:T(4,128)S(1)} %get-tuple-element.56), channel_id=1, source_target_pairs={{0,64},{64,128},{128,192},{192,256},{256,320},{320,384},{384,448},... | collective-permute-start | bytes 884744 | tf_op jit(solution)/shard_map/ppermute | solution.py:28
  56.3 6.6 %collective-permute-start.3 = (f32[1,6,36,128]{3,0,2,1:T(1,128)S(1)}, f32[1,6,36,128]{3,0,2,1:T(1,128)S(1)}, u32[]{:S(2)}, u32[]{:S(2)}) collective-permute-start(f32[1,6,36,128]{3,0,2,1:T(1,128)S(1)} %get-tuple-element.50), channel_id=1, source_target_pairs={{1,0},{2,1},{3,2},{4,3},{5,4},{6,5},{7,6},{8,7},{9,8},{10,9},{11,1... | collective-permute-start | bytes 331784 | tf_op jit(solution)/shard_map/ppermute | solution.py:31
  59.9 10.0 %collective-permute-start.2 = (f32[1,6,36,128]{3,0,2,1:T(1,128)S(1)}, f32[1,6,36,128]{3,0,2,1:T(1,128)S(1)}, u32[]{:S(2)}, u32[]{:S(2)}) collective-permute-start(f32[1,6,36,128]{3,0,2,1:T(1,128)S(1)} %get-tuple-element.49), channel_id=1, source_target_pairs={{0,1},{1,2},{2,3},{3,4},{4,5},{5,6},{6,7},{7,8},{8,9},{9,10},{10,1... | collective-permute-start | bytes 331784 | tf_op jit(solution)/shard_map/ppermute | solution.py:28
  71.2 10.1 %collective-permute-start.5 = (f32[1,6,36,128]{3,0,2,1:T(1,128)S(1)}, f32[1,6,36,128]{3,0,2,1:T(1,128)S(1)}, u32[]{:S(2)}, u32[]{:S(2)}) collective-permute-start(f32[1,6,36,128]{3,0,2,1:T(1,128)S(1)} %get-tuple-element.46), channel_id=1, source_target_pairs={{1,0},{2,1},{3,2},{4,3},{5,4},{6,5},{7,6},{8,7},{9,8},{10,9},{11,1... | collective-permute-start | bytes 331784 | tf_op jit(solution)/shard_map/ppermute | solution.py:31
  73.1 10.0 %collective-permute-start.4 = (f32[1,6,36,128]{3,0,2,1:T(1,128)S(1)}, f32[1,6,36,128]{3,0,2,1:T(1,128)S(1)}, u32[]{:S(2)}, u32[]{:S(2)}) collective-permute-start(f32[1,6,36,128]{3,0,2,1:T(1,128)S(1)} %get-tuple-element.45), channel_id=1, source_target_pairs={{0,1},{1,2},{2,3},{3,4},{4,5},{5,6},{6,7},{7,8},{8,9},{9,10},{10,1... | collective-permute-start | bytes 331784 | tf_op jit(solution)/shard_map/ppermute | solution.py:28
  84.4 6.6 %collective-permute-start.7 = (f32[1,6,36,128]{3,0,2,1:T(1,128)S(1)}, f32[1,6,36,128]{3,0,2,1:T(1,128)S(1)}, u32[]{:S(2)}, u32[]{:S(2)}) collective-permute-start(f32[1,6,36,128]{3,0,2,1:T(1,128)S(1)} %get-tuple-element.42), channel_id=1, source_target_pairs={{1,0},{2,1},{3,2},{4,3},{5,4},{6,5},{7,6},{8,7},{9,8},{10,9},{11,1... | collective-permute-start | bytes 331784 | tf_op jit(solution)/shard_map/ppermute | solution.py:31
  87.9 10.0 %collective-permute-start.6 = (f32[1,6,36,128]{3,0,2,1:T(1,128)S(1)}, f32[1,6,36,128]{3,0,2,1:T(1,128)S(1)}, u32[]{:S(2)}, u32[]{:S(2)}) collective-permute-start(f32[1,6,36,128]{3,0,2,1:T(1,128)S(1)} %get-tuple-element.41), channel_id=1, source_target_pairs={{0,1},{1,2},{2,3},{3,4},{4,5},{5,6},{6,7},{7,8},{8,9},{9,10},{10,1... | collective-permute-start | bytes 331784 | tf_op jit(solution)/shard_map/ppermute | solution.py:28
  99.1 6.6 %collective-permute-start.9 = (f32[1,6,36,128]{3,0,2,1:T(1,128)S(1)}, f32[1,6,36,128]{3,0,2,1:T(1,128)S(1)}, u32[]{:S(2)}, u32[]{:S(2)}) collective-permute-start(f32[1,6,36,128]{3,0,2,1:T(1,128)S(1)} %get-tuple-element.38), channel_id=1, source_target_pairs={{1,0},{2,1},{3,2},{4,3},{5,4},{6,5},{7,6},{8,7},{9,8},{10,9},{11,1... | collective-permute-start | bytes 331784 | tf_op jit(solution)/shard_map/ppermute | solution.py:31
  101.1 10.0 %collective-permute-start.8 = (f32[1,6,36,128]{3,0,2,1:T(1,128)S(1)}, f32[1,6,36,128]{3,0,2,1:T(1,128)S(1)}, u32[]{:S(2)}, u32[]{:S(2)}) collective-permute-start(f32[1,6,36,128]{3,0,2,1:T(1,128)S(1)} %get-tuple-element.37), channel_id=1, source_target_pairs={{0,1},{1,2},{2,3},{3,4},{4,5},{5,6},{6,7},{7,8},{8,9},{9,10},{10,1... | collective-permute-start | bytes 331784 | tf_op jit(solution)/shard_map/ppermute | solution.py:28
  112.3 6.6 %collective-permute-start.11 = (f32[1,6,36,128]{3,0,2,1:T(1,128)S(1)}, f32[1,6,36,128]{3,0,2,1:T(1,128)S(1)}, u32[]{:S(2)}, u32[]{:S(2)}) collective-permute-start(f32[1,6,36,128]{3,0,2,1:T(1,128)S(1)} %get-tuple-element.34), channel_id=1, source_target_pairs={{1,0},{2,1},{3,2},{4,3},{5,4},{6,5},{7,6},{8,7},{9,8},{10,9},{11,1... | collective-permute-start | bytes 331784 | tf_op jit(solution)/shard_map/ppermute | solution.py:31
  114.3 10.0 %collective-permute-start.10 = (f32[1,6,36,128]{3,0,2,1:T(1,128)S(1)}, f32[1,6,36,128]{3,0,2,1:T(1,128)S(1)}, u32[]{:S(2)}, u32[]{:S(2)}) collective-permute-start(f32[1,6,36,128]{3,0,2,1:T(1,128)S(1)} %get-tuple-element.33), channel_id=1, source_target_pairs={{0,1},{1,2},{2,3},{3,4},{4,5},{5,6},{6,7},{7,8},{8,9},{9,10},{10,1... | collective-permute-start | bytes 331784 | tf_op jit(solution)/shard_map/ppermute | solution.py:28
  125.5 6.6 %collective-permute-start.13 = (f32[1,6,36,128]{3,0,2,1:T(1,128)S(1)}, f32[1,6,36,128]{3,0,2,1:T(1,128)S(1)}, u32[]{:S(2)}, u32[]{:S(2)}) collective-permute-start(f32[1,6,36,128]{3,0,2,1:T(1,128)S(1)} %get-tuple-element.30), channel_id=1, source_target_pairs={{1,0},{2,1},{3,2},{4,3},{5,4},{6,5},{7,6},{8,7},{9,8},{10,9},{11,1... | collective-permute-start | bytes 331784 | tf_op jit(solution)/shard_map/ppermute | solution.py:31
  127.5 10.0 %collective-permute-start.12 = (f32[1,6,36,128]{3,0,2,1:T(1,128)S(1)}, f32[1,6,36,128]{3,0,2,1:T(1,128)S(1)}, u32[]{:S(2)}, u32[]{:S(2)}) collective-permute-start(f32[1,6,36,128]{3,0,2,1:T(1,128)S(1)} %get-tuple-element.29), channel_id=1, source_target_pairs={{0,1},{1,2},{2,3},{3,4},{4,5},{5,6},{6,7},{7,8},{8,9},{9,10},{10,1... | collective-permute-start | bytes 331784 | tf_op jit(solution)/shard_map/ppermute | solution.py:28
  138.7 6.6 %collective-permute-start.15 = (f32[1,6,36,128]{3,0,2,1:T(1,128)S(1)}, f32[1,6,36,128]{3,0,2,1:T(1,128)S(1)}, u32[]{:S(2)}, u32[]{:S(2)}) collective-permute-start(f32[1,6,36,128]{3,0,2,1:T(1,128)S(1)} %get-tuple-element.26), channel_id=1, source_target_pairs={{1,0},{2,1},{3,2},{4,3},{5,4},{6,5},{7,6},{8,7},{9,8},{10,9},{11,1... | collective-permute-start | bytes 331784 | tf_op jit(solution)/shard_map/ppermute | solution.py:31
  140.6 10.0 %collective-permute-start.14 = (f32[1,6,36,128]{3,0,2,1:T(1,128)S(1)}, f32[1,6,36,128]{3,0,2,1:T(1,128)S(1)}, u32[]{:S(2)}, u32[]{:S(2)}) collective-permute-start(f32[1,6,36,128]{3,0,2,1:T(1,128)S(1)} %get-tuple-element.25), channel_id=1, source_target_pairs={{0,1},{1,2},{2,3},{3,4},{4,5},{5,6},{6,7},{7,8},{8,9},{9,10},{10,1... | collective-permute-start | bytes 331784 | tf_op jit(solution)/shard_map/ppermute | solution.py:28
where the time goes:
time: 155 us; the launch traced here: 154 us
  starting transfers between devices  56.1 us (36%)
  waiting for transfers between devices  42.9 us (28%)
  other arithmetic  24.5 us (16%)
  blocking collectives  14.2 us (9%)
  between operations  11.2 us (7%)
  local copies, waits for them, and re-layouts  5.13 us (3%)
    ppermute x10, waiting for transfers between devices, padded(): lax.ppermute(lax.slice_in_dim(block, block.shape[dim] - width, None, axis...  40.2 us
    ppermute x10, starting transfers between devices, padded(): lax.ppermute(lax.slice_in_dim(block, block.shape[dim] - width, None, axis...  32.3 us
    ppermute x10, starting transfers between devices, padded(): lax.ppermute(lax.slice_in_dim(block, 0, width, axis=dim), axis, backward)  23.8 us
    psum x1, blocking collectives, body(): orbital = jnp.sqrt(lax.psum(partial_value, 'freq'))  14.2 us
    mul x8, other arithmetic, body(): east_flux = east_speed * spectrum  7.95 us
    concatenate x1, other arithmetic, interaction(): doubled = jnp.concatenate([extended, extended], axis=2)  3.95 us
    concatenate x1, other arithmetic, redistribute(): doubled = jnp.concatenate([extended, extended], axis=2)  3.95 us
    mul x1, other arithmetic, body(): return (wet_four * (spectrum + increment), orbital)  3.45 us
  transfers between devices with their start and end apart: 20, of which 14 were waited for; matrix products, arithmetic and copies ran while one was open for 7% of the time, Pallas kernels for 0%

commit v1 on v0

v1 whole, which is shorter than its diff:
```python
import math

import jax
import jax.numpy as jnp
from jax import lax
from jax.sharding import PartitionSpec as P

FH = 4
SUBSTEPS = 8


gravity = 9.81
base_freq = 0.03
freq_ratio = 1.05
cell_size = 20.0
sub_step = 2.0
coupling = 0.01
coef_plus = 0.4096
coef_minus = 3.1605
coef_both = 2.589


def from_neighbour(block, axis, distance):
    count = lax.axis_size(axis)
    pairs = [(i, i + distance) for i in range(count) if 0 <= i + distance < count]
    return lax.ppermute(block, axis, pairs)


def halo(block, axis, dim, width, side):
    size = block.shape[dim]
    parts = []
    distance = 1
    need = width
    while need > 0:
        take = min(size, need)
        if side < 0:
            piece = lax.slice_in_dim(block, size - take, size, axis=dim)
            parts.insert(0, from_neighbour(piece, axis, distance))
        else:
            piece = lax.slice_in_dim(block, 0, take, axis=dim)
            parts.append(from_neighbour(piece, axis, -distance))
        need -= take
        distance += 1
    return parts


def physics(radian_freq, water_depth, dir_count):
    square = (radian_freq * radian_freq)[None, :, None]
    column = water_depth[:, None, :]
    depth_ratio = square * column / gravity
    depth_wave = depth_ratio / jnp.sqrt(jnp.tanh(depth_ratio))
    group_speed = (
        radian_freq[None, :, None]
        * column
        / depth_wave
        * (0.5 + depth_wave / jnp.sinh(2.0 * depth_wave))
    )
    orbit_weight = (
        square
        / jnp.sinh(depth_wave) ** 2
        * (radian_freq * (freq_ratio - 1.0))[None, :, None]
        * (2.0 * math.pi / dir_count)
    )
    return (group_speed, orbit_weight)


def angles_of(dir_count):
    angles = (jnp.arange(dir_count, dtype=jnp.float32) + 0.5) * (2.0 * math.pi / dir_count)
    return (jnp.cos(angles), jnp.sin(angles))


def shifted(doubled, freq_start, dir_off, count):
    dir_count = doubled.shape[2] // 2
    starts = (
        jnp.zeros((), jnp.int32),
        freq_start,
        dir_off % dir_count,
        jnp.zeros((), jnp.int32),
    )
    return lax.dynamic_slice(
        doubled, starts, (doubled.shape[0], count, dir_count, doubled.shape[3])
    )


def source_change(extended, quad_offsets, quad_weights, count):
    up_bins, down_bins, up_turn, down_turn = (
        quad_offsets[0],
        quad_offsets[1],
        quad_offsets[2],
        quad_offsets[3],
    )
    weight_up, weight_down = (quad_weights[0], quad_weights[1])
    wide = count + 2 * FH
    doubled = jnp.concatenate([extended, extended], axis=2)
    centre = lax.slice_in_dim(extended, FH, FH + wide, axis=1)
    upper = weight_up * shifted(doubled, FH + up_bins, up_turn, wide) + (
        1.0 - weight_up
    ) * shifted(doubled, FH + up_bins + 1, up_turn, wide)
    lower = weight_down * shifted(doubled, FH - down_bins, -down_turn, wide) + (
        1.0 - weight_down
    ) * shifted(doubled, FH - down_bins - 1, -down_turn, wide)
    transfer = coupling * (
        centre * centre * (coef_plus * upper + coef_minus * lower)
        - coef_both * centre * upper * lower
    )
    spread = jnp.concatenate([transfer, transfer], axis=2)
    gained = weight_up * shifted(spread, FH - up_bins, -up_turn, count) + (
        1.0 - weight_up
    ) * shifted(spread, FH - up_bins - 1, -up_turn, count)
    gained = (
        gained
        + weight_down * shifted(spread, FH + down_bins, down_turn, count)
        + (1.0 - weight_down) * shifted(spread, FH + down_bins + 1, down_turn, count)
    )
    own = lax.slice_in_dim(transfer, FH, FH + count, axis=1)
    return gained - 2.0 * own


def east_west(east_flux, cosines):
    zeros = jnp.zeros_like(east_flux[..., :1])
    behind = jnp.concatenate([zeros, east_flux[..., :-1]], axis=-1)
    ahead = jnp.concatenate([east_flux[..., 1:], zeros], axis=-1)
    east_going = (cosines > 0.0)[None, None, :, None]
    return jnp.where(east_going, east_flux - behind, ahead - east_flux)


def propagate(spectrum, speed, wet, cosines, sines, northward):
    step_ratio = sub_step / cell_size
    east_speed = speed[:, :, None, :] * cosines[None, None, :, None]
    north_speed = speed[:, :, None, :] * sines[None, None, :, None]
    rows = spectrum.shape[0]
    for substep in range(SUBSTEPS):
        lo, hi = (substep, rows) if northward else (0, rows - substep)
        east_flux = east_speed[lo:hi] * spectrum
        north_flux = north_speed[lo:hi] * spectrum
        along = north_flux[1:] - north_flux[:-1]
        across = east_west(east_flux, cosines)
        if northward:
            spectrum = wet[lo + 1 : hi, None, None, :] * (
                spectrum[1:] - step_ratio * (across[1:] + along)
            )
        else:
            spectrum = wet[lo : hi - 1, None, None, :] * (
                spectrum[:-1] - step_ratio * (across[:-1] + along)
            )
    return spectrum


def body(energy, water_depth, wet_mask, vegetation, canopy, quad_offsets, quad_weights):
    tile_rows, freq_count, dir_count, tile_cols = energy.shape
    wet_field = wet_mask.astype(jnp.float32)
    veg_field = vegetation.astype(jnp.float32)
    wet_four = wet_field[:, None, None, :]
    masked = wet_four * energy
    first_bin = lax.axis_index("freq") * freq_count
    bin_index = (first_bin + jnp.arange(freq_count, dtype=jnp.int32)).astype(jnp.float32)
    radian_freq = 2.0 * math.pi * base_freq * jnp.power(freq_ratio, bin_index)
    half = dir_count // 2
    cosines, sines = angles_of(dir_count)

    fields = jnp.zeros((tile_rows, 1, half, tile_cols), jnp.float32)
    fields = fields.at[:, 0, 0, :].set(wet_field).at[:, 0, 1, :].set(water_depth)
    north_msg = jnp.concatenate([masked[:, :, :half], fields], axis=1)
    south_msg = jnp.concatenate([masked[:, :, half:], fields], axis=1)
    below = halo(north_msg, "geo", 0, SUBSTEPS, -1)
    above = halo(south_msg, "geo", 0, SUBSTEPS, +1)

    low_bins = halo(masked, "freq", 1, 2 * FH, -1)
    high_bins = halo(masked, "freq", 1, 2 * FH, +1)

    group_speed, orbit_weight = physics(radian_freq, water_depth, dir_count)
    partial_value = jnp.sum(orbit_weight * jnp.sum(energy, axis=2), axis=1)
    orbital = jnp.sqrt(lax.psum(partial_value, "freq"))
    full_step = SUBSTEPS * sub_step
    damping = 1.0 + full_step * canopy * veg_field * orbital

    extended = jnp.concatenate(low_bins + [masked] + high_bins, axis=1)
    change = source_change(extended, quad_offsets, quad_weights, freq_count)
    increment = (masked + full_step * change) / damping[:, None, None, :] - masked

    geo_index = lax.axis_index("geo")
    geo_count = lax.axis_size("geo")

    def unpack(parts, offsets, own, own_speed, own_wet):
        spectra, speeds, wets = [], [], []
        for part, offset in zip(parts, offsets):
            valid = (geo_index + offset >= 0) & (geo_index + offset < geo_count)
            depth = jnp.where(valid, part[:, freq_count, 1, :], 1.0)
            spectra.append(part[:, :freq_count])
            wets.append(part[:, freq_count, 0, :])
            speeds.append(physics(radian_freq, depth, dir_count)[0])
        return spectra, speeds, wets

    n_off = [-(len(below) - k) for k in range(len(below))]
    b_spec, b_speed, b_wet = unpack(below, n_off, None, None, None)
    north = propagate(
        jnp.concatenate(b_spec + [masked[:, :, :half]], axis=0),
        jnp.concatenate(b_speed + [group_speed], axis=0),
        jnp.concatenate(b_wet + [wet_field], axis=0),
        cosines[:half],
        sines[:half],
        True,
    )
    s_off = [k + 1 for k in range(len(above))]
    a_spec, a_speed, a_wet = unpack(above, s_off, None, None, None)
    south = propagate(
        jnp.concatenate([masked[:, :, half:]] + a_spec, axis=0),
        jnp.concatenate([group_speed] + a_speed, axis=0),
        jnp.concatenate([wet_field] + a_wet, axis=0),
        cosines[half:],
        sines[half:],
        False,
    )
    moved = jnp.concatenate([north, south], axis=2)
    return (wet_four * (moved + increment), orbital)


def solution(mesh):
    placed = (
        P("geo", "freq", None, None),
        P("geo", None),
        P("geo", None),
        P("geo", None),
        P("geo", None),
        P(),
        P(),
    )
    return jax.shard_map(
        body,
        mesh=mesh,
        in_specs=placed,
        out_specs=(P("geo", "freq", None, None), P("geo", None)),
        check_vma=False,
    )
```

time: 155 us -> 93.6 us (0.60)
  the two profiles are of different devices: /device:TPU:256 before, /device:TPU:248 now
where the time goes in v1:
time: 93.6 us; the launch traced here: 92.9 us
  other arithmetic  24.3 us (26%)
  starting transfers between devices  23.9 us (26%)
  blocking collectives  17.4 us (19%)
  between operations  15.2 us (16%)
  local copies, waits for them, and re-layouts  12.1 us (13%)
    ppermute x8, starting transfers between devices, from_neighbour(): return lax.ppermute(block, axis, pairs)  23.9 us
    psum x1, blocking collectives, body(): orbital = jnp.sqrt(lax.psum(partial_value, 'freq'))  17.4 us
    mul x16, other arithmetic, propagate(): east_flux = east_speed[lo:hi] * spectrum  7.57 us
    slice x16, local copies, waits for them, and re-layouts, east_west(): behind = jnp.concatenate([zeros, east_flux[..., :-1]], axis=-1)  4.89 us
    mul x1, other arithmetic, source_change(): coupling * (centre * centre * (coef_plus * upper + coef_minus * lower) -...  4.85 us
    mul x1, other arithmetic, body(): return (wet_four * (moved + increment), orbital)  3.13 us
    unnamed x16, local copies, waits for them, and re-layouts  2.9 us
    mul x14, other arithmetic, propagate(): north_flux = north_speed[lo:hi] * spectrum  2.85 us
  transfers between devices with their start and end apart: 8, of which 0 were waited for; matrix products, arithmetic and copies ran while one was open for 26% of the time, Pallas kernels for 0%

profile of v1, /device:TPU:248, one launch (start us, length us, event | category | flops | bytes accessed | tf_op | source)
XLA Modules:
  0.0 92.9 jit_solution(12839764186536363237)
XLA Ops:
  0.6 0.7 convert_bitcast_fusion
  1.3 0.6 slice.595
  1.9 1.1 %fusion.156 = (f32[4,6,128]{2,0,1:T(4,128)S(1)}, f32[4,6,36,128]{3,0,2,1:T(4,128)S(1)}) fusion(f32[4,6,36,128]{3,0,2,1:T(4,128)} %param.11, f32[4,128]{1,0:T(4,128)S(1)} %get-tuple-element.125), kind=kLoop, calls=%fused_computation.293 | loop fusion | flops 218112 | bytes 899072 | tf_op jit(solution)/shard_map/reduce_sum | solution.py:172
  3.1 0.7 constant_dynamic-update-slice_fusion.5
  3.9 3.3 %collective-permute-start.2 = (f32[4,7,18,128]{3,0,2,1:T(4,128)S(1)}, f32[4,7,18,128]{3,0,2,1:T(4,128)S(1)}, u32[]{:S(2)}, u32[]{:S(2)}) collective-permute-start(f32[4,7,18,128]{3,0,2,1:T(4,128)S(1)} %get-tuple-element.113), channel_id=1, source_target_pairs={{1,0},{2,1},{3,2},{4,3},{5,4},{6,5},{7,6},{8,7},{9,8},{10,9},{11,1... | collective-permute-start | bytes 774152 | tf_op jit(solution)/shard_map/ppermute | solution.py:26
  7.2 4.0 %collective-permute-start.3 = (f32[4,7,18,128]{3,0,2,1:T(4,128)S(1)}, f32[4,7,18,128]{3,0,2,1:T(4,128)S(1)}, u32[]{:S(2)}, u32[]{:S(2)}) collective-permute-start(f32[4,7,18,128]{3,0,2,1:T(4,128)S(1)} %get-tuple-element.113), channel_id=1, source_target_pairs={{2,0},{3,1},{4,2},{5,3},{6,4},{7,5},{8,6},{9,7},{10,8},{11,9},{12,... | collective-permute-start | bytes 774152 | tf_op jit(solution)/shard_map/ppermute | solution.py:26
  11.2 5.9 %collective-permute-start = (f32[4,7,18,128]{3,0,2,1:T(4,128)S(1)}, f32[4,7,18,128]{3,0,2,1:T(4,128)S(1)}, u32[]{:S(2)}, u32[]{:S(2)}) collective-permute-start(f32[4,7,18,128]{3,0,2,1:T(4,128)S(1)} %get-tuple-element.112), channel_id=1, source_target_pairs={{0,1},{1,2},{2,3},{3,4},{4,5},{5,6},{6,7},{7,8},{8,9},{9,10},{10,1... | collective-permute-start | bytes 774152 | tf_op jit(solution)/shard_map/ppermute | solution.py:26
  17.1 2.7 %collective-permute-start.1 = (f32[4,7,18,128]{3,0,2,1:T(4,128)S(1)}, f32[4,7,18,128]{3,0,2,1:T(4,128)S(1)}, u32[]{:S(2)}, u32[]{:S(2)}) collective-permute-start(f32[4,7,18,128]{3,0,2,1:T(4,128)S(1)} %get-tuple-element.112), channel_id=1, source_target_pairs={{0,2},{1,3},{2,4},{3,5},{4,6},{5,7},{6,8},{7,9},{8,10},{9,11},{10,... | collective-permute-start | bytes 774152 | tf_op jit(solution)/shard_map/ppermute | solution.py:26
  19.9 0.7 fusion.157
  20.5 3.4 %collective-permute-start.6 = (f32[4,2,36,128]{3,0,2,1:T(4,128)S(1)}, f32[4,2,36,128]{3,0,2,1:T(4,128)S(1)}, u32[]{:S(2)}, u32[]{:S(2)}) collective-permute-start(f32[4,2,36,128]{3,0,2,1:T(4,128)S(1)} %get-tuple-element.81), channel_id=1, source_target_pairs={{0,128},{64,192},{128,256},{192,320},{256,384},{320,448},{1,129},{... | collective-permute-start | bytes 442376 | tf_op jit(solution)/shard_map/ppermute | solution.py:26
  24.2 0.6 fusion.168
  24.8 0.6 fusion.167
  39.5 2.1 %collective-permute-start.4 = (f32[4,6,36,128]{3,0,2,1:T(4,128)S(1)}, f32[4,6,36,128]{3,0,2,1:T(4,128)}, u32[]{:S(2)}, u32[]{:S(2)}) collective-permute-start(f32[4,6,36,128]{3,0,2,1:T(4,128)S(1)} %get-tuple-element.79), channel_id=1, source_target_pairs={{0,64},{64,128},{128,192},{192,256},{256,320},{320,384},{384,448},... | collective-permute-start | bytes 1327112 | tf_op jit(solution)/shard_map/ppermute | solution.py:26
  41.6 0.7 constant_dynamic-update-slice_fusion.4
  42.2 1.3 %collective-permute-start.5 = (f32[4,6,36,128]{3,0,2,1:T(4,128)S(1)}, f32[4,6,36,128]{3,0,2,1:T(4,128)}, u32[]{:S(2)}, u32[]{:S(2)}) collective-permute-start(f32[4,6,36,128]{3,0,2,1:T(4,128)S(1)} %get-tuple-element.79), channel_id=1, source_target_pairs={{64,0},{128,64},{192,128},{256,192},{320,256},{384,320},{448,384},... | collective-permute-start | bytes 1327112 | tf_op jit(solution)/shard_map/ppermute | solution.py:26
  43.5 1.3 %collective-permute-start.7 = (f32[4,2,36,128]{3,0,2,1:T(4,128)}, f32[4,2,36,128]{3,0,2,1:T(4,128)}, u32[]{:S(2)}, u32[]{:S(2)}) collective-permute-start(f32[4,2,36,128]{3,0,2,1:T(4,128)} %get-tuple-element.80), channel_id=1, source_target_pairs={{128,0},{192,64},{256,128},{320,192},{384,256},{448,320},{129,1},{... | collective-permute-start | bytes 442376 | tf_op jit(solution)/shard_map/ppermute | solution.py:26
  45.0 0.9 multiply_reduce_fusion
  46.0 0.4 fusion.94
  46.4 0.3 fusion.151
  46.7 0.7 slice_multiply_fusion.11
  47.9 0.7 slice_multiply_fusion.9
  48.7 0.3 fusion.149
  49.1 0.7 slice_multiply_fusion.7
  50.2 0.5 slice_multiply_fusion.28
  51.0 0.4 slice_multiply_fusion.26
  51.6 0.4 slice_multiply_fusion.24
  52.3 0.4 slice_multiply_fusion.22
  52.7 0.8 slice_multiply_fusion.21
  53.8 0.4 fusion.96
  54.2 0.3 fusion.155
  54.5 0.6 slice_multiply_fusion.5
  55.1 0.3 fusion.154
  55.5 0.6 slice_multiply_fusion.3
  56.5 0.6 slice_multiply_fusion.1
  57.2 0.3 fusion.152
  57.5 0.3 slice_multiply_fusion.20
  58.1 0.3 slice_multiply_fusion.18
  59.0 0.4 fusion.164
  59.7 0.8 slice_multiply_fusion.13
  60.5 0.9 %fusion.163 = (f32[5,6,18,127]{3,0,2,1:T(8,128)S(1)}, f32[5,6,18,127]{3,0,2,1:T(8,128)}) fusion(f32[5,6,18,128]{3,0,2,1:T(8,128)S(1)} %get-tuple-element.42), kind=kLoop, calls=%fused_computation.300 | loop fusion | bytes 1097280 | tf_op jit(solution)/shard_map/slice | solution.py:121
  61.5 17.4 %psum.7 = f32[4,128]{1,0:T(4,128)S(1)} all-reduce(f32[4,128]{1,0:T(4,128)} %get-tuple-element.116), channel_id=1, replica_groups=mesh['freq'=8,'geo'=64] {'freq'}, use_global_device_ids=true, to_apply=%region_2.0 | all-reduce | flops 512 | bytes 4096 | tf_op jit(solution)/shard_map/psum | solution.py:173
  78.9 2.2 %fusion.106 = (f32[4,6,18,128]{3,0,2,1:T(4,128)S(1)}, f32[4,6,18,128]{3,0,2,1:T(4,128)S(1)}) fusion(f32[5,6,18,128]{3,0,2,1:T(8,128)} %slice_multiply_fusion.21, f32[5,6,18,127]{3,0,2,1:T(8,128)S(1)} %get-tuple-element.83, f32[5,6,18,127]{3,0,2,1:T(8,128)S(1)} %get-tuple-element.82, f32[5,6,18,128]{3,0,2,1:T(8,128)S(1)} %get-tuple-element.28, ...), kind=kLoop, calls=%fused_computation.209 | loop fusion | flops 884736 | bytes 3311204 | tf_op jit(solution)/shard_map/mul | solution.py:139
  81.1 0.6 multiply_add_fusion
  81.7 1.1 %constant_dynamic-update-slice_fusion.3 = f32[4,22,36,128]{3,0,2,1:T(4,128)S(1)} fusion(f32[4,22,36,128]{3,0,2,1:T(4,128)S(1)} %copy-done, f32[4,6,36,128]{3,0,2,1:T(4,128)} %collective-permute-done.4), kind=kLoop, calls=%fused_computation.255 | loop fusion | bytes 884736
  82.9 1.1 %constant_dynamic-update-slice_fusion.1 = f32[4,22,36,128]{3,0,2,1:T(4,128)S(1)} fusion(f32[4,22,36,128]{3,0,2,1:T(4,128)S(1)} %constant_dynamic-update-slice_fusion.2, f32[4,6,36,128]{3,0,2,1:T(4,128)} %collective-permute-done.5), kind=kLoop, calls=%fused_computation.253 | loop fusion | bytes 884736
  84.0 0.9 %constant_dynamic-update-slice_fusion = f32[4,22,36,128]{3,0,2,1:T(4,128)S(1)} fusion(f32[4,22,36,128]{3,0,2,1:T(4,128)S(1)} %constant_dynamic-update-slice_fusion.1, f32[4,2,36,128]{3,0,2,1:T(4,128)} %collective-permute-done.7), kind=kLoop, calls=%fused_computation.252 | loop fusion | bytes 294912 | tf_op jit(solution)/shard_map/concatenate | solution.py:177
  84.9 4.8 %subtract_multiply_fusion = f32[4,14,36,128]{3,0,2,1:T(4,128)S(1)} fusion(s32[]{:T(128)S(6)} %select_n.212, s32[]{:T(128)S(6)} %select_n.211, f32[4,22,36,128]{3,0,2,1:T(4,128)S(1)} %constant_dynamic-update-slice_fusion, s32[]{:T(128)S(6)} %select_n.209, s32[]{:T(128)S(6)} %select_n.208, s32[]{:T(128)S(6)} %select_n.207, s32[]{:T(128)S(6)} %select_n.205, ...), kind=kLoop, calls=%fused_computation.28 | loop fusion | flops 5677056 | bytes 3981352 | tf_op jit(solution)/shard_map/mul | solution.py:102
  89.8 3.1 %fusion.93 = f32[4,6,36,128]{3,0,2,1:T(4,128)} fusion(f32[4,6,36,128]{3,0,2,1:T(4,128)S(1)} %get-tuple-element.79, f32[4,6,18,128]{3,0,2,1:T(4,128)S(1)} %get-tuple-element.119, f32[4,6,18,128]{3,0,2,1:T(4,128)S(1)} %get-tuple-element.118, f32[4,14,36,128]{3,0,2,1:T(4,128)S(1)} %subtract_multiply_fusion, s32[]{:T(128)S(6)} %select_n.220, s32[]{:T(128)S(6)} %select_n.219, ...), kind=kLoop, calls=%fused_computation.190 | loop fusion | flops 2211840 | bytes 2805800 | tf_op jit(solution)/shard_map/mul | solution.py:215
  (71 shorter events, 4.5 us)
Async XLA Ops:
  0.6 2.5 %copy-start.4 = (f32[4,128]{1,0:T(4,128)S(1)}, f32[4,128]{1,0:T(4,128)}, u32[]{:S(2)}) copy-start(f32[4,128]{1,0:T(4,128)} %param.12) | copy-start | bytes 6148
  1.9 22.3 %copy-start.1 = (s32[4]{0:T(128)S(1)}, s32[4]{0:T(128)}, u32[]{:S(2)}) copy-start(s32[4]{0:T(128)} %param.16) | copy-start | bytes 52
  1.9 22.9 %copy-start.5 = (f32[2]{0:T(128)S(1)}, f32[2]{0:T(128)}, u32[]{:S(2)}) copy-start(f32[2]{0:T(128)} %param.17) | copy-start | bytes 28
  3.9 39.6 %collective-permute-start.2 = (f32[4,7,18,128]{3,0,2,1:T(4,128)S(1)}, f32[4,7,18,128]{3,0,2,1:T(4,128)S(1)}, u32[]{:S(2)}, u32[]{:S(2)}) collective-permute-start(f32[4,7,18,128]{3,0,2,1:T(4,128)S(1)} %get-tuple-element.113), channel_id=1, source_target_pairs={{1,0},{2,1},{3,2},{4,3},{5,4},{6,5},{7,6},{8,7},{9,8},{10,9},{11,1... | collective-permute-start | bytes 774152 | tf_op jit(solution)/shard_map/ppermute | solution.py:26
  7.2 37.7 %collective-permute-start.3 = (f32[4,7,18,128]{3,0,2,1:T(4,128)S(1)}, f32[4,7,18,128]{3,0,2,1:T(4,128)S(1)}, u32[]{:S(2)}, u32[]{:S(2)}) collective-permute-start(f32[4,7,18,128]{3,0,2,1:T(4,128)S(1)} %get-tuple-element.113), channel_id=1, source_target_pairs={{2,0},{3,1},{4,2},{5,3},{6,4},{7,5},{8,6},{9,7},{10,8},{11,9},{12,... | collective-permute-start | bytes 774152 | tf_op jit(solution)/shard_map/ppermute | solution.py:26
  11.2 31.0 %collective-permute-start = (f32[4,7,18,128]{3,0,2,1:T(4,128)S(1)}, f32[4,7,18,128]{3,0,2,1:T(4,128)S(1)}, u32[]{:S(2)}, u32[]{:S(2)}) collective-permute-start(f32[4,7,18,128]{3,0,2,1:T(4,128)S(1)} %get-tuple-element.112), channel_id=1, source_target_pairs={{0,1},{1,2},{2,3},{3,4},{4,5},{5,6},{6,7},{7,8},{8,9},{9,10},{10,1... | collective-permute-start | bytes 774152 | tf_op jit(solution)/shard_map/ppermute | solution.py:26
  17.1 27.7 %collective-permute-start.1 = (f32[4,7,18,128]{3,0,2,1:T(4,128)S(1)}, f32[4,7,18,128]{3,0,2,1:T(4,128)S(1)}, u32[]{:S(2)}, u32[]{:S(2)}) collective-permute-start(f32[4,7,18,128]{3,0,2,1:T(4,128)S(1)} %get-tuple-element.112), channel_id=1, source_target_pairs={{0,2},{1,3},{2,4},{3,5},{4,6},{5,7},{6,8},{7,9},{8,10},{9,11},{10,... | collective-permute-start | bytes 774152 | tf_op jit(solution)/shard_map/ppermute | solution.py:26
  20.5 19.0 %collective-permute-start.6 = (f32[4,2,36,128]{3,0,2,1:T(4,128)S(1)}, f32[4,2,36,128]{3,0,2,1:T(4,128)S(1)}, u32[]{:S(2)}, u32[]{:S(2)}) collective-permute-start(f32[4,2,36,128]{3,0,2,1:T(4,128)S(1)} %get-tuple-element.81), channel_id=1, source_target_pairs={{0,128},{64,192},{128,256},{192,320},{256,384},{320,448},{1,129},{... | collective-permute-start | bytes 442376 | tf_op jit(solution)/shard_map/ppermute | solution.py:26
  39.5 42.2 %collective-permute-start.4 = (f32[4,6,36,128]{3,0,2,1:T(4,128)S(1)}, f32[4,6,36,128]{3,0,2,1:T(4,128)}, u32[]{:S(2)}, u32[]{:S(2)}) collective-permute-start(f32[4,6,36,128]{3,0,2,1:T(4,128)S(1)} %get-tuple-element.79), channel_id=1, source_target_pairs={{0,64},{64,128},{128,192},{192,256},{256,320},{320,384},{384,448},... | collective-permute-start | bytes 1327112 | tf_op jit(solution)/shard_map/ppermute | solution.py:26
  42.2 40.6 %collective-permute-start.5 = (f32[4,6,36,128]{3,0,2,1:T(4,128)S(1)}, f32[4,6,36,128]{3,0,2,1:T(4,128)}, u32[]{:S(2)}, u32[]{:S(2)}) collective-permute-start(f32[4,6,36,128]{3,0,2,1:T(4,128)S(1)} %get-tuple-element.79), channel_id=1, source_target_pairs={{64,0},{128,64},{192,128},{256,192},{320,256},{384,320},{448,384},... | collective-permute-start | bytes 1327112 | tf_op jit(solution)/shard_map/ppermute | solution.py:26
  43.5 40.4 %collective-permute-start.7 = (f32[4,2,36,128]{3,0,2,1:T(4,128)}, f32[4,2,36,128]{3,0,2,1:T(4,128)}, u32[]{:S(2)}, u32[]{:S(2)}) collective-permute-start(f32[4,2,36,128]{3,0,2,1:T(4,128)} %get-tuple-element.80), channel_id=1, source_target_pairs={{128,0},{192,64},{256,128},{320,192},{384,256},{448,320},{129,1},{... | collective-permute-start | bytes 442376 | tf_op jit(solution)/shard_map/ppermute | solution.py:26
  78.9 2.2 %copy-start.2 = (s32[4,128]{1,0:T(4,128)S(1)}, s32[4,128]{1,0:T(4,128)}, u32[]{:S(2)}) copy-start(s32[4,128]{1,0:T(4,128)} %param.14) | copy-start | bytes 6148
  78.9 2.3 %copy-start.3 = (f32[4,128]{1,0:T(4,128)S(1)}, f32[4,128]{1,0:T(4,128)}, u32[]{:S(2)}) copy-start(f32[4,128]{1,0:T(4,128)} %param.15) | copy-start | bytes 6148
  78.9 2.9 %copy-start = (f32[4,22,36,128]{3,0,2,1:T(4,128)S(1)}, f32[4,22,36,128]{3,0,2,1:T(4,128)}, u32[]{:S(2)}) copy-start(f32[4,22,36,128]{3,0,2,1:T(4,128)} %constant_dynamic-update-slice_fusion.4) | copy-start | bytes 4866052

commit v2 on v1

--- a/solution.py
+++ b/solution.py
@@ -42,6 +42,16 @@
         need -= take
         distance += 1
     return parts
+
+
+def butterfly_sum(value, axis):
+    count = lax.axis_size(axis)
+    assert count & (count - 1) == 0
+    step = 1
+    while step < count:
+        value = value + lax.ppermute(value, axis, [(i, i ^ step) for i in range(count)])
+        step *= 2
+    return value
 
 
 def physics(radian_freq, water_depth, dir_count):
@@ -170,7 +180,7 @@
 
     group_speed, orbit_weight = physics(radian_freq, water_depth, dir_count)
     partial_value = jnp.sum(orbit_weight * jnp.sum(energy, axis=2), axis=1)
-    orbital = jnp.sqrt(lax.psum(partial_value, "freq"))
+    orbital = jnp.sqrt(butterfly_sum(partial_value, "freq"))
     full_step = SUBSTEPS * sub_step
     damping = 1.0 + full_step * canopy * veg_field * orbital
 
@@ -181,7 +191,7 @@
     geo_index = lax.axis_index("geo")
     geo_count = lax.axis_size("geo")
 
-    def unpack(parts, offsets, own, own_speed, own_wet):
+    def unpack(parts, offsets):
         spectra, speeds, wets = [], [], []
         for part, offset in zip(parts, offsets):
             valid = (geo_index + offset >= 0) & (geo_index + offset < geo_count)
@@ -192,7 +202,7 @@
         return spectra, speeds, wets
 
     n_off = [-(len(below) - k) for k in range(len(below))]
-    b_spec, b_speed, b_wet = unpack(below, n_off, None, None, None)
+    b_spec, b_speed, b_wet = unpack(below, n_off)
     north = propagate(
         jnp.concatenate(b_spec + [masked[:, :, :half]], axis=0),
         jnp.concatenate(b_speed + [group_speed], axis=0),
@@ -202,7 +212,7 @@
         True,
     )
     s_off = [k + 1 for k in range(len(above))]
-    a_spec, a_speed, a_wet = unpack(above, s_off, None, None, None)
+    a_spec, a_speed, a_wet = unpack(above, s_off)
     south = propagate(
         jnp.concatenate([masked[:, :, half:]] + a_spec, axis=0),
         jnp.concatenate([group_speed] + a_speed, axis=0),

time: 93.6 us -> 84.2 us (0.90)
  the two profiles are of different devices: /device:TPU:248 before, /device:TPU:254 now
where the time goes in v2:
time: 84.2 us; the launch traced here: 83.5 us
  starting transfers between devices  34.7 us (41%)
  other arithmetic  19.7 us (23%)
  between operations  15 us (18%)
  local copies, waits for them, and re-layouts  7.12 us (8%)
  waiting for transfers between devices  6.97 us (8%)
    ppermute x8, starting transfers between devices, from_neighbour(): return lax.ppermute(block, axis, pairs)  27.3 us
    mul x16, other arithmetic, propagate(): east_flux = east_speed[lo:hi] * spectrum  7.59 us
    ppermute x3, starting transfers between devices, butterfly_sum(): lax.ppermute(value, axis, [(i, i ^ step) for i in range(count)])  7.42 us
    ppermute x3, waiting for transfers between devices, butterfly_sum(): lax.ppermute(value, axis, [(i, i ^ step) for i in range(count)])  6.95 us
    slice x16, local copies, waits for them, and re-layouts, east_west(): behind = jnp.concatenate([zeros, east_flux[..., :-1]], axis=-1)  4.14 us
    mul x1, other arithmetic, source_change(): coupling * (centre * centre * (coef_plus * upper + coef_minus * lower) -...  3.97 us
    mul x1, other arithmetic, body(): return (wet_four * (moved + increment), orbital)  3.24 us
  transfers between devices with their start and end apart: 11, of which 3 were waited for; matrix products, arithmetic and copies ran while one was open for 20% of the time, Pallas kernels for 0%

profile of v2, /device:TPU:254, one launch (start us, length us, event | category | flops | bytes accessed | tf_op | source)
XLA Modules:
  0.0 83.5 jit_solution(9433969576541111193)
XLA Ops:
  0.6 0.7 convert_bitcast_fusion
  1.3 0.6 slice.595
  1.9 1.1 %fusion.156 = (f32[4,6,128]{2,0,1:T(4,128)S(1)}, f32[4,6,36,128]{3,0,2,1:T(4,128)S(1)}) fusion(f32[4,6,36,128]{3,0,2,1:T(4,128)} %param.11, f32[4,128]{1,0:T(4,128)S(1)} %get-tuple-element.125), kind=kLoop, calls=%fused_computation.294 | loop fusion | flops 218112 | bytes 899072 | tf_op jit(solution)/shard_map/reduce_sum | solution.py:182
  3.1 0.7 constant_dynamic-update-slice_fusion.5
  3.9 3.3 %collective-permute-start.2 = (f32[4,7,18,128]{3,0,2,1:T(4,128)S(1)}, f32[4,7,18,128]{3,0,2,1:T(4,128)S(1)}, u32[]{:S(2)}, u32[]{:S(2)}) collective-permute-start(f32[4,7,18,128]{3,0,2,1:T(4,128)S(1)} %get-tuple-element.113), channel_id=1, source_target_pairs={{1,0},{2,1},{3,2},{4,3},{5,4},{6,5},{7,6},{8,7},{9,8},{10,9},{11,1... | collective-permute-start | bytes 774152 | tf_op jit(solution)/shard_map/ppermute | solution.py:26
  7.2 4.0 %collective-permute-start.3 = (f32[4,7,18,128]{3,0,2,1:T(4,128)S(1)}, f32[4,7,18,128]{3,0,2,1:T(4,128)S(1)}, u32[]{:S(2)}, u32[]{:S(2)}) collective-permute-start(f32[4,7,18,128]{3,0,2,1:T(4,128)S(1)} %get-tuple-element.113), channel_id=1, source_target_pairs={{2,0},{3,1},{4,2},{5,3},{6,4},{7,5},{8,6},{9,7},{10,8},{11,9},{12,... | collective-permute-start | bytes 774152 | tf_op jit(solution)/shard_map/ppermute | solution.py:26
  11.2 5.9 %collective-permute-start = (f32[4,7,18,128]{3,0,2,1:T(4,128)S(1)}, f32[4,7,18,128]{3,0,2,1:T(4,128)S(1)}, u32[]{:S(2)}, u32[]{:S(2)}) collective-permute-start(f32[4,7,18,128]{3,0,2,1:T(4,128)S(1)} %get-tuple-element.112), channel_id=1, source_target_pairs={{0,1},{1,2},{2,3},{3,4},{4,5},{5,6},{6,7},{7,8},{8,9},{9,10},{10,1... | collective-permute-start | bytes 774152 | tf_op jit(solution)/shard_map/ppermute | solution.py:26
  17.1 2.7 %collective-permute-start.1 = (f32[4,7,18,128]{3,0,2,1:T(4,128)S(1)}, f32[4,7,18,128]{3,0,2,1:T(4,128)S(1)}, u32[]{:S(2)}, u32[]{:S(2)}) collective-permute-start(f32[4,7,18,128]{3,0,2,1:T(4,128)S(1)} %get-tuple-element.112), channel_id=1, source_target_pairs={{0,2},{1,3},{2,4},{3,5},{4,6},{5,7},{6,8},{7,9},{8,10},{9,11},{10,... | collective-permute-start | bytes 774152 | tf_op jit(solution)/shard_map/ppermute | solution.py:26
  19.9 1.3 %collective-permute-start.6 = (f32[4,2,36,128]{3,0,2,1:T(4,128)S(1)}, f32[4,2,36,128]{3,0,2,1:T(4,128)S(1)}, u32[]{:S(2)}, u32[]{:S(2)}) collective-permute-start(f32[4,2,36,128]{3,0,2,1:T(4,128)S(1)} %get-tuple-element.81), channel_id=1, source_target_pairs={{0,128},{64,192},{128,256},{192,320},{256,384},{320,448},{1,129},{... | collective-permute-start | bytes 442376 | tf_op jit(solution)/shard_map/ppermute | solution.py:26
  21.4 0.6 fusion.168
  22.1 0.7 fusion.167
  36.5 1.9 %collective-permute-start.4 = (f32[4,6,36,128]{3,0,2,1:T(4,128)S(1)}, f32[4,6,36,128]{3,0,2,1:T(4,128)S(1)}, u32[]{:S(2)}, u32[]{:S(2)}) collective-permute-start(f32[4,6,36,128]{3,0,2,1:T(4,128)S(1)} %get-tuple-element.79), channel_id=1, source_target_pairs={{0,64},{64,128},{128,192},{192,256},{256,320},{320,384},{384,448},... | collective-permute-start | bytes 1327112 | tf_op jit(solution)/shard_map/ppermute | solution.py:26
  38.4 3.6 %collective-permute-start.5 = (f32[4,6,36,128]{3,0,2,1:T(4,128)S(1)}, f32[4,6,36,128]{3,0,2,1:T(4,128)S(1)}, u32[]{:S(2)}, u32[]{:S(2)}) collective-permute-start(f32[4,6,36,128]{3,0,2,1:T(4,128)S(1)} %get-tuple-element.79), channel_id=1, source_target_pairs={{64,0},{128,64},{192,128},{256,192},{320,256},{384,320},{448,384},... | collective-permute-start | bytes 1327112 | tf_op jit(solution)/shard_map/ppermute | solution.py:26
  42.1 4.6 %collective-permute-start.7 = (f32[4,2,36,128]{3,0,2,1:T(4,128)S(1)}, f32[4,2,36,128]{3,0,2,1:T(4,128)S(1)}, u32[]{:S(2)}, u32[]{:S(2)}) collective-permute-start(f32[4,2,36,128]{3,0,2,1:T(4,128)S(1)} %get-tuple-element.80), channel_id=1, source_target_pairs={{128,0},{192,64},{256,128},{320,192},{384,256},{448,320},{129,1},{... | collective-permute-start | bytes 442376 | tf_op jit(solution)/shard_map/ppermute | solution.py:26
  46.8 0.3 multiply_reduce_fusion
  47.2 0.4 fusion.94
  47.7 0.3 fusion.151
  48.0 0.7 slice_multiply_fusion.11
  48.7 0.3 fusion.150
  49.2 0.7 slice_multiply_fusion.9
  50.0 0.3 fusion.149
  50.3 0.7 slice_multiply_fusion.7
  51.2 0.3 fusion.148
  51.5 0.5 slice_multiply_fusion.28
  52.3 0.4 slice_multiply_fusion.26
  52.9 0.4 slice_multiply_fusion.24
  53.6 0.4 slice_multiply_fusion.22
  54.3 0.4 fusion.96
  54.8 0.3 fusion.155
  55.1 0.6 slice_multiply_fusion.5
  55.6 0.3 fusion.154
  56.1 0.6 slice_multiply_fusion.3
  56.8 0.3 fusion.153
  57.1 0.6 slice_multiply_fusion.1
  57.8 0.3 fusion.152
  58.1 0.3 slice_multiply_fusion.20
  58.6 0.3 slice_multiply_fusion.18
  59.6 0.4 fusion.164
  59.9 1.9 %collective-permute-start.8 = (f32[4,128]{1,0:T(4,128)S(1)}, f32[4,128]{1,0:T(4,128)S(1)}, u32[]{:S(2)}, u32[]{:S(2)}) collective-permute-start(f32[4,128]{1,0:T(4,128)S(1)} %get-tuple-element.116), channel_id=1, source_target_pairs={{0,64},{64,0},{128,192},{192,128},{256,320},{320,256},{384,448},{4... | collective-permute-start | bytes 6152 | tf_op jit(solution)/shard_map/ppermute | solution.py:52
  62.2 0.8 collective-permute-done.8
  63.0 2.7 %collective-permute-start.9 = (f32[4,128]{1,0:T(4,128)S(1)}, f32[4,128]{1,0:T(4,128)S(1)}, u32[]{:S(2)}, u32[]{:S(2)}) collective-permute-start(f32[4,128]{1,0:T(4,128)S(1)} %add.437), channel_id=1, source_target_pairs={{0,128},{64,192},{128,0},{192,64},{256,384},{320,448},{384,256},{4... | collective-permute-start | bytes 6152 | tf_op jit(solution)/shard_map/ppermute | solution.py:52
  65.9 2.5 %collective-permute-done.9 = f32[4,128]{1,0:T(4,128)S(1)} collective-permute-done((f32[4,128]{1,0:T(4,128)S(1)}, f32[4,128]{1,0:T(4,128)S(1)}, u32[]{:S(2)}, u32[]{:S(2)}) %collective-permute-start.9) | collective-permute-done | bytes 2080 | tf_op jit(solution)/shard_map/ppermute | solution.py:52
  68.5 2.8 %collective-permute-start.10 = (f32[4,128]{1,0:T(4,128)S(1)}, f32[4,128]{1,0:T(4,128)S(1)}, u32[]{:S(2)}, u32[]{:S(2)}) collective-permute-start(f32[4,128]{1,0:T(4,128)S(1)} %add.438), channel_id=1, source_target_pairs={{0,256},{64,320},{128,384},{192,448},{256,0},{320,64},{384,128},{4... | collective-permute-start | bytes 6152 | tf_op jit(solution)/shard_map/ppermute | solution.py:52
  71.3 0.5 fusion.106
  71.8 3.6 %collective-permute-done.10 = f32[4,128]{1,0:T(4,128)S(1)} collective-permute-done((f32[4,128]{1,0:T(4,128)S(1)}, f32[4,128]{1,0:T(4,128)S(1)}, u32[]{:S(2)}, u32[]{:S(2)}) %collective-permute-start.10) | collective-permute-done | bytes 2080 | tf_op jit(solution)/shard_map/ppermute | solution.py:52
  75.4 0.6 multiply_add_fusion
  76.3 4.0 %subtract_multiply_fusion = f32[4,14,36,128]{3,0,2,1:T(4,128)S(1)} fusion(s32[]{:T(128)S(6)} %select_n.212, s32[]{:T(128)S(6)} %select_n.211, f32[4,22,36,128]{3,0,2,1:T(4,128)S(1)} %constant_dynamic-update-slice_fusion, s32[]{:T(128)S(6)} %select_n.209, s32[]{:T(128)S(6)} %select_n.208, s32[]{:T(128)S(6)} %select_n.207, s32[]{:T(128)S(6)} %select_n.205, ...), kind=kLoop, calls=%fused_computation.28 | loop fusion | flops 5677056 | bytes 3981352 | tf_op jit(solution)/shard_map/mul | solution.py:112
  80.3 3.2 %fusion.93 = f32[4,6,36,128]{3,0,2,1:T(4,128)} fusion(f32[4,6,36,128]{3,0,2,1:T(4,128)S(1)} %get-tuple-element.79, f32[4,6,18,128]{3,0,2,1:T(4,128)S(1)} %get-tuple-element.119, f32[4,6,18,128]{3,0,2,1:T(4,128)S(1)} %get-tuple-element.118, f32[4,14,36,128]{3,0,2,1:T(4,128)S(1)} %subtract_multiply_fusion, s32[]{:T(128)S(6)} %select_n.220, s32[]{:T(128)S(6)} %select_n.219, ...), kind=kLoop, calls=%fused_computation.190 | loop fusion | flops 2211840 | bytes 2805800 | tf_op jit(solution)/shard_map/mul | solution.py:225
  (76 shorter events, 4.0 us)
Async XLA Ops:
  0.6 2.5 %copy-start.1 = (f32[4,128]{1,0:T(4,128)S(1)}, f32[4,128]{1,0:T(4,128)}, u32[]{:S(2)}) copy-start(f32[4,128]{1,0:T(4,128)} %param.12) | copy-start | bytes 6148
  1.9 19.5 %copy-start = (s32[4]{0:T(128)S(1)}, s32[4]{0:T(128)}, u32[]{:S(2)}) copy-start(s32[4]{0:T(128)} %param.16) | copy-start | bytes 52
  1.9 20.1 %copy-start.2 = (f32[2]{0:T(128)S(1)}, f32[2]{0:T(128)}, u32[]{:S(2)}) copy-start(f32[2]{0:T(128)} %param.17) | copy-start | bytes 28
  3.9 38.2 %collective-permute-start.2 = (f32[4,7,18,128]{3,0,2,1:T(4,128)S(1)}, f32[4,7,18,128]{3,0,2,1:T(4,128)S(1)}, u32[]{:S(2)}, u32[]{:S(2)}) collective-permute-start(f32[4,7,18,128]{3,0,2,1:T(4,128)S(1)} %get-tuple-element.113), channel_id=1, source_target_pairs={{1,0},{2,1},{3,2},{4,3},{5,4},{6,5},{7,6},{8,7},{9,8},{10,9},{11,1... | collective-permute-start | bytes 774152 | tf_op jit(solution)/shard_map/ppermute | solution.py:26
  7.2 39.5 %collective-permute-start.3 = (f32[4,7,18,128]{3,0,2,1:T(4,128)S(1)}, f32[4,7,18,128]{3,0,2,1:T(4,128)S(1)}, u32[]{:S(2)}, u32[]{:S(2)}) collective-permute-start(f32[4,7,18,128]{3,0,2,1:T(4,128)S(1)} %get-tuple-element.113), channel_id=1, source_target_pairs={{2,0},{3,1},{4,2},{5,3},{6,4},{7,5},{8,6},{9,7},{10,8},{11,9},{12,... | collective-permute-start | bytes 774152 | tf_op jit(solution)/shard_map/ppermute | solution.py:26
  11.2 27.2 %collective-permute-start = (f32[4,7,18,128]{3,0,2,1:T(4,128)S(1)}, f32[4,7,18,128]{3,0,2,1:T(4,128)S(1)}, u32[]{:S(2)}, u32[]{:S(2)}) collective-permute-start(f32[4,7,18,128]{3,0,2,1:T(4,128)S(1)} %get-tuple-element.112), channel_id=1, source_target_pairs={{0,1},{1,2},{2,3},{3,4},{4,5},{5,6},{6,7},{7,8},{8,9},{9,10},{10,1... | collective-permute-start | bytes 774152 | tf_op jit(solution)/shard_map/ppermute | solution.py:26
  17.1 29.6 %collective-permute-start.1 = (f32[4,7,18,128]{3,0,2,1:T(4,128)S(1)}, f32[4,7,18,128]{3,0,2,1:T(4,128)S(1)}, u32[]{:S(2)}, u32[]{:S(2)}) collective-permute-start(f32[4,7,18,128]{3,0,2,1:T(4,128)S(1)} %get-tuple-element.112), channel_id=1, source_target_pairs={{0,2},{1,3},{2,4},{3,5},{4,6},{5,7},{6,8},{7,9},{8,10},{9,11},{10,... | collective-permute-start | bytes 774152 | tf_op jit(solution)/shard_map/ppermute | solution.py:26
  19.9 16.6 %collective-permute-start.6 = (f32[4,2,36,128]{3,0,2,1:T(4,128)S(1)}, f32[4,2,36,128]{3,0,2,1:T(4,128)S(1)}, u32[]{:S(2)}, u32[]{:S(2)}) collective-permute-start(f32[4,2,36,128]{3,0,2,1:T(4,128)S(1)} %get-tuple-element.81), channel_id=1, source_target_pairs={{0,128},{64,192},{128,256},{192,320},{256,384},{320,448},{1,129},{... | collective-permute-start | bytes 442376 | tf_op jit(solution)/shard_map/ppermute | solution.py:26
  36.5 39.6 %collective-permute-start.4 = (f32[4,6,36,128]{3,0,2,1:T(4,128)S(1)}, f32[4,6,36,128]{3,0,2,1:T(4,128)S(1)}, u32[]{:S(2)}, u32[]{:S(2)}) collective-permute-start(f32[4,6,36,128]{3,0,2,1:T(4,128)S(1)} %get-tuple-element.79), channel_id=1, source_target_pairs={{0,64},{64,128},{128,192},{192,256},{256,320},{320,384},{384,448},... | collective-permute-start | bytes 1327112 | tf_op jit(solution)/shard_map/ppermute | solution.py:26
  38.4 37.7 %collective-permute-start.5 = (f32[4,6,36,128]{3,0,2,1:T(4,128)S(1)}, f32[4,6,36,128]{3,0,2,1:T(4,128)S(1)}, u32[]{:S(2)}, u32[]{:S(2)}) collective-permute-start(f32[4,6,36,128]{3,0,2,1:T(4,128)S(1)} %get-tuple-element.79), channel_id=1, source_target_pairs={{64,0},{128,64},{192,128},{256,192},{320,256},{384,320},{448,384},... | collective-permute-start | bytes 1327112 | tf_op jit(solution)/shard_map/ppermute | solution.py:26
  42.1 34.1 %collective-permute-start.7 = (f32[4,2,36,128]{3,0,2,1:T(4,128)S(1)}, f32[4,2,36,128]{3,0,2,1:T(4,128)S(1)}, u32[]{:S(2)}, u32[]{:S(2)}) collective-permute-start(f32[4,2,36,128]{3,0,2,1:T(4,128)S(1)} %get-tuple-element.80), channel_id=1, source_target_pairs={{128,0},{192,64},{256,128},{320,192},{384,256},{448,320},{129,1},{... | collective-permute-start | bytes 442376 | tf_op jit(solution)/shard_map/ppermute | solution.py:26
  59.9 3.0 %collective-permute-start.8 = (f32[4,128]{1,0:T(4,128)S(1)}, f32[4,128]{1,0:T(4,128)S(1)}, u32[]{:S(2)}, u32[]{:S(2)}) collective-permute-start(f32[4,128]{1,0:T(4,128)S(1)} %get-tuple-element.116), channel_id=1, source_target_pairs={{0,64},{64,0},{128,192},{192,128},{256,320},{320,256},{384,448},{4... | collective-permute-start | bytes 6152 | tf_op jit(solution)/shard_map/ppermute | solution.py:52
  63.0 5.5 %collective-permute-start.9 = (f32[4,128]{1,0:T(4,128)S(1)}, f32[4,128]{1,0:T(4,128)S(1)}, u32[]{:S(2)}, u32[]{:S(2)}) collective-permute-start(f32[4,128]{1,0:T(4,128)S(1)} %add.437), channel_id=1, source_target_pairs={{0,128},{64,192},{128,0},{192,64},{256,384},{320,448},{384,256},{4... | collective-permute-start | bytes 6152 | tf_op jit(solution)/shard_map/ppermute | solution.py:52
  68.5 7.0 %collective-permute-start.10 = (f32[4,128]{1,0:T(4,128)S(1)}, f32[4,128]{1,0:T(4,128)S(1)}, u32[]{:S(2)}, u32[]{:S(2)}) collective-permute-start(f32[4,128]{1,0:T(4,128)S(1)} %add.438), channel_id=1, source_target_pairs={{0,256},{64,320},{128,384},{192,448},{256,0},{320,64},{384,128},{4... | collective-permute-start | bytes 6152 | tf_op jit(solution)/shard_map/ppermute | solution.py:52
  71.2 4.2 %copy-start.3 = (s32[4,128]{1,0:T(4,128)S(1)}, s32[4,128]{1,0:T(4,128)}, u32[]{:S(2)}) copy-start(s32[4,128]{1,0:T(4,128)} %param.14) | copy-start | bytes 6148
  71.3 4.2 %copy-start.4 = (f32[4,128]{1,0:T(4,128)S(1)}, f32[4,128]{1,0:T(4,128)}, u32[]{:S(2)}) copy-start(f32[4,128]{1,0:T(4,128)} %param.15) | copy-start | bytes 6148

commit v3 on v2

--- a/solution.py
+++ b/solution.py
@@ -20,13 +20,16 @@
 coef_both = 2.589
 
 
-def from_neighbour(block, axis, distance):
+def from_neighbour(block, axis, distance, cyclic=False):
     count = lax.axis_size(axis)
-    pairs = [(i, i + distance) for i in range(count) if 0 <= i + distance < count]
+    if cyclic:
+        pairs = [(i, (i + distance) % count) for i in range(count)]
+    else:
+        pairs = [(i, i + distance) for i in range(count) if 0 <= i + distance < count]
     return lax.ppermute(block, axis, pairs)
 
 
-def halo(block, axis, dim, width, side):
+def halo(block, axis, dim, width, side, cyclic=False):
     size = block.shape[dim]
     parts = []
     distance = 1
@@ -35,10 +38,10 @@
         take = min(size, need)
         if side < 0:
             piece = lax.slice_in_dim(block, size - take, size, axis=dim)
-            parts.insert(0, from_neighbour(piece, axis, distance))
+            parts.insert(0, from_neighbour(piece, axis, distance, cyclic))
         else:
             piece = lax.slice_in_dim(block, 0, take, axis=dim)
-            parts.append(from_neighbour(piece, axis, -distance))
+            parts.append(from_neighbour(piece, axis, -distance, cyclic))
         need -= take
         distance += 1
     return parts
@@ -52,6 +55,29 @@
         value = value + lax.ppermute(value, axis, [(i, i ^ step) for i in range(count)])
         step *= 2
     return value
+
+
+def gathered_sum(known, index, count, value):
+    reach = max(known)
+    if count > 2 * (2 * reach + 1) - 2 or count % 2:
+        return butterfly_sum(value, "freq")
+    far = count // 2
+    ordered = jnp.stack([known[o] for o in range(-reach, reach + 1)])
+    more = from_neighbour(ordered, "freq", far, True)
+    table = []
+    for rel in range(count):
+        off = rel if rel <= reach else rel - count
+        if -reach <= off <= reach:
+            table.append(known[off])
+        else:
+            table.append(more[rel - far + reach])
+    table = jnp.stack(table)
+    table = jnp.concatenate([table, table], axis=0)
+    start = (count - index) % count
+    glob = lax.dynamic_slice_in_dim(table, start, count, axis=0)
+    while glob.shape[0] > 1:
+        glob = glob[0::2] + glob[1::2]
+    return glob[0]
 
 
 def physics(radian_freq, water_depth, dir_count):
@@ -175,12 +201,42 @@
     below = halo(north_msg, "geo", 0, SUBSTEPS, -1)
     above = halo(south_msg, "geo", 0, SUBSTEPS, +1)
 
-    low_bins = halo(masked, "freq", 1, 2 * FH, -1)
-    high_bins = halo(masked, "freq", 1, 2 * FH, +1)
-
     group_speed, orbit_weight = physics(radian_freq, water_depth, dir_count)
     partial_value = jnp.sum(orbit_weight * jnp.sum(energy, axis=2), axis=1)
-    orbital = jnp.sqrt(butterfly_sum(partial_value, "freq"))
+
+    freq_index = lax.axis_index("freq")
+    freq_total = lax.axis_size("freq")
+    slot = jnp.zeros((tile_rows, 1, dir_count, tile_cols), jnp.float32)
+    slot = slot.at[:, 0, 0, :].set(partial_value)
+
+    def tagged_halo(side):
+        pieces = []
+        distance = 1
+        need = 2 * FH
+        while need > 0:
+            take = min(freq_count, need)
+            lo = freq_count - take if side < 0 else 0
+            piece = jnp.concatenate(
+                [lax.slice_in_dim(masked, lo, lo + take, axis=1), slot], axis=1
+            )
+            got = from_neighbour(piece, "freq", -side * distance, True)
+            source = freq_index + side * distance
+            inside = (source >= 0) & (source < freq_total)
+            pieces.append(
+                (distance * side, jnp.where(inside, got[:, :take], 0.0), got[:, take, 0, :])
+            )
+            need -= take
+            distance += 1
+        return pieces
+
+    low = tagged_halo(-1)
+    high = tagged_halo(+1)
+    low_bins = [p[1] for p in reversed(low)]
+    high_bins = [p[1] for p in high]
+    known = {0: partial_value}
+    for offset, _, value in low + high:
+        known[offset] = value
+    orbital = jnp.sqrt(gathered_sum(known, freq_index, freq_total, partial_value))
     full_step = SUBSTEPS * sub_step
     damping = 1.0 + full_step * canopy * veg_field * orbital
 

time: 84.2 us -> 79 us (0.938)
  the two profiles are of different devices: /device:TPU:254 before, /device:TPU:2 now
where the time goes in v3:
time: 79 us; the launch traced here: 78.4 us
  starting transfers between devices  32.9 us (42%)
  other arithmetic  20.2 us (26%)
  between operations  15.9 us (20%)
  local copies, waits for them, and re-layouts  6.89 us (9%)
  waiting for transfers between devices  2.56 us (3%)
    ppermute x9, starting transfers between devices, from_neighbour(): return lax.ppermute(block, axis, pairs)  32.9 us
    mul x16, other arithmetic, propagate(): east_flux = east_speed[lo:hi] * spectrum  7.76 us
    slice x16, local copies, waits for them, and re-layouts, east_west(): behind = jnp.concatenate([zeros, east_flux[..., :-1]], axis=-1)  3.96 us
    mul x1, other arithmetic, source_change(): coupling * (centre * centre * (coef_plus * upper + coef_minus * lower) -...  3.8 us
    mul x1, other arithmetic, body(): return (wet_four * (moved + increment), orbital)  3.06 us
    ppermute x9, waiting for transfers between devices, from_neighbour(): return lax.ppermute(block, axis, pairs)  2.56 us
  transfers between devices with their start and end apart: 9, of which 2 were waited for; matrix products, arithmetic and copies ran while one was open for 25% of the time, Pallas kernels for 0%

profile of v3, /device:TPU:2, one launch (start us, length us, event | category | flops | bytes accessed | tf_op | source)
XLA Modules:
  0.0 78.4 jit_solution(11672768703510828983)
XLA Ops:
  0.6 0.7 convert_bitcast_fusion
  1.3 0.6 slice.672
  1.9 1.1 %fusion.162 = (f32[4,6,128]{2,0,1:T(4,128)S(1)}, f32[4,6,36,128]{3,0,2,1:T(4,128)S(1)}) fusion(f32[4,6,36,128]{3,0,2,1:T(4,128)} %param.13, f32[4,128]{1,0:T(4,128)S(1)} %get-tuple-element.149), kind=kLoop, calls=%fused_computation.328 | loop fusion | flops 218112 | bytes 899072 | tf_op jit(solution)/shard_map/reduce_sum | solution.py:205
  3.1 0.7 constant_dynamic-update-slice_fusion.20
  3.9 1.3 %collective-permute-start.2 = (f32[4,7,18,128]{3,0,2,1:T(4,128)S(1)}, f32[4,7,18,128]{3,0,2,1:T(4,128)S(1)}, u32[]{:S(2)}, u32[]{:S(2)}) collective-permute-start(f32[4,7,18,128]{3,0,2,1:T(4,128)S(1)} %get-tuple-element.135), channel_id=1, source_target_pairs={{1,0},{2,1},{3,2},{4,3},{5,4},{6,5},{7,6},{8,7},{9,8},{10,9},{11,1... | collective-permute-start | bytes 774152 | tf_op jit(solution)/shard_map/ppermute | solution.py:29
  5.2 1.3 %collective-permute-start.3 = (f32[4,7,18,128]{3,0,2,1:T(4,128)S(1)}, f32[4,7,18,128]{3,0,2,1:T(4,128)S(1)}, u32[]{:S(2)}, u32[]{:S(2)}) collective-permute-start(f32[4,7,18,128]{3,0,2,1:T(4,128)S(1)} %get-tuple-element.135), channel_id=1, source_target_pairs={{2,0},{3,1},{4,2},{5,3},{6,4},{7,5},{8,6},{9,7},{10,8},{11,9},{12,... | collective-permute-start | bytes 774152 | tf_op jit(solution)/shard_map/ppermute | solution.py:29
  6.5 4.6 %collective-permute-start = (f32[4,7,18,128]{3,0,2,1:T(4,128)S(1)}, f32[4,7,18,128]{3,0,2,1:T(4,128)S(1)}, u32[]{:S(2)}, u32[]{:S(2)}) collective-permute-start(f32[4,7,18,128]{3,0,2,1:T(4,128)S(1)} %get-tuple-element.134), channel_id=1, source_target_pairs={{0,1},{1,2},{2,3},{3,4},{4,5},{5,6},{6,7},{7,8},{8,9},{9,10},{10,1... | collective-permute-start | bytes 774152 | tf_op jit(solution)/shard_map/ppermute | solution.py:29
  11.1 5.4 %collective-permute-start.1 = (f32[4,7,18,128]{3,0,2,1:T(4,128)S(1)}, f32[4,7,18,128]{3,0,2,1:T(4,128)S(1)}, u32[]{:S(2)}, u32[]{:S(2)}) collective-permute-start(f32[4,7,18,128]{3,0,2,1:T(4,128)S(1)} %get-tuple-element.134), channel_id=1, source_target_pairs={{0,2},{1,3},{2,4},{3,5},{4,6},{5,7},{6,8},{7,9},{8,10},{9,11},{10,... | collective-permute-start | bytes 774152 | tf_op jit(solution)/shard_map/ppermute | solution.py:29
  16.8 0.6 fusion.172
  17.4 0.7 fusion.173
  32.8 0.3 multiply_reduce_fusion
  33.3 1.7 %collective-permute-start.5 = (f32[4,7,36,128]{3,0,2,1:T(4,128)S(1)}, f32[4,7,36,128]{3,0,2,1:T(4,128)S(1)}, u32[]{:S(2)}, u32[]{:S(2)}) collective-permute-start(f32[4,7,36,128]{3,0,2,1:T(4,128)S(1)} %pad_maximum_fusion.4), channel_id=1, source_target_pairs={{0,448},{64,0},{128,64},{192,128},{256,192},{320,256},{384,320},{4... | collective-permute-start | bytes 1548296 | tf_op jit(solution)/shard_map/ppermute | solution.py:29
  35.1 0.4 fusion.94
  35.6 0.3 fusion.156
  35.9 0.7 slice_multiply_fusion.11
  36.6 0.3 fusion.155
  37.1 0.7 slice_multiply_fusion.9
  37.9 0.3 fusion.154
  38.2 0.7 slice_multiply_fusion.7
  39.1 0.3 fusion.153
  39.4 0.5 slice_multiply_fusion.28
  40.0 0.2 fusion.166
  40.2 0.4 slice_multiply_fusion.26
  40.6 0.2 fusion.165
  40.8 0.4 slice_multiply_fusion.24
  41.3 0.2 fusion.164
  41.5 0.4 slice_multiply_fusion.22
  42.2 0.4 fusion.96
  42.7 0.3 fusion.160
  43.0 0.6 slice_multiply_fusion.5
  43.5 0.3 fusion.159
  44.0 0.6 slice_multiply_fusion.3
  44.7 0.3 fusion.158
  45.0 0.6 slice_multiply_fusion.1
  45.7 0.3 fusion.157
  46.0 0.3 slice_multiply_fusion.20
  46.5 0.5 slice_multiply_fusion.18
  47.3 0.3 slice_multiply_fusion.16
  47.8 0.3 slice_multiply_fusion.14
  48.5 3.4 %collective-permute-start.6 = (f32[4,3,36,128]{3,0,2,1:T(4,128)S(1)}, f32[4,3,36,128]{3,0,2,1:T(4,128)S(1)}, u32[]{:S(2)}, u32[]{:S(2)}) collective-permute-start(f32[4,3,36,128]{3,0,2,1:T(4,128)S(1)} %get-tuple-element.129), channel_id=1, source_target_pairs={{0,128},{64,192},{128,256},{192,320},{256,384},{320,448},{384,0},{... | collective-permute-start | bytes 663560 | tf_op jit(solution)/shard_map/ppermute | solution.py:29
  51.9 7.5 %collective-permute-start.7 = (f32[4,3,36,128]{3,0,2,1:T(4,128)S(1)}, f32[4,3,36,128]{3,0,2,1:T(4,128)S(1)}, u32[]{:S(2)}, u32[]{:S(2)}) collective-permute-start(f32[4,3,36,128]{3,0,2,1:T(4,128)S(1)} %get-tuple-element.128), channel_id=1, source_target_pairs={{0,384},{64,448},{128,0},{192,64},{256,128},{320,192},{384,256},{4... | collective-permute-start | bytes 663560 | tf_op jit(solution)/shard_map/ppermute | solution.py:29
  59.4 0.5 fusion.106
  60.0 1.4 %collective-permute-done.6 = f32[4,3,36,128]{3,0,2,1:T(4,128)S(1)} collective-permute-done((f32[4,3,36,128]{3,0,2,1:T(4,128)S(1)}, f32[4,3,36,128]{3,0,2,1:T(4,128)S(1)}, u32[]{:S(2)}, u32[]{:S(2)}) %collective-permute-start.6) | collective-permute-done | bytes 221216 | tf_op jit(solution)/shard_map/ppermute | solution.py:29
  61.7 1.1 %collective-permute-done.7 = f32[4,3,36,128]{3,0,2,1:T(4,128)S(1)} collective-permute-done((f32[4,3,36,128]{3,0,2,1:T(4,128)S(1)}, f32[4,3,36,128]{3,0,2,1:T(4,128)S(1)}, u32[]{:S(2)}, u32[]{:S(2)}) %collective-permute-start.7) | collective-permute-done | bytes 221216 | tf_op jit(solution)/shard_map/ppermute | solution.py:29
  62.9 7.6 %collective-permute-start.8 = (f32[5,4,128]{2,1,0:T(4,128)S(1)}, f32[5,4,128]{2,1,0:T(4,128)S(1)}, u32[]{:S(2)}, u32[]{:S(2)}) collective-permute-start(f32[5,4,128]{2,1,0:T(4,128)S(1)} %get-tuple-element.126), channel_id=1, source_target_pairs={{0,256},{64,320},{128,384},{192,448},{256,0},{320,64},{384,128},{4... | collective-permute-start | bytes 30728 | tf_op jit(solution)/shard_map/ppermute | solution.py:29
  70.8 3.8 %subtract_multiply_fusion = f32[4,14,36,128]{3,0,2,1:T(4,128)S(1)} fusion(s32[]{:T(128)S(6)} %select_n.255, s32[]{:T(128)S(6)} %select_n.254, f32[4,22,36,128]{3,0,2,1:T(4,128)S(1)} %fusion.108, s32[]{:T(128)S(6)} %select_n.252, s32[]{:T(128)S(6)} %select_n.251, s32[]{:T(128)S(6)} %select_n.250, s32[]{:T(128)S(6)} %select_n.248, ...), kind=kLoop, calls=%fused_computation.28 | loop fusion | flops 5677056 | bytes 3981352 | tf_op jit(solution)/shard_map/mul | solution.py:138
  74.8 0.6 multiply_add_fusion
  75.4 3.1 %fusion.93 = f32[4,6,36,128]{3,0,2,1:T(4,128)} fusion(f32[4,6,36,128]{3,0,2,1:T(4,128)S(1)} %get-tuple-element.99, f32[4,6,18,128]{3,0,2,1:T(4,128)S(1)} %get-tuple-element.143, f32[4,6,18,128]{3,0,2,1:T(4,128)S(1)} %get-tuple-element.142, f32[4,14,36,128]{3,0,2,1:T(4,128)S(1)} %subtract_multiply_fusion, s32[]{:T(128)S(6)} %select_n.263, s32[]{:T(128)S(6)} %select_n.262, ...), kind=kLoop, calls=%fused_computation.193 | loop fusion | flops 2211840 | bytes 2805800 | tf_op jit(solution)/shard_map/mul | solution.py:281
  (90 shorter events, 3.7 us)
Async XLA Ops:
  0.6 2.5 %copy-start.1 = (f32[4,128]{1,0:T(4,128)S(1)}, f32[4,128]{1,0:T(4,128)}, u32[]{:S(2)}) copy-start(f32[4,128]{1,0:T(4,128)} %param.14) | copy-start | bytes 6148
  1.9 14.9 %copy-start.2 = (f32[2]{0:T(128)S(1)}, f32[2]{0:T(128)}, u32[]{:S(2)}) copy-start(f32[2]{0:T(128)} %param.19) | copy-start | bytes 28
  1.9 15.5 %copy-start = (s32[4]{0:T(128)S(1)}, s32[4]{0:T(128)}, u32[]{:S(2)}) copy-start(s32[4]{0:T(128)} %param.18) | copy-start | bytes 52
  3.9 28.7 %collective-permute-start.2 = (f32[4,7,18,128]{3,0,2,1:T(4,128)S(1)}, f32[4,7,18,128]{3,0,2,1:T(4,128)S(1)}, u32[]{:S(2)}, u32[]{:S(2)}) collective-permute-start(f32[4,7,18,128]{3,0,2,1:T(4,128)S(1)} %get-tuple-element.135), channel_id=1, source_target_pairs={{1,0},{2,1},{3,2},{4,3},{5,4},{6,5},{7,6},{8,7},{9,8},{10,9},{11,1... | collective-permute-start | bytes 774152 | tf_op jit(solution)/shard_map/ppermute | solution.py:29
  5.2 27.5 %collective-permute-start.3 = (f32[4,7,18,128]{3,0,2,1:T(4,128)S(1)}, f32[4,7,18,128]{3,0,2,1:T(4,128)S(1)}, u32[]{:S(2)}, u32[]{:S(2)}) collective-permute-start(f32[4,7,18,128]{3,0,2,1:T(4,128)S(1)} %get-tuple-element.135), channel_id=1, source_target_pairs={{2,0},{3,1},{4,2},{5,3},{6,4},{7,5},{8,6},{9,7},{10,8},{11,9},{12,... | collective-permute-start | bytes 774152 | tf_op jit(solution)/shard_map/ppermute | solution.py:29
  6.5 26.1 %collective-permute-start = (f32[4,7,18,128]{3,0,2,1:T(4,128)S(1)}, f32[4,7,18,128]{3,0,2,1:T(4,128)S(1)}, u32[]{:S(2)}, u32[]{:S(2)}) collective-permute-start(f32[4,7,18,128]{3,0,2,1:T(4,128)S(1)} %get-tuple-element.134), channel_id=1, source_target_pairs={{0,1},{1,2},{2,3},{3,4},{4,5},{5,6},{6,7},{7,8},{8,9},{9,10},{10,1... | collective-permute-start | bytes 774152 | tf_op jit(solution)/shard_map/ppermute | solution.py:29
  11.1 21.6 %collective-permute-start.1 = (f32[4,7,18,128]{3,0,2,1:T(4,128)S(1)}, f32[4,7,18,128]{3,0,2,1:T(4,128)S(1)}, u32[]{:S(2)}, u32[]{:S(2)}) collective-permute-start(f32[4,7,18,128]{3,0,2,1:T(4,128)S(1)} %get-tuple-element.134), channel_id=1, source_target_pairs={{0,2},{1,3},{2,4},{3,5},{4,6},{5,7},{6,8},{7,9},{8,10},{9,11},{10,... | collective-permute-start | bytes 774152 | tf_op jit(solution)/shard_map/ppermute | solution.py:29
  33.3 28.1 %collective-permute-start.4 = (f32[4,7,36,128]{3,0,2,1:T(4,128)S(1)}, f32[4,7,36,128]{3,0,2,1:T(4,128)S(1)}, u32[]{:S(2)}, u32[]{:S(2)}) collective-permute-start(f32[4,7,36,128]{3,0,2,1:T(4,128)S(1)} %pad_maximum_fusion.4), channel_id=1, source_target_pairs={{0,64},{64,128},{128,192},{192,256},{256,320},{320,384},{384,448},... | collective-permute-start | bytes 1548296 | tf_op jit(solution)/shard_map/ppermute | solution.py:29
  33.3 28.4 %collective-permute-start.5 = (f32[4,7,36,128]{3,0,2,1:T(4,128)S(1)}, f32[4,7,36,128]{3,0,2,1:T(4,128)S(1)}, u32[]{:S(2)}, u32[]{:S(2)}) collective-permute-start(f32[4,7,36,128]{3,0,2,1:T(4,128)S(1)} %pad_maximum_fusion.4), channel_id=1, source_target_pairs={{0,448},{64,0},{128,64},{192,128},{256,192},{320,256},{384,320},{4... | collective-permute-start | bytes 1548296 | tf_op jit(solution)/shard_map/ppermute | solution.py:29
  48.5 12.9 %collective-permute-start.6 = (f32[4,3,36,128]{3,0,2,1:T(4,128)S(1)}, f32[4,3,36,128]{3,0,2,1:T(4,128)S(1)}, u32[]{:S(2)}, u32[]{:S(2)}) collective-permute-start(f32[4,3,36,128]{3,0,2,1:T(4,128)S(1)} %get-tuple-element.129), channel_id=1, source_target_pairs={{0,128},{64,192},{128,256},{192,320},{256,384},{320,448},{384,0},{... | collective-permute-start | bytes 663560 | tf_op jit(solution)/shard_map/ppermute | solution.py:29
  51.9 11.0 %collective-permute-start.7 = (f32[4,3,36,128]{3,0,2,1:T(4,128)S(1)}, f32[4,3,36,128]{3,0,2,1:T(4,128)S(1)}, u32[]{:S(2)}, u32[]{:S(2)}) collective-permute-start(f32[4,3,36,128]{3,0,2,1:T(4,128)S(1)} %get-tuple-element.128), channel_id=1, source_target_pairs={{0,384},{64,448},{128,0},{192,64},{256,128},{320,192},{384,256},{4... | collective-permute-start | bytes 663560 | tf_op jit(solution)/shard_map/ppermute | solution.py:29
  62.9 11.7 %collective-permute-start.8 = (f32[5,4,128]{2,1,0:T(4,128)S(1)}, f32[5,4,128]{2,1,0:T(4,128)S(1)}, u32[]{:S(2)}, u32[]{:S(2)}) collective-permute-start(f32[5,4,128]{2,1,0:T(4,128)S(1)} %get-tuple-element.126), channel_id=1, source_target_pairs={{0,256},{64,320},{128,384},{192,448},{256,0},{320,64},{384,128},{4... | collective-permute-start | bytes 30728 | tf_op jit(solution)/shard_map/ppermute | solution.py:29
  70.8 4.0 %copy-start.3 = (s32[4,128]{1,0:T(4,128)S(1)}, s32[4,128]{1,0:T(4,128)}, u32[]{:S(2)}) copy-start(s32[4,128]{1,0:T(4,128)} %param.16) | copy-start | bytes 6148
  70.8 4.0 %copy-start.4 = (f32[4,128]{1,0:T(4,128)S(1)}, f32[4,128]{1,0:T(4,128)}, u32[]{:S(2)}) copy-start(f32[4,128]{1,0:T(4,128)} %param.17) | copy-start | bytes 6148

commit v4 on v3

--- a/solution.py
+++ b/solution.py
@@ -1,9 +1,14 @@
+import functools
 import math
 
 import jax
 import jax.numpy as jnp
 from jax import lax
+from jax.experimental import pallas as pl
+from jax.experimental.pallas import tpu as pltpu
 from jax.sharding import PartitionSpec as P
+
+INTERPRET = False
 
 FH = 4
 SUBSTEPS = 8
@@ -160,26 +165,50 @@
     return jnp.where(east_going, east_flux - behind, ahead - east_flux)
 
 
-def propagate(spectrum, speed, wet, cosines, sines, northward):
+def propagate_kernel(p_ref, ex_ref, ny_ref, wet_ref, east_ref, o_ref, *, northward):
     step_ratio = sub_step / cell_size
-    east_speed = speed[:, :, None, :] * cosines[None, None, :, None]
-    north_speed = speed[:, :, None, :] * sines[None, None, :, None]
-    rows = spectrum.shape[0]
+    spectrum = p_ref[:, 0]
+    east_speed = ex_ref[:, 0]
+    north_speed = ny_ref[:, 0]
+    wet = wet_ref[...]
+    east_going = east_ref[...] > 0.0
+    rows, _, cols = spectrum.shape
+    col = lax.broadcasted_iota(jnp.int32, spectrum.shape[1:], 1)
     for substep in range(SUBSTEPS):
         lo, hi = (substep, rows) if northward else (0, rows - substep)
         east_flux = east_speed[lo:hi] * spectrum
         north_flux = north_speed[lo:hi] * spectrum
+        behind = jnp.where(col == 0, 0.0, pltpu.roll(east_flux, 1, 2))
+        ahead = jnp.where(col == cols - 1, 0.0, pltpu.roll(east_flux, cols - 1, 2))
+        across = jnp.where(east_going, east_flux - behind, ahead - east_flux)
         along = north_flux[1:] - north_flux[:-1]
-        across = east_west(east_flux, cosines)
         if northward:
-            spectrum = wet[lo + 1 : hi, None, None, :] * (
+            spectrum = wet[lo + 1 : hi, None, :] * (
                 spectrum[1:] - step_ratio * (across[1:] + along)
             )
         else:
-            spectrum = wet[lo : hi - 1, None, None, :] * (
+            spectrum = wet[lo : hi - 1, None, :] * (
                 spectrum[:-1] - step_ratio * (across[:-1] + along)
             )
-    return spectrum
+    o_ref[:, 0] = spectrum
+
+
+def propagate(spectrum, speed, wet, cosines, sines, northward):
+    rows, freq_count, dirs, cols = spectrum.shape
+    out_rows = rows - SUBSTEPS
+    east_speed = speed[:, :, None, :] * cosines[None, None, :, None]
+    north_speed = speed[:, :, None, :] * sines[None, None, :, None]
+    east_going = jnp.broadcast_to((cosines > 0.0).astype(jnp.float32)[:, None], (dirs, cols))
+    block = pl.BlockSpec((rows, 1, dirs, cols), lambda b: (0, b, 0, 0))
+    whole = lambda shape: pl.BlockSpec(shape, lambda b: (0, 0))
+    return pl.pallas_call(
+        functools.partial(propagate_kernel, northward=northward),
+        out_shape=jax.ShapeDtypeStruct((out_rows, freq_count, dirs, cols), jnp.float32),
+        grid=(freq_count,),
+        in_specs=[block, block, block, whole((rows, cols)), whole((dirs, cols))],
+        out_specs=pl.BlockSpec((out_rows, 1, dirs, cols), lambda b: (0, b, 0, 0)),
+        interpret=INTERPRET,
+    )(spectrum, east_speed, north_speed, wet, east_going)
 
 
 def body(energy, water_depth, wet_mask, vegetation, canopy, quad_offsets, quad_weights):

time: 79 us -> 93.9 us (1.19)
  Pallas kernels: 0 us -> 14.2 us
  local copies, waits for them, and re-layouts: 6.89 us -> 12.6 us
  other arithmetic: 20.2 us -> 16.7 us
  waiting for transfers between devices: 2.56 us -> 1.52 us
  between operations: 15.9 us -> 14.9 us
    pallas_call x0 -> x2, Pallas kernels: none -> 14.2 us  [propagate(): pl.pallas_call(functools.partial(propagate_kernel, northward=northward),...]
    mul x31 -> x2, other arithmetic: 9.56 us -> 1.94 us  [the longest x1 1.93 us: propagate(): north_speed = speed[:, :, None, :] * sines[None, None, :, None]]
    slice x22 -> x1, local copies, waits for them, and re-layouts: 3.98 us -> 0.07 us  [body(): cosines[:half]]
    unnamed x23 -> x41, local copies, waits for them, and re-layouts: 0.18 us -> 2.57 us
    concatenate x0 -> x4, local copies, waits for them, and re-layouts: none -> 2.3 us  [the longest x1 1.14 us: body(): jnp.concatenate([masked[:, :, half:]] + a_spec, axis=0)]
    pallas_call x0 -> x2, local copies, waits for them, and re-layouts: none -> 2.1 us  [propagate(): pl.pallas_call(functools.partial(propagate_kernel, northward=northward),...]
    broadcast_in_dim x0 -> x2, local copies, waits for them, and re-layouts: none -> 1.33 us  [propagate(): jnp.broadcast_to((cosines > 0.0).astype(jnp.float32)[:, None], (dirs, cols))]
    ppermute x9, waiting for transfers between devices: 2.56 us -> 1.52 us  [from_neighbour(): return lax.ppermute(block, axis, pairs)]
  transfers between devices with their start and end apart: 9 -> 9, of which waited for: 2 -> 1; matrix products, arithmetic and copies ran while one was open for 25% -> 22% of each run, Pallas kernels for 0% -> 15%
where the time goes in v4:
time: 93.9 us; the launch traced here: 92.8 us
  starting transfers between devices  32.9 us (35%)
  other arithmetic  16.7 us (18%)
  between operations  14.9 us (16%)
  Pallas kernels  14.2 us (15%)
  local copies, waits for them, and re-layouts  12.6 us (13%)
  waiting for transfers between devices  1.52 us (2%)
    ppermute x9, starting transfers between devices, from_neighbour(): return lax.ppermute(block, axis, pairs)  32.9 us
    pallas_call x2, Pallas kernels, propagate(): pl.pallas_call(functools.partial(propagate_kernel, northward=northward),...  14.2 us
    mul x1, other arithmetic, source_change(): coupling * (centre * centre * (coef_plus * upper + coef_minus * lower) -...  3.91 us
    mul x1, other arithmetic, body(): return (wet_four * (moved + increment), orbital)  3.18 us
    unnamed x41, local copies, waits for them, and re-layouts  2.57 us
    pallas_call x2, local copies, waits for them, and re-layouts, propagate(): pl.pallas_call(functools.partial(propagate_kernel, northward=northward),...  2.1 us
    mul x1, other arithmetic, propagate(): north_speed = speed[:, :, None, :] * sines[None, None, :, None]  1.93 us
  transfers between devices with their start and end apart: 9, of which 1 were waited for; matrix products, arithmetic and copies ran while one was open for 22% of the time, Pallas kernels for 15%

profile of v4, /device:TPU:2, one launch (start us, length us, event | category | flops | bytes accessed | tf_op | source)
XLA Modules:
  0.0 92.8 jit_solution(5569563825880514734)
XLA Ops:
  0.6 0.7 convert_bitcast_fusion
  1.3 0.6 slice.226
  1.9 1.1 %fusion.56 = (f32[4,6,128]{2,0,1:T(4,128)S(1)}, f32[4,6,36,128]{3,0,2,1:T(4,128)S(1)}) fusion(f32[4,6,36,128]{3,0,2,1:T(4,128)} %param.13, f32[4,128]{1,0:T(4,128)S(1)} %get-tuple-element.79), kind=kLoop, calls=%fused_computation.158 | loop fusion | flops 218112 | bytes 899072 | tf_op jit(solution)/shard_map/reduce_sum | solution.py:234
  3.1 0.7 constant_dynamic-update-slice_fusion.20
  3.8 0.1 pad_maximum_fusion.6
  3.9 1.3 %collective-permute-start.3 = (f32[4,7,18,128]{3,0,2,1:T(4,128)S(1)}, f32[4,7,18,128]{3,0,2,1:T(4,128)}, u32[]{:S(2)}, u32[]{:S(2)}) collective-permute-start(f32[4,7,18,128]{3,0,2,1:T(4,128)S(1)} %get-tuple-element.69), channel_id=1, source_target_pairs={{2,0},{3,1},{4,2},{5,3},{6,4},{7,5},{8,6},{9,7},{10,8},{11,9},{12,... | collective-permute-start | bytes 774152 | tf_op jit(solution)/shard_map/ppermute | solution.py:34
  5.2 1.3 %collective-permute-start.2 = (f32[4,7,18,128]{3,0,2,1:T(4,128)S(1)}, f32[4,7,18,128]{3,0,2,1:T(4,128)S(1)}, u32[]{:S(2)}, u32[]{:S(2)}) collective-permute-start(f32[4,7,18,128]{3,0,2,1:T(4,128)S(1)} %get-tuple-element.69), channel_id=1, source_target_pairs={{1,0},{2,1},{3,2},{4,3},{5,4},{6,5},{7,6},{8,7},{9,8},{10,9},{11,1... | collective-permute-start | bytes 774152 | tf_op jit(solution)/shard_map/ppermute | solution.py:34
  6.5 4.6 %collective-permute-start.1 = (f32[4,7,18,128]{3,0,2,1:T(4,128)S(1)}, f32[4,7,18,128]{3,0,2,1:T(4,128)S(1)}, u32[]{:S(2)}, u32[]{:S(2)}) collective-permute-start(f32[4,7,18,128]{3,0,2,1:T(4,128)S(1)} %get-tuple-element.68), channel_id=1, source_target_pairs={{0,1},{1,2},{2,3},{3,4},{4,5},{5,6},{6,7},{7,8},{8,9},{9,10},{10,1... | collective-permute-start | bytes 774152 | tf_op jit(solution)/shard_map/ppermute | solution.py:34
  11.1 5.5 %collective-permute-start = (f32[4,7,18,128]{3,0,2,1:T(4,128)S(1)}, f32[4,7,18,128]{3,0,2,1:T(4,128)S(1)}, u32[]{:S(2)}, u32[]{:S(2)}) collective-permute-start(f32[4,7,18,128]{3,0,2,1:T(4,128)S(1)} %get-tuple-element.68), channel_id=1, source_target_pairs={{0,2},{1,3},{2,4},{3,5},{4,6},{5,7},{6,8},{7,9},{8,10},{9,11},{10,... | collective-permute-start | bytes 774152 | tf_op jit(solution)/shard_map/ppermute | solution.py:34
  16.6 0.1 fusion.61
  16.7 0.7 compare_convert_fusion.1
  17.4 0.6 fusion.60
  18.0 0.6 fusion.58
  18.7 0.7 fusion.59
  33.2 0.7 slice_bitcast_fusion.4
  33.9 0.3 multiply_reduce_fusion
  34.2 0.4 copy-done.1
  34.6 0.1 pad_maximum_fusion.4
  34.8 0.0 collective-permute-start.4
  34.8 1.7 %collective-permute-start.5 = (f32[4,7,36,128]{3,0,2,1:T(4,128)S(1)}, f32[4,7,36,128]{3,0,2,1:T(4,128)S(1)}, u32[]{:S(2)}, u32[]{:S(2)}) collective-permute-start(f32[4,7,36,128]{3,0,2,1:T(4,128)S(1)} %pad_maximum_fusion.4), channel_id=1, source_target_pairs={{0,448},{64,0},{128,64},{192,128},{256,192},{320,256},{384,320},{4... | collective-permute-start | bytes 1548296 | tf_op jit(solution)/shard_map/ppermute | solution.py:34
  36.5 0.9 %slice.278 = f32[4,6,18,128]{3,0,2,1:T(4,128)S(1)} slice(f32[4,7,18,128]{3,0,2,1:T(4,128)} %collective-permute-done.3), slice={[0:4], [0:6], [0:18], [0:128]} | slice | bytes 442368 | tf_op jit(solution)/shard_map/slice | solution.py:284
  37.5 0.2 pad_maximum_fusion.3
  37.7 1.1 %copy.16.p_ref = f32[12,6,18,128]{3,2,1,0:T(8,128)} copy(f32[12,6,18,128]{3,0,2,1:T(8,128)S(1)} %pad_maximum_fusion.3) | data formatting | bytes 1327104 | tf_op jit(solution)/shard_map/concatenate | solution.py:302
  38.9 0.9 pad_maximum_fusion.7
  39.8 3.4 %collective-permute-start.6 = (f32[4,3,36,128]{3,0,2,1:T(4,128)}, f32[4,3,36,128]{3,0,2,1:T(4,128)}, u32[]{:S(2)}, u32[]{:S(2)}) collective-permute-start(f32[4,3,36,128]{3,0,2,1:T(4,128)} %get-tuple-element.63), channel_id=1, source_target_pairs={{0,128},{64,192},{128,256},{192,320},{256,384},{320,448},{384,0},{... | collective-permute-start | bytes 663560 | tf_op jit(solution)/shard_map/ppermute | solution.py:34
  43.2 1.9 %broadcast_multiply_fusion = (f32[12,6,18,128]{3,2,1,0:T(8,128)}, f32[12,6,18,128]{3,2,1,0:T(8,128)}, f32[12,6,18,128]{3,2,1,0:T(8,128)}, f32[12,6,18,128]{3,2,1,0:T(8,128)}) fusion(f32[18]{0:T(128)S(1)} %copy-done.7, f32[12,6,128]{2,1,0:T(8,128)S(1)} %copy.15, f32[18]{0:T(128)S(1)} %get-tuple-element.95, f32[18]{0:T(128)S(1)} %get-tuple-element.94, ...), kind=kLoop, calls=%fused_computation.49 | loop fusion | flops 663552 | bytes 2728224 | tf_op jit(solution)/shard_map/mul | solution.py:200
  45.2 0.2 pad_maximum_fusion.2
  45.4 0.6 pad_maximum_fusion.11
  46.0 0.7 broadcast_in_dim.25.east_ref
  46.6 7.0 %shard_map.87 = f32[4,6,18,128]{3,2,1,0:T(8,128)} custom-call(f32[12,6,18,128]{3,2,1,0:T(8,128)} %copy.16.p_ref, f32[12,6,18,128]{3,2,1,0:T(8,128)} %get-tuple-element.67.ex_ref, f32[12,6,18,128]{3,2,1,0:T(8,128)} %get-tuple-element.66.ny_ref, f32[12,128]{1,0:T(8,128)} %get-tuple-element.77.wet_ref, f32[18,128]{1,0:T(8,128)} %broadcast_in_dim.25.east_ref), custom_call_target="tpu_custom_call" | custom-call | tf_op jit(solution)/shard_map/pallas_call | solution.py:204
  53.7 1.0 %copy.18 = f32[4,6,18,128]{3,0,2,1:T(4,128)S(1)} copy(f32[4,6,18,128]{3,2,1,0:T(8,128)} %shard_map.87) | data formatting | bytes 442368 | tf_op jit(solution)/shard_map/pallas_call | solution.py:204
  54.7 1.1 %copy.14.p_ref = f32[12,6,18,128]{3,2,1,0:T(8,128)} copy(f32[12,6,18,128]{3,0,2,1:T(8,128)S(1)} %pad_maximum_fusion.2) | data formatting | bytes 1327104 | tf_op jit(solution)/shard_map/concatenate | solution.py:292
  55.8 0.7 broadcast_in_dim.24.east_ref
  56.5 7.2 %shard_map.86 = f32[4,6,18,128]{3,2,1,0:T(8,128)} custom-call(f32[12,6,18,128]{3,2,1,0:T(8,128)} %copy.14.p_ref, f32[12,6,18,128]{3,2,1,0:T(8,128)} %get-tuple-element.96.ex_ref, f32[12,6,18,128]{3,2,1,0:T(8,128)} %get-tuple-element.97.ny_ref, f32[12,128]{1,0:T(8,128)} %get-tuple-element.76.wet_ref, f32[18,128]{1,0:T(8,128)} %broadcast_in_dim.24.east_ref), custom_call_target="tpu_custom_call" | custom-call | tf_op jit(solution)/shard_map/pallas_call | solution.py:204
  63.7 1.0 %copy.17 = f32[4,6,18,128]{3,0,2,1:T(4,128)S(1)} copy(f32[4,6,18,128]{3,2,1,0:T(8,128)} %shard_map.86) | data formatting | bytes 442368 | tf_op jit(solution)/shard_map/pallas_call | solution.py:204
  64.8 7.5 %collective-permute-start.7 = (f32[4,3,36,128]{3,0,2,1:T(4,128)S(1)}, f32[4,3,36,128]{3,0,2,1:T(4,128)S(1)}, u32[]{:S(2)}, u32[]{:S(2)}) collective-permute-start(f32[4,3,36,128]{3,0,2,1:T(4,128)S(1)} %copy-done), channel_id=1, source_target_pairs={{0,384},{64,448},{128,0},{192,64},{256,128},{320,192},{384,256},{4... | collective-permute-start | bytes 663560 | tf_op jit(solution)/shard_map/ppermute | solution.py:34
  72.4 0.7 constant_dynamic-update-slice_fusion.7
  73.0 0.9 %fusion.25 = f32[4,22,36,128]{3,0,2,1:T(4,128)S(1)} fusion(f32[4,3,36,128]{3,0,2,1:T(4,128)} %collective-permute-done.6, pred[]{:T(512)S(6)} %and.62), kind=kLoop, calls=%fused_computation.62 | loop fusion | flops 36863 | bytes 294913
  74.0 0.2 constant_dynamic-update-slice_fusion.2
  74.2 0.1 constant_dynamic-update-slice_fusion.1
  74.3 1.5 %collective-permute-done.7 = f32[4,3,36,128]{3,0,2,1:T(4,128)S(1)} collective-permute-done((f32[4,3,36,128]{3,0,2,1:T(4,128)S(1)}, f32[4,3,36,128]{3,0,2,1:T(4,128)S(1)}, u32[]{:S(2)}, u32[]{:S(2)}) %collective-permute-start.7) | collective-permute-done | bytes 221216 | tf_op jit(solution)/shard_map/ppermute | solution.py:34
  75.8 7.6 %collective-permute-start.8 = (f32[5,4,128]{2,1,0:T(4,128)S(1)}, f32[5,4,128]{2,1,0:T(4,128)S(1)}, u32[]{:S(2)}, u32[]{:S(2)}) collective-permute-start(f32[5,4,128]{2,1,0:T(4,128)S(1)} %get-tuple-element.60), channel_id=1, source_target_pairs={{0,256},{64,320},{128,384},{192,448},{256,0},{320,64},{384,128},{4... | collective-permute-start | bytes 30728 | tf_op jit(solution)/shard_map/ppermute | solution.py:34
  83.4 0.2 constant_dynamic-update-slice_fusion
  83.7 3.9 %subtract_multiply_fusion = f32[4,14,36,128]{3,0,2,1:T(4,128)S(1)} fusion(s32[]{:T(128)S(6)} %select_n.183, s32[]{:T(128)S(6)} %select_n.182, f32[4,22,36,128]{3,0,2,1:T(4,128)S(1)} %fusion.24, s32[]{:T(128)S(6)} %select_n.180, s32[]{:T(128)S(6)} %select_n.179, s32[]{:T(128)S(6)} %select_n.178, s32[]{:T(128)S(6)} %select_n.176, ...), kind=kLoop, calls=%fused_computation.28 | loop fusion | flops 5677056 | bytes 3981352 | tf_op jit(solution)/shard_map/mul | solution.py:143
  87.6 0.7 constant_dynamic-update-slice_fusion.15
  88.4 0.7 constant_dynamic-update-slice_fusion.9
  89.1 0.6 multiply_add_fusion
  89.7 3.2 %fusion.23 = f32[4,6,36,128]{3,0,2,1:T(4,128)} fusion(f32[4,6,36,128]{3,0,2,1:T(4,128)S(1)} %get-tuple-element.49, f32[4,6,18,128]{3,0,2,1:T(4,128)S(1)} %copy.18, f32[4,6,18,128]{3,0,2,1:T(4,128)S(1)} %copy.17, f32[4,14,36,128]{3,0,2,1:T(4,128)S(1)} %subtract_multiply_fusion, s32[]{:T(128)S(6)} %select_n.191, s32[]{:T(128)S(6)} %select_n.190, ...), kind=kLoop, calls=%fused_computation.53 | loop fusion | flops 2211840 | bytes 2805800 | tf_op jit(solution)/shard_map/mul | solution.py:310
  (69 shorter events, 0.5 us)
Async XLA Ops:
  0.6 2.5 %copy-start.8 = (f32[4,128]{1,0:T(4,128)S(1)}, f32[4,128]{1,0:T(4,128)}, u32[]{:S(2)}) copy-start(f32[4,128]{1,0:T(4,128)} %param.14) | copy-start | bytes 6148
  1.9 16.1 %copy-start.9 = (f32[2]{0:T(128)S(1)}, f32[2]{0:T(128)}, u32[]{:S(2)}) copy-start(f32[2]{0:T(128)} %param.19) | copy-start | bytes 28
  1.9 16.7 %copy-start.5 = (s32[4]{0:T(128)S(1)}, s32[4]{0:T(128)}, u32[]{:S(2)}) copy-start(s32[4]{0:T(128)} %param.18) | copy-start | bytes 52
  3.9 29.3 %collective-permute-start.3 = (f32[4,7,18,128]{3,0,2,1:T(4,128)S(1)}, f32[4,7,18,128]{3,0,2,1:T(4,128)}, u32[]{:S(2)}, u32[]{:S(2)}) collective-permute-start(f32[4,7,18,128]{3,0,2,1:T(4,128)S(1)} %get-tuple-element.69), channel_id=1, source_target_pairs={{2,0},{3,1},{4,2},{5,3},{6,4},{7,5},{8,6},{9,7},{10,8},{11,9},{12,... | collective-permute-start | bytes 774152 | tf_op jit(solution)/shard_map/ppermute | solution.py:34
  5.2 27.9 %collective-permute-start.2 = (f32[4,7,18,128]{3,0,2,1:T(4,128)S(1)}, f32[4,7,18,128]{3,0,2,1:T(4,128)S(1)}, u32[]{:S(2)}, u32[]{:S(2)}) collective-permute-start(f32[4,7,18,128]{3,0,2,1:T(4,128)S(1)} %get-tuple-element.69), channel_id=1, source_target_pairs={{1,0},{2,1},{3,2},{4,3},{5,4},{6,5},{7,6},{8,7},{9,8},{10,9},{11,1... | collective-permute-start | bytes 774152 | tf_op jit(solution)/shard_map/ppermute | solution.py:34
  6.5 26.6 %collective-permute-start.1 = (f32[4,7,18,128]{3,0,2,1:T(4,128)S(1)}, f32[4,7,18,128]{3,0,2,1:T(4,128)S(1)}, u32[]{:S(2)}, u32[]{:S(2)}) collective-permute-start(f32[4,7,18,128]{3,0,2,1:T(4,128)S(1)} %get-tuple-element.68), channel_id=1, source_target_pairs={{0,1},{1,2},{2,3},{3,4},{4,5},{5,6},{6,7},{7,8},{8,9},{9,10},{10,1... | collective-permute-start | bytes 774152 | tf_op jit(solution)/shard_map/ppermute | solution.py:34
  11.1 22.8 %collective-permute-start = (f32[4,7,18,128]{3,0,2,1:T(4,128)S(1)}, f32[4,7,18,128]{3,0,2,1:T(4,128)S(1)}, u32[]{:S(2)}, u32[]{:S(2)}) collective-permute-start(f32[4,7,18,128]{3,0,2,1:T(4,128)S(1)} %get-tuple-element.68), channel_id=1, source_target_pairs={{0,2},{1,3},{2,4},{3,5},{4,6},{5,7},{6,8},{7,9},{8,10},{9,11},{10,... | collective-permute-start | bytes 774152 | tf_op jit(solution)/shard_map/ppermute | solution.py:34
  33.2 1.1 %copy-start.3 = (f32[4,7,18,128]{3,0,2,1:T(4,128)}, f32[4,7,18,128]{3,0,2,1:T(4,128)S(1)}, u32[]{:S(2)}) copy-start(f32[4,7,18,128]{3,0,2,1:T(4,128)S(1)} %collective-permute-done.2) | copy-start | bytes 774148
  33.9 0.7 copy-start.1
  34.6 2.8 %copy-start.4 = (f32[4,7,18,128]{3,0,2,1:T(4,128)S(1)}, f32[4,7,18,128]{3,0,2,1:T(4,128)}, u32[]{:S(2)}) copy-start(f32[4,7,18,128]{3,0,2,1:T(4,128)} %copy-done.3) | copy-start | bytes 774148
  34.8 39.2 %collective-permute-start.4 = (f32[4,7,36,128]{3,0,2,1:T(4,128)S(1)}, f32[4,7,36,128]{3,0,2,1:T(4,128)S(1)}, u32[]{:S(2)}, u32[]{:S(2)}) collective-permute-start(f32[4,7,36,128]{3,0,2,1:T(4,128)S(1)} %pad_maximum_fusion.4), channel_id=1, source_target_pairs={{0,64},{64,128},{128,192},{192,256},{256,320},{320,384},{384,448},... | collective-permute-start | bytes 1548296 | tf_op jit(solution)/shard_map/ppermute | solution.py:34
  34.8 39.5 %collective-permute-start.5 = (f32[4,7,36,128]{3,0,2,1:T(4,128)S(1)}, f32[4,7,36,128]{3,0,2,1:T(4,128)S(1)}, u32[]{:S(2)}, u32[]{:S(2)}) collective-permute-start(f32[4,7,36,128]{3,0,2,1:T(4,128)S(1)} %pad_maximum_fusion.4), channel_id=1, source_target_pairs={{0,448},{64,0},{128,64},{192,128},{256,192},{320,256},{384,320},{4... | collective-permute-start | bytes 1548296 | tf_op jit(solution)/shard_map/ppermute | solution.py:34
  37.7 5.5 %copy-start.6 = (f32[18]{0:T(128)S(1)}, f32[18]{0:T(128)}, u32[]{:S(2)}) copy-start(f32[18]{0:T(128)} %get-tuple-element.92) | copy-start | bytes 220
  37.7 5.5 %copy-start.7 = (f32[18]{0:T(128)S(1)}, f32[18]{0:T(128)}, u32[]{:S(2)}) copy-start(f32[18]{0:T(128)} %get-tuple-element.93) | copy-start | bytes 220
  39.8 32.6 %collective-permute-start.6 = (f32[4,3,36,128]{3,0,2,1:T(4,128)}, f32[4,3,36,128]{3,0,2,1:T(4,128)}, u32[]{:S(2)}, u32[]{:S(2)}) collective-permute-start(f32[4,3,36,128]{3,0,2,1:T(4,128)} %get-tuple-element.63), channel_id=1, source_target_pairs={{0,128},{64,192},{128,256},{192,320},{256,384},{320,448},{384,0},{... | collective-permute-start | bytes 663560 | tf_op jit(solution)/shard_map/ppermute | solution.py:34
  43.2 2.0 %copy-start.2 = (f32[4,7,18,128]{3,0,2,1:T(4,128)S(1)}, f32[4,7,18,128]{3,0,2,1:T(4,128)}, u32[]{:S(2)}) copy-start(f32[4,7,18,128]{3,0,2,1:T(4,128)} %copy-done.1) | copy-start | bytes 774148
  45.1 0.8 copy-start.11
  53.6 2.2 %copy-start.10 = (f32[18]{0:T(128)S(1)}, f32[18]{0:T(128)}, u32[]{:S(2)}) copy-start(f32[18]{0:T(128)} %get-tuple-element.90) | copy-start | bytes 220
  56.5 8.3 %copy-start = (f32[4,3,36,128]{3,0,2,1:T(4,128)S(1)}, f32[4,3,36,128]{3,0,2,1:T(4,128)}, u32[]{:S(2)}) copy-start(f32[4,3,36,128]{3,0,2,1:T(4,128)} %get-tuple-element.62) | copy-start | bytes 663556
  64.8 11.0 %collective-permute-start.7 = (f32[4,3,36,128]{3,0,2,1:T(4,128)S(1)}, f32[4,3,36,128]{3,0,2,1:T(4,128)S(1)}, u32[]{:S(2)}, u32[]{:S(2)}) collective-permute-start(f32[4,3,36,128]{3,0,2,1:T(4,128)S(1)} %copy-done), channel_id=1, source_target_pairs={{0,384},{64,448},{128,0},{192,64},{256,128},{320,192},{384,256},{4... | collective-permute-start | bytes 663560 | tf_op jit(solution)/shard_map/ppermute | solution.py:34
  75.8 11.8 %collective-permute-start.8 = (f32[5,4,128]{2,1,0:T(4,128)S(1)}, f32[5,4,128]{2,1,0:T(4,128)S(1)}, u32[]{:S(2)}, u32[]{:S(2)}) collective-permute-start(f32[5,4,128]{2,1,0:T(4,128)S(1)} %get-tuple-element.60), channel_id=1, source_target_pairs={{0,256},{64,320},{128,384},{192,448},{256,0},{320,64},{384,128},{4... | collective-permute-start | bytes 30728 | tf_op jit(solution)/shard_map/ppermute | solution.py:34
  83.7 5.4 %copy-start.12 = (s32[4,128]{1,0:T(4,128)S(1)}, s32[4,128]{1,0:T(4,128)}, u32[]{:S(2)}) copy-start(s32[4,128]{1,0:T(4,128)} %param.16) | copy-start | bytes 6148
  83.7 5.4 %copy-start.13 = (f32[4,128]{1,0:T(4,128)S(1)}, f32[4,128]{1,0:T(4,128)}, u32[]{:S(2)}) copy-start(f32[4,128]{1,0:T(4,128)} %param.17) | copy-start | bytes 6148

commit v5 on v3

--- a/solution.py
+++ b/solution.py
@@ -208,39 +208,21 @@
     freq_total = lax.axis_size("freq")
     slot = jnp.zeros((tile_rows, 1, dir_count, tile_cols), jnp.float32)
     slot = slot.at[:, 0, 0, :].set(partial_value)
-
-    def tagged_halo(side):
-        pieces = []
-        distance = 1
-        need = 2 * FH
-        while need > 0:
-            take = min(freq_count, need)
-            lo = freq_count - take if side < 0 else 0
-            piece = jnp.concatenate(
-                [lax.slice_in_dim(masked, lo, lo + take, axis=1), slot], axis=1
-            )
-            got = from_neighbour(piece, "freq", -side * distance, True)
-            source = freq_index + side * distance
-            inside = (source >= 0) & (source < freq_total)
-            pieces.append(
-                (distance * side, jnp.where(inside, got[:, :take], 0.0), got[:, take, 0, :])
-            )
-            need -= take
-            distance += 1
-        return pieces
-
-    low = tagged_halo(-1)
-    high = tagged_halo(+1)
-    low_bins = [p[1] for p in reversed(low)]
-    high_bins = [p[1] for p in high]
-    known = {0: partial_value}
-    for offset, _, value in low + high:
-        known[offset] = value
-    orbital = jnp.sqrt(gathered_sum(known, freq_index, freq_total, partial_value))
+    gathered = lax.all_gather(jnp.concatenate([masked, slot], axis=1), "freq", axis=1, tiled=True)
+    gathered = gathered.reshape(tile_rows, freq_total, freq_count + 1, dir_count, tile_cols)
+    partials = gathered[:, :, freq_count, 0, :]
+    spectrum_all = gathered[:, :, :freq_count].reshape(
+        tile_rows, freq_total * freq_count, dir_count, tile_cols
+    )
+    padded_all = jnp.pad(spectrum_all, ((0, 0), (2 * FH, 2 * FH), (0, 0), (0, 0)))
+    extended = lax.dynamic_slice_in_dim(padded_all, first_bin, freq_count + 4 * FH, axis=1)
+    glob = jnp.moveaxis(partials, 1, 0)
+    while glob.shape[0] > 1:
+        glob = glob[0::2] + glob[1::2]
+    orbital = jnp.sqrt(glob[0])
     full_step = SUBSTEPS * sub_step
     damping = 1.0 + full_step * canopy * veg_field * orbital
 
-    extended = jnp.concatenate(low_bins + [masked] + high_bins, axis=1)
     change = source_change(extended, quad_offsets, quad_weights, freq_count)
     increment = (masked + full_step * change) / damping[:, None, None, :] - masked
 

time: 79 us -> 116 us (1.47)
  the two profiles are of different devices: /device:TPU:2 before, /device:TPU:1 now
where the time goes in v5:
time: 116 us; the launch traced here: 115 us
  waiting for transfers between devices  34.5 us (30%)
  between operations  28 us (24%)
  other arithmetic  22.8 us (20%)
  local copies, waits for them, and re-layouts  17.7 us (15%)
  starting transfers between devices  12.3 us (11%)
    all_gather x1, waiting for transfers between devices, body(): lax.all_gather(jnp.concatenate([masked, slot], axis=1), 'freq', axis=1, t...  34.5 us
    ppermute x4, starting transfers between devices, from_neighbour(): return lax.ppermute(block, axis, pairs)  12.3 us
    mul x16, other arithmetic, propagate(): east_flux = east_speed[lo:hi] * spectrum  8.76 us
    slice x16, local copies, waits for them, and re-layouts, east_west(): behind = jnp.concatenate([zeros, east_flux[..., :-1]], axis=-1)  3.96 us
    mul x1, other arithmetic, source_change(): coupling * (centre * centre * (coef_plus * upper + coef_minus * lower) -...  3.75 us
    slice x6, local copies, waits for them, and re-layouts, propagate(): wet[lo + 1:hi, None, None, :]  3.61 us
    mul x1, other arithmetic, body(): return (wet_four * (moved + increment), orbital)  3.01 us
  transfers between devices with their start and end apart: 5, of which 1 were waited for; matrix products, arithmetic and copies ran while one was open for 11% of the time, Pallas kernels for 0%

profile of v5, /device:TPU:1, one launch (start us, length us, event | category | flops | bytes accessed | tf_op | source)
XLA Modules:
  0.0 115.2 jit_solution(11909362313528127280)
XLA Ops:
  7.2 0.7 fusion.169
  7.9 1.1 fusion.159
  9.1 0.6 slice.640
  9.7 1.3 %constant_dynamic-update-slice_fusion = f32[4,1,18,128]{3,0,2,1:T(4,128)S(1)} fusion(f32[4,1,18,128]{3,0,2,1:T(4,128)S(1)} %scatter.10, s32[]{:T(128)} %bitcast.2, f32[4,128]{1,0:T(4,128)} %param.14), kind=kLoop, calls=%fused_computation.258 | loop fusion | bytes 4100 | tf_op jit(solution)/shard_map/scatter | solution.py:198
  11.1 1.3 %collective-permute-start.2 = (f32[4,7,18,128]{3,0,2,1:T(4,128)S(1)}, f32[4,7,18,128]{3,0,2,1:T(4,128)S(1)}, u32[]{:S(2)}, u32[]{:S(2)}) collective-permute-start(f32[4,7,18,128]{3,0,2,1:T(4,128)S(1)} %get-tuple-element.123), channel_id=1, source_target_pairs={{1,0},{2,1},{3,2},{4,3},{5,4},{6,5},{7,6},{8,7},{9,8},{10,9},{11,1... | collective-permute-start | bytes 774152 | tf_op jit(solution)/shard_map/ppermute | solution.py:29
  12.4 1.3 %collective-permute-start.3 = (f32[4,7,18,128]{3,0,2,1:T(4,128)S(1)}, f32[4,7,18,128]{3,0,2,1:T(4,128)S(1)}, u32[]{:S(2)}, u32[]{:S(2)}) collective-permute-start(f32[4,7,18,128]{3,0,2,1:T(4,128)S(1)} %get-tuple-element.123), channel_id=1, source_target_pairs={{2,0},{3,1},{4,2},{5,3},{6,4},{7,5},{8,6},{9,7},{10,8},{11,9},{12,... | collective-permute-start | bytes 774152 | tf_op jit(solution)/shard_map/ppermute | solution.py:29
  13.7 6.5 %collective-permute-start.1 = (f32[4,7,18,128]{3,0,2,1:T(4,128)S(1)}, f32[4,7,18,128]{3,0,2,1:T(4,128)S(1)}, u32[]{:S(2)}, u32[]{:S(2)}) collective-permute-start(f32[4,7,18,128]{3,0,2,1:T(4,128)S(1)} %get-tuple-element.122), channel_id=1, source_target_pairs={{0,2},{1,3},{2,4},{3,5},{4,6},{5,7},{6,8},{7,9},{8,10},{9,11},{10,... | collective-permute-start | bytes 774152 | tf_op jit(solution)/shard_map/ppermute | solution.py:29
  20.2 3.2 %collective-permute-start = (f32[4,7,18,128]{3,0,2,1:T(4,128)S(1)}, f32[4,7,18,128]{3,0,2,1:T(4,128)S(1)}, u32[]{:S(2)}, u32[]{:S(2)}) collective-permute-start(f32[4,7,18,128]{3,0,2,1:T(4,128)S(1)} %get-tuple-element.122), channel_id=1, source_target_pairs={{0,1},{1,2},{2,3},{3,4},{4,5},{5,6},{6,7},{7,8},{8,9},{9,10},{10,1... | collective-permute-start | bytes 774152 | tf_op jit(solution)/shard_map/ppermute | solution.py:29
  23.6 0.5 fusion.172
  24.1 1.3 %fusion.170 = (f32[1]{0:T(128)}, f32[1]{0:T(128)}) fusion(f32[2]{0:T(128)} %param.19), kind=kLoop, calls=%fused_computation.307 | loop fusion | bytes 16 | tf_op jit(solution)/shard_map/slice | solution.py:128
  25.4 1.5 %fusion.171 = (s32[1]{0:T(128)}, s32[1]{0:T(128)}, s32[1]{0:T(128)}, s32[1]{0:T(128)}) fusion(s32[4]{0:T(128)} %param.18), kind=kLoop, calls=%fused_computation.308 | loop fusion | bytes 32 | tf_op jit(solution)/shard_map/slice | solution.py:125
  40.5 0.6 slice.815
  41.1 0.6 slice.814
  41.7 0.6 slice.813
  42.3 0.6 slice.644
  42.9 0.6 slice.643
  43.5 0.6 slice.642
  44.1 1.0 multiply_reduce_fusion
  45.1 0.6 pad_maximum_fusion.4
  45.8 0.4 fusion.96
  46.2 0.3 fusion.158
  46.6 0.6 slice_multiply_fusion.5
  47.6 0.6 slice_multiply_fusion.3
  48.1 0.3 fusion.156
  48.6 0.6 slice_multiply_fusion.1
  49.6 0.3 slice_multiply_fusion.20
  50.2 0.3 slice_multiply_fusion.18
  51.9 0.9 select_maximum_fusion
  52.8 1.0 slice.817
  53.8 1.2 %fusion.94 = (f32[12,6,18,128]{3,0,2,1:T(8,128)S(1)}, f32[12,6,18,128]{3,0,2,1:T(8,128)S(1)}, f32[12,6,18,128]{3,0,2,1:T(8,128)S(1)}, f32[12,6,18,128]{3,0,2,1:T(8,128)S(1)}, f32[12,6,18,128]{3,0,2,1:T(8,128)S(1)}) fusion(f32[18]{0:T(128)} %get-tuple-element.155, f32[12,6,128]{2,0,1:T(8,128)} %get-tuple-element.124, ...), kind=kLoop, calls=%fused_computation.195 | loop fusion | flops 995328 | bytes 4018320 | tf_op jit(solution)/shard_map/mul | solution.py:170
  55.1 0.3 fusion.154
  55.4 0.8 slice_multiply_fusion.11
  56.8 0.8 slice_multiply_fusion.9
  57.6 0.3 fusion.152
  58.3 0.8 slice_multiply_fusion.7
  59.1 0.3 fusion.151
  59.5 0.5 slice_multiply_fusion.28
  60.3 0.4 slice_multiply_fusion.26
  61.0 0.6 slice_multiply_fusion.24
  61.8 0.4 slice_multiply_fusion.22
  62.5 0.6 fusion.106
  63.2 34.5 %all-gather.2.cloned.1.call-done = f32[4,56,36,128]{3,0,2,1:T(4,128)} async-done(((f32[4,7,36,128]{3,0,2,1:T(4,128)}), f32[4,56,36,128]{3,0,2,1:T(4,128)}) %all-gather.2.cloned.1.call-update) | async-done | bytes 4128784 | tf_op jit(solution)/shard_map/all_gather | solution.py:211
  97.6 2.2 %slice.954 = f32[4,8,6,36,128]{4,0,3,2,1:T(4,128)S(1)} slice(f32[4,8,7,36,128]{4,0,3,2,1:T(4,128)} %bitcast.61), slice={[0:4], [0:8], [0:6], [0:36], [0:128]} | slice | bytes 7077888 | tf_op jit(solution)/shard_map/slice | solution.py:214
  99.9 0.7 slice_bitcast_fusion
  100.6 0.3 pad_dynamic-slice_fusion.1
  101.0 0.6 multiply_add_fusion
  101.6 3.8 %subtract_multiply_fusion = f32[4,14,36,128]{3,0,2,1:T(4,128)S(1)} fusion(s32[]{:T(128)S(6)} %select_n.216, s32[]{:T(128)S(6)} %select_n.215, f32[4,22,36,128]{3,0,2,1:T(4,128)S(1)} %pad_dynamic-slice_fusion.1, s32[]{:T(128)S(6)} %select_n.213, s32[]{:T(128)S(6)} %select_n.212, s32[]{:T(128)S(6)} %select_n.211, s32[]{:T(128)S(6)} %select_n.209, ...), kind=kLoop, calls=%fused_computation.28 | loop fusion | flops 5160960 | bytes 6193196 | tf_op jit(solution)/shard_map/mul | solution.py:138
  105.4 3.0 %fusion.93 = f32[4,6,36,128]{3,0,2,1:T(4,128)} fusion(f32[4,6,18,128]{3,0,2,1:T(4,128)S(1)} %get-tuple-element.129, f32[4,6,18,128]{3,0,2,1:T(4,128)S(1)} %get-tuple-element.128, f32[4,14,36,128]{3,0,2,1:T(4,128)S(1)} %subtract_multiply_fusion, s32[]{:T(128)S(6)} %select_n.224, s32[]{:T(128)S(6)} %select_n.223, s32[]{:T(128)S(6)} %select_n.221, ...), kind=kLoop, calls=%fused_computation.192 | loop fusion | flops 2322432 | bytes 2805800 | tf_op jit(solution)/shard_map/mul | solution.py:263
  (76 shorter events, 5.4 us)
Async XLA Ops:
  7.2 90.5 %all-gather.2.cloned.1.call-start = ((), (), s32[]{:S(2)}) async-start(), calls=%async_computation | async-start | bytes 4644864 | tf_op jit(solution)/shard_map/all_gather | solution.py:211
  11.1 29.2 %collective-permute-start.2 = (f32[4,7,18,128]{3,0,2,1:T(4,128)S(1)}, f32[4,7,18,128]{3,0,2,1:T(4,128)S(1)}, u32[]{:S(2)}, u32[]{:S(2)}) collective-permute-start(f32[4,7,18,128]{3,0,2,1:T(4,128)S(1)} %get-tuple-element.123), channel_id=1, source_target_pairs={{1,0},{2,1},{3,2},{4,3},{5,4},{6,5},{7,6},{8,7},{9,8},{10,9},{11,1... | collective-permute-start | bytes 774152 | tf_op jit(solution)/shard_map/ppermute | solution.py:29
  12.4 28.0 %collective-permute-start.3 = (f32[4,7,18,128]{3,0,2,1:T(4,128)S(1)}, f32[4,7,18,128]{3,0,2,1:T(4,128)S(1)}, u32[]{:S(2)}, u32[]{:S(2)}) collective-permute-start(f32[4,7,18,128]{3,0,2,1:T(4,128)S(1)} %get-tuple-element.123), channel_id=1, source_target_pairs={{2,0},{3,1},{4,2},{5,3},{6,4},{7,5},{8,6},{9,7},{10,8},{11,9},{12,... | collective-permute-start | bytes 774152 | tf_op jit(solution)/shard_map/ppermute | solution.py:29
  13.7 26.7 %collective-permute-start.1 = (f32[4,7,18,128]{3,0,2,1:T(4,128)S(1)}, f32[4,7,18,128]{3,0,2,1:T(4,128)S(1)}, u32[]{:S(2)}, u32[]{:S(2)}) collective-permute-start(f32[4,7,18,128]{3,0,2,1:T(4,128)S(1)} %get-tuple-element.122), channel_id=1, source_target_pairs={{0,2},{1,3},{2,4},{3,5},{4,6},{5,7},{6,8},{7,9},{8,10},{9,11},{10,... | collective-permute-start | bytes 774152 | tf_op jit(solution)/shard_map/ppermute | solution.py:29
  20.2 20.2 %collective-permute-start = (f32[4,7,18,128]{3,0,2,1:T(4,128)S(1)}, f32[4,7,18,128]{3,0,2,1:T(4,128)S(1)}, u32[]{:S(2)}, u32[]{:S(2)}) collective-permute-start(f32[4,7,18,128]{3,0,2,1:T(4,128)S(1)} %get-tuple-element.122), channel_id=1, source_target_pairs={{0,1},{1,2},{2,3},{3,4},{4,5},{5,6},{6,7},{7,8},{8,9},{9,10},{10,1... | collective-permute-start | bytes 774152 | tf_op jit(solution)/shard_map/ppermute | solution.py:29
  40.4 5.4 %copy-start.2 = (f32[4,7,18,128]{3,0,2,1:T(4,128)}, f32[4,7,18,128]{3,0,2,1:T(4,128)S(1)}, u32[]{:S(2)}) copy-start(f32[4,7,18,128]{3,0,2,1:T(4,128)S(1)} %collective-permute-done) | copy-start | bytes 774148
  40.4 6.1 %copy-start.1 = (f32[4,7,18,128]{3,0,2,1:T(4,128)}, f32[4,7,18,128]{3,0,2,1:T(4,128)S(1)}, u32[]{:S(2)}) copy-start(f32[4,7,18,128]{3,0,2,1:T(4,128)S(1)} %collective-permute-done.1) | copy-start | bytes 774148
  51.7 2.1 %slice-start = ((f32[4,7,18,128]{3,0,2,1:T(4,128)}), f32[4,6,18,128]{3,0,2,1:T(4,128)S(1)}, s32[]{:S(2)}) async-start(f32[4,7,18,128]{3,0,2,1:T(4,128)} %copy-done.1), calls=%async_computation.1 | async-start | bytes 442368 | tf_op jit(solution)/shard_map/slice | solution.py:237
  53.8 1.6 %copy-start.5 = (f32[11,128]{1,0:T(8,128)S(1)}, f32[11,128]{1,0:T(8,128)}, u32[]{:S(2)}) copy-start(f32[11,128]{1,0:T(8,128)} %slice.815) | copy-start | bytes 16900
  56.1 0.7 copy-start.4
  57.6 0.7 copy-start.3
  59.5 0.8 copy-start.8
  60.3 0.7 copy-start.7
  61.0 0.9 copy-start.6
  99.9 1.1 copy-start.9
  99.9 1.1 copy-start.10
  101.0 4.4 %copy-start = (f32[4,6,36,128]{3,0,2,1:T(4,128)S(1)}, f32[4,6,36,128]{3,0,2,1:T(4,128)}, u32[]{:S(2)}) copy-start(f32[4,6,36,128]{3,0,2,1:T(4,128)} %param.13) | copy-start | bytes 1327108
Sparse Core Ops, SparseCore 0:
  52.9 44.6 all-gather.1

commit v6 on v5

--- a/solution.py
+++ b/solution.py
@@ -118,7 +118,9 @@
     )
 
 
-def source_change(extended, quad_offsets, quad_weights, count):
+def interaction(extended, masked, quad_offsets, quad_weights):
+    count = masked.shape[1]
+    doubled = jnp.concatenate([extended, extended], axis=2)
     up_bins, down_bins, up_turn, down_turn = (
         quad_offsets[0],
         quad_offsets[1],
@@ -126,30 +128,37 @@
         quad_offsets[3],
     )
     weight_up, weight_down = (quad_weights[0], quad_weights[1])
-    wide = count + 2 * FH
+    upper = weight_up * shifted(doubled, FH + up_bins, up_turn, count) + (
+        1.0 - weight_up
+    ) * shifted(doubled, FH + up_bins + 1, up_turn, count)
+    lower = weight_down * shifted(doubled, FH - down_bins, -down_turn, count) + (
+        1.0 - weight_down
+    ) * shifted(doubled, FH - down_bins - 1, -down_turn, count)
+    return coupling * (
+        masked * masked * (coef_plus * upper + coef_minus * lower)
+        - coef_both * masked * upper * lower
+    )
+
+
+def redistribute(extended, transfer, quad_offsets, quad_weights):
+    count = transfer.shape[1]
     doubled = jnp.concatenate([extended, extended], axis=2)
-    centre = lax.slice_in_dim(extended, FH, FH + wide, axis=1)
-    upper = weight_up * shifted(doubled, FH + up_bins, up_turn, wide) + (
+    up_bins, down_bins, up_turn, down_turn = (
+        quad_offsets[0],
+        quad_offsets[1],
+        quad_offsets[2],
+        quad_offsets[3],
+    )
+    weight_up, weight_down = (quad_weights[0], quad_weights[1])
+    gained = weight_up * shifted(doubled, FH - up_bins, -up_turn, count) + (
         1.0 - weight_up
-    ) * shifted(doubled, FH + up_bins + 1, up_turn, wide)
-    lower = weight_down * shifted(doubled, FH - down_bins, -down_turn, wide) + (
-        1.0 - weight_down
-    ) * shifted(doubled, FH - down_bins - 1, -down_turn, wide)
-    transfer = coupling * (
-        centre * centre * (coef_plus * upper + coef_minus * lower)
-        - coef_both * centre * upper * lower
-    )
-    spread = jnp.concatenate([transfer, transfer], axis=2)
-    gained = weight_up * shifted(spread, FH - up_bins, -up_turn, count) + (
-        1.0 - weight_up
-    ) * shifted(spread, FH - up_bins - 1, -up_turn, count)
+    ) * shifted(doubled, FH - up_bins - 1, -up_turn, count)
     gained = (
         gained
-        + weight_down * shifted(spread, FH + down_bins, down_turn, count)
-        + (1.0 - weight_down) * shifted(spread, FH + down_bins + 1, down_turn, count)
-    )
-    own = lax.slice_in_dim(transfer, FH, FH + count, axis=1)
-    return gained - 2.0 * own
+        + weight_down * shifted(doubled, FH + down_bins, down_turn, count)
+        + (1.0 - weight_down) * shifted(doubled, FH + down_bins + 1, down_turn, count)
+    )
+    return gained - 2.0 * transfer
 
 
 def east_west(east_flux, cosines):
@@ -160,12 +169,12 @@
     return jnp.where(east_going, east_flux - behind, ahead - east_flux)
 
 
-def propagate(spectrum, speed, wet, cosines, sines, northward):
+def propagate(spectrum, speed, wet, cosines, sines, northward, substeps):
     step_ratio = sub_step / cell_size
     east_speed = speed[:, :, None, :] * cosines[None, None, :, None]
     north_speed = speed[:, :, None, :] * sines[None, None, :, None]
     rows = spectrum.shape[0]
-    for substep in range(SUBSTEPS):
+    for substep in range(substeps):
         lo, hi = (substep, rows) if northward else (0, rows - substep)
         east_flux = east_speed[lo:hi] * spectrum
         north_flux = north_speed[lo:hi] * spectrum
@@ -182,83 +191,121 @@
     return spectrum
 
 
+def tagged_exchange(block, tags, axis, width):
+    rows, bins, dirs, cols = block.shape
+    index = lax.axis_index(axis)
+    count = lax.axis_size(axis)
+    slot = jnp.zeros((rows, 1, dirs, cols), jnp.float32)
+    for k in range(tags.shape[0]):
+        slot = slot.at[:, 0, k, :].set(tags[k])
+    got = {}
+    for side in (-1, 1):
+        lo = bins - width if side < 0 else 0
+        piece = jnp.concatenate([lax.slice_in_dim(block, lo, lo + width, axis=1), slot], axis=1)
+        recv = from_neighbour(piece, axis, -side, True)
+        source = index + side
+        inside = (source >= 0) & (source < count)
+        got[side] = (
+            jnp.where(inside, recv[:, :width], 0.0),
+            [recv[:, width, k, :] for k in range(tags.shape[0])],
+        )
+    return got
+
+
 def body(energy, water_depth, wet_mask, vegetation, canopy, quad_offsets, quad_weights):
     tile_rows, freq_count, dir_count, tile_cols = energy.shape
     wet_field = wet_mask.astype(jnp.float32)
     veg_field = vegetation.astype(jnp.float32)
     wet_four = wet_field[:, None, None, :]
     masked = wet_four * energy
-    first_bin = lax.axis_index("freq") * freq_count
+    freq_index = lax.axis_index("freq")
+    freq_total = lax.axis_size("freq")
+    first_bin = freq_index * freq_count
     bin_index = (first_bin + jnp.arange(freq_count, dtype=jnp.int32)).astype(jnp.float32)
     radian_freq = 2.0 * math.pi * base_freq * jnp.power(freq_ratio, bin_index)
     half = dir_count // 2
     cosines, sines = angles_of(dir_count)
+    group_speed, orbit_weight = physics(radian_freq, water_depth, dir_count)
+    partial_value = jnp.sum(orbit_weight * jnp.sum(energy, axis=2), axis=1)
+    geo_index = lax.axis_index("geo")
+    geo_count = lax.axis_size("geo")
+    first_half = SUBSTEPS // 2
+    assert tile_rows >= first_half and SUBSTEPS - first_half <= tile_rows
 
     fields = jnp.zeros((tile_rows, 1, half, tile_cols), jnp.float32)
     fields = fields.at[:, 0, 0, :].set(wet_field).at[:, 0, 1, :].set(water_depth)
     north_msg = jnp.concatenate([masked[:, :, :half], fields], axis=1)
     south_msg = jnp.concatenate([masked[:, :, half:], fields], axis=1)
-    below = halo(north_msg, "geo", 0, SUBSTEPS, -1)
-    above = halo(south_msg, "geo", 0, SUBSTEPS, +1)
-
-    group_speed, orbit_weight = physics(radian_freq, water_depth, dir_count)
-    partial_value = jnp.sum(orbit_weight * jnp.sum(energy, axis=2), axis=1)
-
-    freq_index = lax.axis_index("freq")
-    freq_total = lax.axis_size("freq")
-    slot = jnp.zeros((tile_rows, 1, dir_count, tile_cols), jnp.float32)
-    slot = slot.at[:, 0, 0, :].set(partial_value)
-    gathered = lax.all_gather(jnp.concatenate([masked, slot], axis=1), "freq", axis=1, tiled=True)
-    gathered = gathered.reshape(tile_rows, freq_total, freq_count + 1, dir_count, tile_cols)
-    partials = gathered[:, :, freq_count, 0, :]
-    spectrum_all = gathered[:, :, :freq_count].reshape(
-        tile_rows, freq_total * freq_count, dir_count, tile_cols
-    )
-    padded_all = jnp.pad(spectrum_all, ((0, 0), (2 * FH, 2 * FH), (0, 0), (0, 0)))
-    extended = lax.dynamic_slice_in_dim(padded_all, first_bin, freq_count + 4 * FH, axis=1)
-    glob = jnp.moveaxis(partials, 1, 0)
-    while glob.shape[0] > 1:
-        glob = glob[0::2] + glob[1::2]
-    orbital = jnp.sqrt(glob[0])
-    full_step = SUBSTEPS * sub_step
-    damping = 1.0 + full_step * canopy * veg_field * orbital
-
-    change = source_change(extended, quad_offsets, quad_weights, freq_count)
-    increment = (masked + full_step * change) / damping[:, None, None, :] - masked
-
-    geo_index = lax.axis_index("geo")
-    geo_count = lax.axis_size("geo")
-
-    def unpack(parts, offsets):
-        spectra, speeds, wets = [], [], []
-        for part, offset in zip(parts, offsets):
-            valid = (geo_index + offset >= 0) & (geo_index + offset < geo_count)
-            depth = jnp.where(valid, part[:, freq_count, 1, :], 1.0)
-            spectra.append(part[:, :freq_count])
-            wets.append(part[:, freq_count, 0, :])
-            speeds.append(physics(radian_freq, depth, dir_count)[0])
-        return spectra, speeds, wets
-
-    n_off = [-(len(below) - k) for k in range(len(below))]
-    b_spec, b_speed, b_wet = unpack(below, n_off)
+    below = from_neighbour(north_msg, "geo", 1)
+    above = from_neighbour(south_msg, "geo", -1)
+    spectrum_halo = tagged_exchange(masked, partial_value[None], "freq", FH)
+
+    def rim(part, offset):
+        valid = (geo_index + offset >= 0) & (geo_index + offset < geo_count)
+        depth = jnp.where(valid, part[:, freq_count, 1, :], 1.0)
+        return part[:, :freq_count], physics(radian_freq, depth, dir_count)[0], part[:, freq_count, 0, :]
+
+    b_spec, b_speed, b_wet = rim(below, -1)
+    a_spec, a_speed, a_wet = rim(above, 1)
+    north_speed = jnp.concatenate([b_speed, group_speed], axis=0)
+    north_wet = jnp.concatenate([b_wet, wet_field], axis=0)
+    south_speed = jnp.concatenate([group_speed, a_speed], axis=0)
+    south_wet = jnp.concatenate([wet_field, a_wet], axis=0)
     north = propagate(
-        jnp.concatenate(b_spec + [masked[:, :, :half]], axis=0),
-        jnp.concatenate(b_speed + [group_speed], axis=0),
-        jnp.concatenate(b_wet + [wet_field], axis=0),
+        jnp.concatenate([b_spec[tile_rows - first_half :], masked[:, :, :half]], axis=0),
+        north_speed[tile_rows - first_half :],
+        north_wet[tile_rows - first_half :],
         cosines[:half],
         sines[:half],
         True,
-    )
-    s_off = [k + 1 for k in range(len(above))]
-    a_spec, a_speed, a_wet = unpack(above, s_off)
+        first_half,
+    )
     south = propagate(
-        jnp.concatenate([masked[:, :, half:]] + a_spec, axis=0),
-        jnp.concatenate([group_speed] + a_speed, axis=0),
-        jnp.concatenate([wet_field] + a_wet, axis=0),
+        jnp.concatenate([masked[:, :, half:], a_spec[:first_half]], axis=0),
+        south_speed[: 2 * tile_rows - (tile_rows - first_half)],
+        south_wet[: 2 * tile_rows - (tile_rows - first_half)],
         cosines[half:],
         sines[half:],
         False,
-    )
+        first_half,
+    )
+    extended = jnp.concatenate([spectrum_halo[-1][0], masked, spectrum_halo[1][0]], axis=1)
+    transfer = interaction(extended, masked, quad_offsets, quad_weights)
+    known = {0: partial_value, -1: spectrum_halo[-1][1][0], 1: spectrum_halo[1][1][0]}
+
+    second = SUBSTEPS - first_half
+    north_mid = from_neighbour(north, "geo", 1)
+    south_mid = from_neighbour(south, "geo", -1)
+    transfer_halo = tagged_exchange(
+        transfer, jnp.stack([known[-1], known[0], known[1]]), "freq", FH
+    )
+    known[-2] = transfer_halo[-1][1][0]
+    known[2] = transfer_halo[1][1][2]
+    north = propagate(
+        jnp.concatenate([north_mid[tile_rows - second :], north], axis=0),
+        north_speed[tile_rows - second :],
+        north_wet[tile_rows - second :],
+        cosines[:half],
+        sines[:half],
+        True,
+        second,
+    )
+    south = propagate(
+        jnp.concatenate([south, south_mid[:second]], axis=0),
+        south_speed[: tile_rows + second],
+        south_wet[: tile_rows + second],
+        cosines[half:],
+        sines[half:],
+        False,
+        second,
+    )
+    spread = jnp.concatenate([transfer_halo[-1][0], transfer, transfer_halo[1][0]], axis=1)
+    change = redistribute(spread, transfer, quad_offsets, quad_weights)
+
+    orbital = jnp.sqrt(gathered_sum(known, freq_index, freq_total, partial_value))
+    full_step = SUBSTEPS * sub_step
+    damping = 1.0 + full_step * canopy * veg_field * orbital
+    increment = (masked + full_step * change) / damping[:, None, None, :] - masked
     moved = jnp.concatenate([north, south], axis=2)
     return (wet_four * (moved + increment), orbital)
 

time: 116 us -> 82.8 us (0.71)
  the two profiles are of different devices: /device:TPU:1 before, /device:TPU:267 now
where the time goes in v6:
time: 82.8 us; the launch traced here: 82.2 us
  other arithmetic  24.7 us (30%)
  starting transfers between devices  24.4 us (29%)
  between operations  15.3 us (18%)
  waiting for transfers between devices  9.85 us (12%)
  local copies, waits for them, and re-layouts  7.97 us (10%)
    ppermute x9, starting transfers between devices, from_neighbour(): return lax.ppermute(block, axis, pairs)  24.4 us
    ppermute x9, waiting for transfers between devices, from_neighbour(): return lax.ppermute(block, axis, pairs)  9.85 us
    mul x16, other arithmetic, propagate(): east_flux = east_speed[lo:hi] * spectrum  4.93 us
    concatenate x1, other arithmetic, interaction(): doubled = jnp.concatenate([extended, extended], axis=2)  3.95 us
    concatenate x1, other arithmetic, redistribute(): doubled = jnp.concatenate([extended, extended], axis=2)  3.95 us
    slice x16, local copies, waits for them, and re-layouts, east_west(): behind = jnp.concatenate([zeros, east_flux[..., :-1]], axis=-1)  3.06 us
    mul x1, other arithmetic, body(): return (wet_four * (moved + increment), orbital)  2.64 us
    mul x1, other arithmetic, interaction(): coupling * (masked * masked * (coef_plus * upper + coef_minus * lower) -...  1.86 us
  transfers between devices with their start and end apart: 9, of which 3 were waited for; matrix products, arithmetic and copies ran while one was open for 30% of the time, Pallas kernels for 0%

profile of v6, /device:TPU:267, one launch (start us, length us, event | category | flops | bytes accessed | tf_op | source)
XLA Modules:
  0.0 82.2 jit_solution(3952142796213894160)
XLA Ops:
  0.7 0.6 slice.687
  1.3 0.7 convert_bitcast_fusion
  1.9 1.1 %fusion.141 = (f32[4,6,128]{2,0,1:T(4,128)S(1)}, f32[4,6,36,128]{3,0,2,1:T(4,128)S(1)}) fusion(f32[4,6,36,128]{3,0,2,1:T(4,128)} %param.19, f32[4,128]{1,0:T(4,128)S(1)} %get-tuple-element.177), kind=kLoop, calls=%fused_computation.296 | loop fusion | flops 218112 | bytes 899072 | tf_op jit(solution)/shard_map/reduce_sum | solution.py:229
  3.1 1.3 %constant_dynamic-update-slice_fusion.19 = f32[4,1,18,128]{3,0,2,1:T(4,128)S(1)} fusion(f32[4,1,18,128]{3,0,2,1:T(4,128)S(1)} %scatter.20, s32[]{:T(128)} %bitcast.2, f32[4,128]{1,0:T(4,128)} %param.20), kind=kLoop, calls=%fused_computation.251 | loop fusion | bytes 4100 | tf_op jit(solution)/shard_map/scatter | solution.py:236
  4.6 3.2 %collective-permute-start = (f32[4,7,18,128]{3,0,2,1:T(4,128)S(1)}, f32[4,7,18,128]{3,0,2,1:T(4,128)S(1)}, u32[]{:S(2)}, u32[]{:S(2)}) collective-permute-start(f32[4,7,18,128]{3,0,2,1:T(4,128)S(1)} %get-tuple-element.160), channel_id=1, source_target_pairs={{0,1},{1,2},{2,3},{3,4},{4,5},{5,6},{6,7},{7,8},{8,9},{9,10},{10,1... | collective-permute-start | bytes 774152 | tf_op jit(solution)/shard_map/ppermute | solution.py:29
  7.8 2.1 %collective-permute-start.2 = (f32[4,7,18,128]{3,0,2,1:T(4,128)S(1)}, f32[4,7,18,128]{3,0,2,1:T(4,128)S(1)}, u32[]{:S(2)}, u32[]{:S(2)}) collective-permute-start(f32[4,7,18,128]{3,0,2,1:T(4,128)S(1)} %get-tuple-element.161), channel_id=1, source_target_pairs={{1,0},{2,1},{3,2},{4,3},{5,4},{6,5},{7,6},{8,7},{9,8},{10,9},{11,1... | collective-permute-start | bytes 774152 | tf_op jit(solution)/shard_map/ppermute | solution.py:29
  10.2 0.7 fusion.144
  10.9 0.6 fusion.145
  11.5 0.7 and_reduce_fusion
  12.3 0.6 slice.826
  27.1 0.2 add_multiply_fusion.1
  27.5 2.3 %collective-permute-start.4 = (f32[4,5,36,128]{3,0,2,1:T(4,128)S(1)}, f32[4,5,36,128]{3,0,2,1:T(4,128)S(1)}, u32[]{:S(2)}, u32[]{:S(2)}) collective-permute-start(f32[4,5,36,128]{3,0,2,1:T(4,128)S(1)} %get-tuple-element.178), channel_id=1, source_target_pairs={{0,64},{64,128},{128,192},{192,256},{256,320},{320,384},{384,448},... | collective-permute-start | bytes 1105928 | tf_op jit(solution)/shard_map/ppermute | solution.py:29
  30.0 0.2 fusion.129
  30.2 0.4 slice_multiply_fusion.23
  30.7 0.2 fusion.128
  30.9 0.4 slice_multiply_fusion.19
  31.4 0.2 fusion.127
  31.6 0.4 slice_multiply_fusion.15
  32.0 0.2 fusion.126
  32.2 0.3 fusion.86
  32.6 3.2 %collective-permute-start.1 = (f32[4,6,18,128]{3,0,2,1:T(4,128)S(1)}, f32[4,6,18,128]{3,0,2,1:T(4,128)S(1)}, u32[]{:S(2)}, u32[]{:S(2)}) collective-permute-start(f32[4,6,18,128]{3,0,2,1:T(4,128)S(1)} %fusion.86), channel_id=1, source_target_pairs={{0,1},{1,2},{2,3},{3,4},{4,5},{5,6},{6,7},{7,8},{8,9},{9,10},{10,1... | collective-permute-start | bytes 663560 | tf_op jit(solution)/shard_map/ppermute | solution.py:29
  36.0 0.2 fusion.138
  36.2 0.4 slice_multiply_fusion.11
  36.5 0.2 fusion.137
  36.8 0.3 slice_multiply_fusion.7
  37.3 0.3 slice_multiply_fusion.3
  37.9 5.2 %collective-permute-done.1 = f32[4,6,18,128]{3,0,2,1:T(4,128)S(1)} collective-permute-done((f32[4,6,18,128]{3,0,2,1:T(4,128)S(1)}, f32[4,6,18,128]{3,0,2,1:T(4,128)S(1)}, u32[]{:S(2)}, u32[]{:S(2)}) %collective-permute-start.1) | collective-permute-done | bytes 221216 | tf_op jit(solution)/shard_map/ppermute | solution.py:29
  43.3 0.2 fusion.125
  43.5 0.4 slice_multiply_fusion.22
  44.2 0.4 slice_multiply_fusion.18
  44.8 0.4 slice_multiply_fusion.14
  45.5 0.6 fusion.81
  46.1 6.5 %collective-permute-start.3 = (f32[4,6,18,128]{3,0,2,1:T(4,128)S(1)}, f32[4,6,18,128]{3,0,2,1:T(4,128)S(1)}, u32[]{:S(2)}, u32[]{:S(2)}) collective-permute-start(f32[4,6,18,128]{3,0,2,1:T(4,128)S(1)} %get-tuple-element.173), channel_id=1, source_target_pairs={{1,0},{2,1},{3,2},{4,3},{5,4},{6,5},{7,6},{8,7},{9,8},{10,9},{11,1... | collective-permute-start | bytes 663560 | tf_op jit(solution)/shard_map/ppermute | solution.py:29
  52.6 0.7 constant_dynamic-update-slice_fusion.18
  53.5 3.9 %maximum_maximum_fusion = f32[4,14,72,128]{3,0,2,1:T(4,128)S(1)} fusion(f32[4,4,36,128]{3,0,2,1:T(4,128)S(1)} %slice_select_fusion.2, f32[4,6,36,128]{3,0,2,1:T(4,128)S(1)} %get-tuple-element.149, f32[4,4,36,128]{3,0,2,1:T(4,128)S(1)} %slice_select_fusion.3), kind=kLoop, calls=%fused_computation | loop fusion | flops 2580480 | bytes 3096576 | tf_op jit(solution)/shard_map/concatenate | solution.py:123
  57.4 1.9 %broadcast_multiply_fusion = (f32[4,6,36,128]{3,0,2,1:T(4,128)S(1)}, f32[4,6,36,128]{3,0,2,1:T(4,128)S(1)}) fusion(f32[4,6,36,128]{3,0,2,1:T(4,128)S(1)} %get-tuple-element.149, f32[4,14,72,128]{3,0,2,1:T(4,128)S(1)} %maximum_maximum_fusion, s32[]{:T(128)S(6)} %select_n.209, s32[]{:T(128)S(6)} %select_n.208, f32[]{:T(128)S(6)} %sub.303, s32[]{:T(128)S(6)} %select_n.206, ...), kind=kLoop, calls=%fused_computation.194 | loop fusion | flops 1769472 | bytes 3096616 | tf_op jit(solution)/shard_map/mul | solution.py:137
  59.4 1.2 %constant_dynamic-update-slice_fusion.17 = f32[4,1,36,128]{3,0,2,1:T(4,128)S(1)} fusion(f32[4,1,36,128]{3,0,2,1:T(4,128)S(1)} %constant_dynamic-update-slice_fusion.18, s32[]{:T(128)} %bitcast.20, f32[4,5,36,128]{3,0,2,1:T(4,128)S(1)} %collective-permute-done.5, pred[]{:T(512)} %and_reduce_fusion), kind=kLoop, calls=%fused_computation.247 | loop fusion | flops 512 | bytes 6149 | tf_op jit(solution)/shard_map/scatter | solution.py:200
  60.7 2.6 %collective-permute-start.6 = (f32[4,5,36,128]{3,0,2,1:T(4,128)S(1)}, f32[4,5,36,128]{3,0,2,1:T(4,128)S(1)}, u32[]{:S(2)}, u32[]{:S(2)}) collective-permute-start(f32[4,5,36,128]{3,0,2,1:T(4,128)S(1)} %get-tuple-element.158), channel_id=1, source_target_pairs={{0,64},{64,128},{128,192},{192,256},{256,320},{320,384},{384,448},... | collective-permute-start | bytes 1105928 | tf_op jit(solution)/shard_map/ppermute | solution.py:29
  63.7 0.3 slice_multiply_fusion.10
  64.3 0.3 slice_multiply_fusion.6
  64.8 0.3 slice_multiply_fusion.2
  65.4 0.3 fusion.71
  65.7 2.1 %collective-permute-done.6 = f32[4,5,36,128]{3,0,2,1:T(4,128)S(1)} collective-permute-done((f32[4,5,36,128]{3,0,2,1:T(4,128)S(1)}, f32[4,5,36,128]{3,0,2,1:T(4,128)S(1)}, u32[]{:S(2)}, u32[]{:S(2)}) %collective-permute-start.6) | collective-permute-done | bytes 368672 | tf_op jit(solution)/shard_map/ppermute | solution.py:29
  67.8 2.5 %collective-permute-done.7 = f32[4,5,36,128]{3,0,2,1:T(4,128)S(1)} collective-permute-done((f32[4,5,36,128]{3,0,2,1:T(4,128)S(1)}, f32[4,5,36,128]{3,0,2,1:T(4,128)S(1)}, u32[]{:S(2)}, u32[]{:S(2)}) %collective-permute-start.7) | collective-permute-done | bytes 368672 | tf_op jit(solution)/shard_map/ppermute | solution.py:29
  70.3 4.4 %collective-permute-start.8 = (f32[5,4,128]{2,1,0:T(4,128)S(1)}, f32[5,4,128]{2,1,0:T(4,128)S(1)}, u32[]{:S(2)}, u32[]{:S(2)}) collective-permute-start(f32[5,4,128]{2,1,0:T(4,128)S(1)} %get-tuple-element.150), channel_id=1, source_target_pairs={{0,256},{64,320},{128,384},{192,448},{256,0},{320,64},{384,128},{4... | collective-permute-start | bytes 30728 | tf_op jit(solution)/shard_map/ppermute | solution.py:29
  74.8 3.9 %maximum_maximum_fusion.1 = f32[4,14,72,128]{3,0,2,1:T(4,128)S(1)} fusion(f32[4,4,36,128]{3,0,2,1:T(4,128)S(1)} %slice_select_fusion, f32[4,6,36,128]{3,0,2,1:T(4,128)S(1)} %get-tuple-element.100, f32[4,4,36,128]{3,0,2,1:T(4,128)S(1)} %slice_select_fusion.1), kind=kLoop, calls=%fused_computation.1 | loop fusion | flops 2580480 | bytes 3096576 | tf_op jit(solution)/shard_map/concatenate | solution.py:145
  79.0 0.6 multiply_add_fusion
  79.5 2.6 %fusion.65 = f32[4,6,36,128]{3,0,2,1:T(4,128)} fusion(f32[4,6,36,128]{3,0,2,1:T(4,128)S(1)} %get-tuple-element.149, f32[4,6,36,128]{3,0,2,1:T(4,128)S(1)} %get-tuple-element.101, f32[4,14,72,128]{3,0,2,1:T(4,128)S(1)} %maximum_maximum_fusion.1, s32[]{:T(128)S(6)} %select_n.219, s32[]{:T(128)S(6)} %select_n.218, s32[]{:T(128)S(6)} %select_n.216, ...), kind=kLoop, calls=%fused_computation.119 | loop fusion | flops 1769472 | bytes 3543080 | tf_op jit(solution)/shard_map/mul | solution.py:310
  (92 shorter events, 4.5 us)
Async XLA Ops:
  0.6 10.9 %copy-start.5 = (s32[4]{0:T(128)S(1)}, s32[4]{0:T(128)}, u32[]{:S(2)}) copy-start(s32[4]{0:T(128)} %constant.296.clone.1) | copy-start | bytes 52
  0.6 9.6 %copy-start.2 = (f32[2]{0:T(128)S(1)}, f32[2]{0:T(128)}, u32[]{:S(2)}) copy-start(f32[2]{0:T(128)} %param.25) | copy-start | bytes 28
  0.7 10.2 %copy-start = (s32[4]{0:T(128)S(1)}, s32[4]{0:T(128)}, u32[]{:S(2)}) copy-start(s32[4]{0:T(128)} %param.24) | copy-start | bytes 52
  1.9 25.1 %copy-start.1 = (f32[4,128]{1,0:T(4,128)S(1)}, f32[4,128]{1,0:T(4,128)}, u32[]{:S(2)}) copy-start(f32[4,128]{1,0:T(4,128)} %param.20) | copy-start | bytes 6148
  4.6 22.4 %collective-permute-start = (f32[4,7,18,128]{3,0,2,1:T(4,128)S(1)}, f32[4,7,18,128]{3,0,2,1:T(4,128)S(1)}, u32[]{:S(2)}, u32[]{:S(2)}) collective-permute-start(f32[4,7,18,128]{3,0,2,1:T(4,128)S(1)} %get-tuple-element.160), channel_id=1, source_target_pairs={{0,1},{1,2},{2,3},{3,4},{4,5},{5,6},{6,7},{7,8},{8,9},{9,10},{10,1... | collective-permute-start | bytes 774152 | tf_op jit(solution)/shard_map/ppermute | solution.py:29
  7.8 19.2 %collective-permute-start.2 = (f32[4,7,18,128]{3,0,2,1:T(4,128)S(1)}, f32[4,7,18,128]{3,0,2,1:T(4,128)S(1)}, u32[]{:S(2)}, u32[]{:S(2)}) collective-permute-start(f32[4,7,18,128]{3,0,2,1:T(4,128)S(1)} %get-tuple-element.161), channel_id=1, source_target_pairs={{1,0},{2,1},{3,2},{4,3},{5,4},{6,5},{7,6},{8,7},{9,8},{10,9},{11,1... | collective-permute-start | bytes 774152 | tf_op jit(solution)/shard_map/ppermute | solution.py:29
  27.5 25.1 %collective-permute-start.4 = (f32[4,5,36,128]{3,0,2,1:T(4,128)S(1)}, f32[4,5,36,128]{3,0,2,1:T(4,128)S(1)}, u32[]{:S(2)}, u32[]{:S(2)}) collective-permute-start(f32[4,5,36,128]{3,0,2,1:T(4,128)S(1)} %get-tuple-element.178), channel_id=1, source_target_pairs={{0,64},{64,128},{128,192},{192,256},{256,320},{320,384},{384,448},... | collective-permute-start | bytes 1105928 | tf_op jit(solution)/shard_map/ppermute | solution.py:29
  29.8 23.6 %collective-permute-start.5 = (f32[4,5,36,128]{3,0,2,1:T(4,128)S(1)}, f32[4,5,36,128]{3,0,2,1:T(4,128)S(1)}, u32[]{:S(2)}, u32[]{:S(2)}) collective-permute-start(f32[4,5,36,128]{3,0,2,1:T(4,128)S(1)} %get-tuple-element.179), channel_id=1, source_target_pairs={{0,448},{64,0},{128,64},{192,128},{256,192},{320,256},{384,320},{4... | collective-permute-start | bytes 1105928 | tf_op jit(solution)/shard_map/ppermute | solution.py:29
  32.6 10.6 %collective-permute-start.1 = (f32[4,6,18,128]{3,0,2,1:T(4,128)S(1)}, f32[4,6,18,128]{3,0,2,1:T(4,128)S(1)}, u32[]{:S(2)}, u32[]{:S(2)}) collective-permute-start(f32[4,6,18,128]{3,0,2,1:T(4,128)S(1)} %fusion.86), channel_id=1, source_target_pairs={{0,1},{1,2},{2,3},{3,4},{4,5},{5,6},{6,7},{7,8},{8,9},{9,10},{10,1... | collective-permute-start | bytes 663560 | tf_op jit(solution)/shard_map/ppermute | solution.py:29
  46.1 17.3 %collective-permute-start.3 = (f32[4,6,18,128]{3,0,2,1:T(4,128)S(1)}, f32[4,6,18,128]{3,0,2,1:T(4,128)S(1)}, u32[]{:S(2)}, u32[]{:S(2)}) collective-permute-start(f32[4,6,18,128]{3,0,2,1:T(4,128)S(1)} %get-tuple-element.173), channel_id=1, source_target_pairs={{1,0},{2,1},{3,2},{4,3},{5,4},{6,5},{7,6},{8,7},{9,8},{10,9},{11,1... | collective-permute-start | bytes 663560 | tf_op jit(solution)/shard_map/ppermute | solution.py:29
  60.7 7.1 %collective-permute-start.6 = (f32[4,5,36,128]{3,0,2,1:T(4,128)S(1)}, f32[4,5,36,128]{3,0,2,1:T(4,128)S(1)}, u32[]{:S(2)}, u32[]{:S(2)}) collective-permute-start(f32[4,5,36,128]{3,0,2,1:T(4,128)S(1)} %get-tuple-element.158), channel_id=1, source_target_pairs={{0,64},{64,128},{128,192},{192,256},{256,320},{320,384},{384,448},... | collective-permute-start | bytes 1105928 | tf_op jit(solution)/shard_map/ppermute | solution.py:29
  63.3 6.9 %collective-permute-start.7 = (f32[4,5,36,128]{3,0,2,1:T(4,128)S(1)}, f32[4,5,36,128]{3,0,2,1:T(4,128)S(1)}, u32[]{:S(2)}, u32[]{:S(2)}) collective-permute-start(f32[4,5,36,128]{3,0,2,1:T(4,128)S(1)} %get-tuple-element.159), channel_id=1, source_target_pairs={{0,448},{64,0},{128,64},{192,128},{256,192},{320,256},{384,320},{4... | collective-permute-start | bytes 1105928 | tf_op jit(solution)/shard_map/ppermute | solution.py:29
  70.3 8.7 %copy-start.3 = (s32[4,128]{1,0:T(4,128)S(1)}, s32[4,128]{1,0:T(4,128)}, u32[]{:S(2)}) copy-start(s32[4,128]{1,0:T(4,128)} %param.22) | copy-start | bytes 6148
  70.3 8.7 %copy-start.4 = (f32[4,128]{1,0:T(4,128)S(1)}, f32[4,128]{1,0:T(4,128)}, u32[]{:S(2)}) copy-start(f32[4,128]{1,0:T(4,128)} %param.23) | copy-start | bytes 6148
  70.3 8.5 %collective-permute-start.8 = (f32[5,4,128]{2,1,0:T(4,128)S(1)}, f32[5,4,128]{2,1,0:T(4,128)S(1)}, u32[]{:S(2)}, u32[]{:S(2)}) collective-permute-start(f32[5,4,128]{2,1,0:T(4,128)S(1)} %get-tuple-element.150), channel_id=1, source_target_pairs={{0,256},{64,320},{128,384},{192,448},{256,0},{320,64},{384,128},{4... | collective-permute-start | bytes 30728 | tf_op jit(solution)/shard_map/ppermute | solution.py:29

commit v7 on v3

--- a/solution.py
+++ b/solution.py
@@ -198,8 +198,6 @@
     fields = fields.at[:, 0, 0, :].set(wet_field).at[:, 0, 1, :].set(water_depth)
     north_msg = jnp.concatenate([masked[:, :, :half], fields], axis=1)
     south_msg = jnp.concatenate([masked[:, :, half:], fields], axis=1)
-    below = halo(north_msg, "geo", 0, SUBSTEPS, -1)
-    above = halo(south_msg, "geo", 0, SUBSTEPS, +1)
 
     group_speed, orbit_weight = physics(radian_freq, water_depth, dir_count)
     partial_value = jnp.sum(orbit_weight * jnp.sum(energy, axis=2), axis=1)
@@ -231,6 +229,12 @@
 
     low = tagged_halo(-1)
     high = tagged_halo(+1)
+    arrays = [(p[1], p[2]) for p in low + high]
+    north_msg, south_msg, arrays = lax.optimization_barrier((north_msg, south_msg, arrays))
+    tagged = [(p[0],) + tuple(a) for p, a in zip(low + high, arrays)]
+    low, high = tagged[: len(low)], tagged[len(low) :]
+    below = halo(north_msg, "geo", 0, SUBSTEPS, -1)
+    above = halo(south_msg, "geo", 0, SUBSTEPS, +1)
     low_bins = [p[1] for p in reversed(low)]
     high_bins = [p[1] for p in high]
     known = {0: partial_value}

time: 79 us -> 80.9 us (1.024)
  the two profiles are of different devices: /device:TPU:2 before, /device:TPU:255 now
where the time goes in v7:
time: 80.9 us; the launch traced here: 80.3 us
  starting transfers between devices  24 us (30%)
  other arithmetic  20.8 us (26%)
  between operations  15.5 us (19%)
  waiting for transfers between devices  12.9 us (16%)
  local copies, waits for them, and re-layouts  7.12 us (9%)
    ppermute x9, starting transfers between devices, from_neighbour(): return lax.ppermute(block, axis, pairs)  24 us
    ppermute x9, waiting for transfers between devices, from_neighbour(): return lax.ppermute(block, axis, pairs)  12.9 us
    mul x16, other arithmetic, propagate(): east_flux = east_speed[lo:hi] * spectrum  7.57 us
    mul x1, other arithmetic, source_change(): coupling * (centre * centre * (coef_plus * upper + coef_minus * lower) -...  4.04 us
    slice x16, local copies, waits for them, and re-layouts, east_west(): behind = jnp.concatenate([zeros, east_flux[..., :-1]], axis=-1)  3.96 us
    mul x1, other arithmetic, body(): return (wet_four * (moved + increment), orbital)  3.11 us
  transfers between devices with their start and end apart: 9, of which 2 were waited for; matrix products, arithmetic and copies ran while one was open for 10% of the time, Pallas kernels for 0%

profile of v7, /device:TPU:255, one launch (start us, length us, event | category | flops | bytes accessed | tf_op | source)
XLA Modules:
  0.0 80.3 jit_solution(17173101031207536868)
XLA Ops:
  0.7 0.7 convert_bitcast_fusion
  1.4 1.1 %fusion.168 = (f32[4,6,128]{2,0,1:T(4,128)S(1)}, f32[4,6,36,128]{3,0,2,1:T(4,128)S(1)}) fusion(f32[4,6,36,128]{3,0,2,1:T(4,128)} %param.13, f32[4,128]{1,0:T(4,128)S(1)} %get-tuple-element.165), kind=kLoop, calls=%fused_computation.336 | loop fusion | flops 218112 | bytes 899072 | tf_op jit(solution)/shard_map/reduce_sum | solution.py:203
  2.5 0.8 %add_multiply_fusion.2 = (f32[4,6,128]{2,0,1:T(4,128)S(1)}, f32[4,128]{1,0:T(4,128)S(1)}) fusion(f32[6]{0:T(128)S(1)} %get-tuple-element.183, f32[4,128]{1,0:T(4,128)} %param.14, f32[6]{0:T(128)S(1)} %fusion.135, f32[4,6,128]{2,0,1:T(4,128)S(1)} %get-tuple-element.128, f32[6]{0:T(128)S(1)} %get-tuple-element.182), kind=kLoop, calls=%fused_computation.269 | loop fusion | flops 107008 | bytes 28744 | tf_op jit(solution)/shard_map/mul | solution.py:89
  3.5 0.7 collective-permute-start.2
  4.2 2.3 %collective-permute-start = (f32[4,7,36,128]{3,0,2,1:T(4,128)S(1)}, f32[4,7,36,128]{3,0,2,1:T(4,128)S(1)}, u32[]{:S(2)}, u32[]{:S(2)}) collective-permute-start(f32[4,7,36,128]{3,0,2,1:T(4,128)S(1)} %pad_maximum_fusion.4), channel_id=1, source_target_pairs={{0,64},{64,128},{128,192},{192,256},{256,320},{320,384},{384,448},... | collective-permute-start | bytes 1548296 | tf_op jit(solution)/shard_map/ppermute | solution.py:29
  6.6 1.9 %collective-permute-start.3 = (f32[4,3,36,128]{3,0,2,1:T(4,128)S(1)}, f32[4,3,36,128]{3,0,2,1:T(4,128)S(1)}, u32[]{:S(2)}, u32[]{:S(2)}) collective-permute-start(f32[4,3,36,128]{3,0,2,1:T(4,128)S(1)} %get-tuple-element.140), channel_id=1, source_target_pairs={{0,384},{64,448},{128,0},{192,64},{256,128},{320,192},{384,256},{4... | collective-permute-start | bytes 663560 | tf_op jit(solution)/shard_map/ppermute | solution.py:29
  8.5 4.6 %collective-permute-start.1 = (f32[4,3,36,128]{3,0,2,1:T(4,128)S(1)}, f32[4,3,36,128]{3,0,2,1:T(4,128)S(1)}, u32[]{:S(2)}, u32[]{:S(2)}) collective-permute-start(f32[4,3,36,128]{3,0,2,1:T(4,128)S(1)} %get-tuple-element.141), channel_id=1, source_target_pairs={{0,128},{64,192},{128,256},{192,320},{256,384},{320,448},{384,0},{... | collective-permute-start | bytes 663560 | tf_op jit(solution)/shard_map/ppermute | solution.py:29
  13.2 0.6 fusion.171
  24.0 0.6 slice.672
  24.6 0.7 fusion.170
  29.3 0.7 constant_dynamic-update-slice_fusion.22
  30.5 5.4 %collective-permute-start.5 = (f32[4,7,18,128]{3,0,2,1:T(4,128)S(1)}, f32[4,7,18,128]{3,0,2,1:T(4,128)S(1)}, u32[]{:S(2)}, u32[]{:S(2)}) collective-permute-start(f32[4,7,18,128]{3,0,2,1:T(4,128)S(1)} %get-tuple-element.48), channel_id=1, source_target_pairs={{0,2},{1,3},{2,4},{3,5},{4,6},{5,7},{6,8},{7,9},{8,10},{9,11},{10,... | collective-permute-start | bytes 774152 | tf_op jit(solution)/shard_map/ppermute | solution.py:29
  36.0 3.2 %collective-permute-start.4 = (f32[4,7,18,128]{3,0,2,1:T(4,128)S(1)}, f32[4,7,18,128]{3,0,2,1:T(4,128)S(1)}, u32[]{:S(2)}, u32[]{:S(2)}) collective-permute-start(f32[4,7,18,128]{3,0,2,1:T(4,128)S(1)} %get-tuple-element.48), channel_id=1, source_target_pairs={{0,1},{1,2},{2,3},{3,4},{4,5},{5,6},{6,7},{7,8},{8,9},{9,10},{10,1... | collective-permute-start | bytes 774152 | tf_op jit(solution)/shard_map/ppermute | solution.py:29
  39.2 2.0 %collective-permute-start.7 = (f32[4,7,18,128]{3,0,2,1:T(4,128)S(1)}, f32[4,7,18,128]{3,0,2,1:T(4,128)S(1)}, u32[]{:S(2)}, u32[]{:S(2)}) collective-permute-start(f32[4,7,18,128]{3,0,2,1:T(4,128)S(1)} %get-tuple-element.49), channel_id=1, source_target_pairs={{2,0},{3,1},{4,2},{5,3},{6,4},{7,5},{8,6},{9,7},{10,8},{11,9},{12,... | collective-permute-start | bytes 774152 | tf_op jit(solution)/shard_map/ppermute | solution.py:29
  41.2 2.0 %collective-permute-start.6 = (f32[4,7,18,128]{3,0,2,1:T(4,128)S(1)}, f32[4,7,18,128]{3,0,2,1:T(4,128)S(1)}, u32[]{:S(2)}, u32[]{:S(2)}) collective-permute-start(f32[4,7,18,128]{3,0,2,1:T(4,128)S(1)} %get-tuple-element.49), channel_id=1, source_target_pairs={{1,0},{2,1},{3,2},{4,3},{5,4},{6,5},{7,6},{8,7},{9,8},{10,9},{11,1... | collective-permute-start | bytes 774152 | tf_op jit(solution)/shard_map/ppermute | solution.py:29
  43.3 1.9 %collective-permute-start.8 = (f32[5,4,128]{2,1,0:T(4,128)S(1)}, f32[5,4,128]{2,1,0:T(4,128)S(1)}, u32[]{:S(2)}, u32[]{:S(2)}) collective-permute-start(f32[5,4,128]{2,1,0:T(4,128)S(1)} %get-tuple-element.152), channel_id=1, source_target_pairs={{0,256},{64,320},{128,384},{192,448},{256,0},{320,64},{384,128},{4... | collective-permute-start | bytes 30728 | tf_op jit(solution)/shard_map/ppermute | solution.py:29
  45.5 4.0 %subtract_multiply_fusion = f32[4,14,36,128]{3,0,2,1:T(4,128)S(1)} fusion(s32[]{:T(128)S(6)} %select_n.255, s32[]{:T(128)S(6)} %select_n.254, f32[4,22,36,128]{3,0,2,1:T(4,128)S(1)} %constant_dynamic-update-slice_fusion, s32[]{:T(128)S(6)} %select_n.252, s32[]{:T(128)S(6)} %select_n.251, s32[]{:T(128)S(6)} %select_n.250, s32[]{:T(128)S(6)} %select_n.248, ...), kind=kLoop, calls=%fused_computation.28 | loop fusion | flops 5677056 | bytes 3981352 | tf_op jit(solution)/shard_map/mul | solution.py:138
  49.7 0.6 multiply_add_fusion
  50.3 2.0 %collective-permute-done.4 = f32[4,7,18,128]{3,0,2,1:T(4,128)S(1)} collective-permute-done((f32[4,7,18,128]{3,0,2,1:T(4,128)S(1)}, f32[4,7,18,128]{3,0,2,1:T(4,128)S(1)}, u32[]{:S(2)}, u32[]{:S(2)}) %collective-permute-start.4) | collective-permute-done | bytes 258080 | tf_op jit(solution)/shard_map/ppermute | solution.py:29
  52.3 10.9 %collective-permute-done.6 = f32[4,7,18,128]{3,0,2,1:T(4,128)S(1)} collective-permute-done((f32[4,7,18,128]{3,0,2,1:T(4,128)S(1)}, f32[4,7,18,128]{3,0,2,1:T(4,128)S(1)}, u32[]{:S(2)}, u32[]{:S(2)}) %collective-permute-start.6) | collective-permute-done | bytes 258080 | tf_op jit(solution)/shard_map/ppermute | solution.py:29
  63.4 0.2 add_multiply_fusion.4
  63.7 0.4 fusion.94
  64.1 0.3 fusion.154
  64.4 0.7 slice_multiply_fusion.11
  65.1 0.3 fusion.153
  65.6 0.7 slice_multiply_fusion.9
  66.4 0.3 fusion.152
  66.7 0.7 slice_multiply_fusion.7
  67.6 0.3 fusion.151
  67.9 0.5 slice_multiply_fusion.28
  68.5 0.2 fusion.162
  68.7 0.4 slice_multiply_fusion.26
  69.3 0.4 slice_multiply_fusion.24
  70.0 0.4 slice_multiply_fusion.22
  70.8 0.4 fusion.96
  71.2 0.3 fusion.158
  71.5 0.6 slice_multiply_fusion.5
  72.1 0.3 fusion.157
  72.5 0.6 slice_multiply_fusion.3
  73.2 0.3 fusion.156
  73.5 0.6 slice_multiply_fusion.1
  74.2 0.3 fusion.155
  74.5 0.3 slice_multiply_fusion.20
  75.1 0.3 slice_multiply_fusion.18
  75.6 0.3 slice_multiply_fusion.16
  76.2 0.3 slice_multiply_fusion.14
  76.7 0.5 fusion.106
  77.2 3.1 %fusion.93 = f32[4,6,36,128]{3,0,2,1:T(4,128)} fusion(f32[4,6,36,128]{3,0,2,1:T(4,128)S(1)} %get-tuple-element.129, f32[4,6,18,128]{3,0,2,1:T(4,128)S(1)} %get-tuple-element.159, f32[4,6,18,128]{3,0,2,1:T(4,128)S(1)} %get-tuple-element.158, f32[4,14,36,128]{3,0,2,1:T(4,128)S(1)} %subtract_multiply_fusion, s32[]{:T(128)S(6)} %select_n.263, ...), kind=kLoop, calls=%fused_computation.193 | loop fusion | flops 2211840 | bytes 2805800 | tf_op jit(solution)/shard_map/mul | solution.py:285
  (99 shorter events, 4.1 us)
Async XLA Ops:
  1.4 11.9 %copy-start = (s32[4]{0:T(128)S(1)}, s32[4]{0:T(128)}, u32[]{:S(2)}) copy-start(s32[4]{0:T(128)} %param.18) | copy-start | bytes 52
  3.3 21.3 %copy-start.2 = (f32[2]{0:T(128)S(1)}, f32[2]{0:T(128)}, u32[]{:S(2)}) copy-start(f32[2]{0:T(128)} %param.19) | copy-start | bytes 28
  3.4 25.9 %copy-start.1 = (f32[4,128]{1,0:T(4,128)S(1)}, f32[4,128]{1,0:T(4,128)}, u32[]{:S(2)}) copy-start(f32[4,128]{1,0:T(4,128)} %param.14) | copy-start | bytes 6148
  3.5 26.8 %collective-permute-start.2 = (f32[4,7,36,128]{3,0,2,1:T(4,128)S(1)}, f32[4,7,36,128]{3,0,2,1:T(4,128)S(1)}, u32[]{:S(2)}, u32[]{:S(2)}) collective-permute-start(f32[4,7,36,128]{3,0,2,1:T(4,128)S(1)} %pad_maximum_fusion.4), channel_id=1, source_target_pairs={{0,448},{64,0},{128,64},{192,128},{256,192},{320,256},{384,320},{4... | collective-permute-start | bytes 1548296 | tf_op jit(solution)/shard_map/ppermute | solution.py:29
  4.2 26.2 %collective-permute-start = (f32[4,7,36,128]{3,0,2,1:T(4,128)S(1)}, f32[4,7,36,128]{3,0,2,1:T(4,128)S(1)}, u32[]{:S(2)}, u32[]{:S(2)}) collective-permute-start(f32[4,7,36,128]{3,0,2,1:T(4,128)S(1)} %pad_maximum_fusion.4), channel_id=1, source_target_pairs={{0,64},{64,128},{128,192},{192,256},{256,320},{320,384},{384,448},... | collective-permute-start | bytes 1548296 | tf_op jit(solution)/shard_map/ppermute | solution.py:29
  6.6 23.6 %collective-permute-start.3 = (f32[4,3,36,128]{3,0,2,1:T(4,128)S(1)}, f32[4,3,36,128]{3,0,2,1:T(4,128)S(1)}, u32[]{:S(2)}, u32[]{:S(2)}) collective-permute-start(f32[4,3,36,128]{3,0,2,1:T(4,128)S(1)} %get-tuple-element.140), channel_id=1, source_target_pairs={{0,384},{64,448},{128,0},{192,64},{256,128},{320,192},{384,256},{4... | collective-permute-start | bytes 663560 | tf_op jit(solution)/shard_map/ppermute | solution.py:29
  8.5 21.7 %collective-permute-start.1 = (f32[4,3,36,128]{3,0,2,1:T(4,128)S(1)}, f32[4,3,36,128]{3,0,2,1:T(4,128)S(1)}, u32[]{:S(2)}, u32[]{:S(2)}) collective-permute-start(f32[4,3,36,128]{3,0,2,1:T(4,128)S(1)} %get-tuple-element.141), channel_id=1, source_target_pairs={{0,128},{64,192},{128,256},{192,320},{256,384},{320,448},{384,0},{... | collective-permute-start | bytes 663560 | tf_op jit(solution)/shard_map/ppermute | solution.py:29
  30.5 32.7 %collective-permute-start.5 = (f32[4,7,18,128]{3,0,2,1:T(4,128)S(1)}, f32[4,7,18,128]{3,0,2,1:T(4,128)S(1)}, u32[]{:S(2)}, u32[]{:S(2)}) collective-permute-start(f32[4,7,18,128]{3,0,2,1:T(4,128)S(1)} %get-tuple-element.48), channel_id=1, source_target_pairs={{0,2},{1,3},{2,4},{3,5},{4,6},{5,7},{6,8},{7,9},{8,10},{9,11},{10,... | collective-permute-start | bytes 774152 | tf_op jit(solution)/shard_map/ppermute | solution.py:29
  36.0 16.3 %collective-permute-start.4 = (f32[4,7,18,128]{3,0,2,1:T(4,128)S(1)}, f32[4,7,18,128]{3,0,2,1:T(4,128)S(1)}, u32[]{:S(2)}, u32[]{:S(2)}) collective-permute-start(f32[4,7,18,128]{3,0,2,1:T(4,128)S(1)} %get-tuple-element.48), channel_id=1, source_target_pairs={{0,1},{1,2},{2,3},{3,4},{4,5},{5,6},{6,7},{7,8},{8,9},{9,10},{10,1... | collective-permute-start | bytes 774152 | tf_op jit(solution)/shard_map/ppermute | solution.py:29
  39.2 24.1 %collective-permute-start.7 = (f32[4,7,18,128]{3,0,2,1:T(4,128)S(1)}, f32[4,7,18,128]{3,0,2,1:T(4,128)S(1)}, u32[]{:S(2)}, u32[]{:S(2)}) collective-permute-start(f32[4,7,18,128]{3,0,2,1:T(4,128)S(1)} %get-tuple-element.49), channel_id=1, source_target_pairs={{2,0},{3,1},{4,2},{5,3},{6,4},{7,5},{8,6},{9,7},{10,8},{11,9},{12,... | collective-permute-start | bytes 774152 | tf_op jit(solution)/shard_map/ppermute | solution.py:29
  41.2 22.0 %collective-permute-start.6 = (f32[4,7,18,128]{3,0,2,1:T(4,128)S(1)}, f32[4,7,18,128]{3,0,2,1:T(4,128)S(1)}, u32[]{:S(2)}, u32[]{:S(2)}) collective-permute-start(f32[4,7,18,128]{3,0,2,1:T(4,128)S(1)} %get-tuple-element.49), channel_id=1, source_target_pairs={{1,0},{2,1},{3,2},{4,3},{5,4},{6,5},{7,6},{8,7},{9,8},{10,9},{11,1... | collective-permute-start | bytes 774152 | tf_op jit(solution)/shard_map/ppermute | solution.py:29
  43.3 6.2 %collective-permute-start.8 = (f32[5,4,128]{2,1,0:T(4,128)S(1)}, f32[5,4,128]{2,1,0:T(4,128)S(1)}, u32[]{:S(2)}, u32[]{:S(2)}) collective-permute-start(f32[5,4,128]{2,1,0:T(4,128)S(1)} %get-tuple-element.152), channel_id=1, source_target_pairs={{0,256},{64,320},{128,384},{192,448},{256,0},{320,64},{384,128},{4... | collective-permute-start | bytes 30728 | tf_op jit(solution)/shard_map/ppermute | solution.py:29
  45.4 4.2 %copy-start.3 = (s32[4,128]{1,0:T(4,128)S(1)}, s32[4,128]{1,0:T(4,128)}, u32[]{:S(2)}) copy-start(s32[4,128]{1,0:T(4,128)} %param.16) | copy-start | bytes 6148
  45.5 4.2 %copy-start.4 = (f32[4,128]{1,0:T(4,128)S(1)}, f32[4,128]{1,0:T(4,128)}, u32[]{:S(2)}) copy-start(f32[4,128]{1,0:T(4,128)} %param.17) | copy-start | bytes 6148

commit v8 on v6

--- a/solution.py
+++ b/solution.py
@@ -239,6 +239,7 @@
     below = from_neighbour(north_msg, "geo", 1)
     above = from_neighbour(south_msg, "geo", -1)
     spectrum_halo = tagged_exchange(masked, partial_value[None], "freq", FH)
+    below, above, spectrum_halo = lax.optimization_barrier((below, above, spectrum_halo))
 
     def rim(part, offset):
         valid = (geo_index + offset >= 0) & (geo_index + offset < geo_count)
@@ -279,6 +280,9 @@
     transfer_halo = tagged_exchange(
         transfer, jnp.stack([known[-1], known[0], known[1]]), "freq", FH
     )
+    north_mid, south_mid, transfer_halo = lax.optimization_barrier(
+        (north_mid, south_mid, transfer_halo)
+    )
     known[-2] = transfer_halo[-1][1][0]
     known[2] = transfer_halo[1][1][2]
     north = propagate(

time: 82.8 us -> 81.4 us (0.983)
  the two profiles are of different devices: /device:TPU:267 before, /device:TPU:251 now
where the time goes in v8:
time: 81.4 us; the launch traced here: 80.9 us
  other arithmetic  24.5 us (30%)
  starting transfers between devices  23.4 us (29%)
  between operations  15.4 us (19%)
  waiting for transfers between devices  9.94 us (12%)
  local copies, waits for them, and re-layouts  7.55 us (9%)
    ppermute x9, starting transfers between devices, from_neighbour(): return lax.ppermute(block, axis, pairs)  23.4 us
    ppermute x9, waiting for transfers between devices, from_neighbour(): return lax.ppermute(block, axis, pairs)  9.94 us
    mul x15, other arithmetic, propagate(): east_flux = east_speed[lo:hi] * spectrum  4.99 us
    concatenate x1, other arithmetic, interaction(): doubled = jnp.concatenate([extended, extended], axis=2)  3.95 us
    concatenate x1, other arithmetic, redistribute(): doubled = jnp.concatenate([extended, extended], axis=2)  3.95 us
    slice x16, local copies, waits for them, and re-layouts, east_west(): behind = jnp.concatenate([zeros, east_flux[..., :-1]], axis=-1)  3.05 us
    mul x1, other arithmetic, body(): return (wet_four * (moved + increment), orbital)  2.48 us
    mul x1, other arithmetic, interaction(): coupling * (masked * masked * (coef_plus * upper + coef_minus * lower) -...  1.67 us
  transfers between devices with their start and end apart: 9, of which 2 were waited for; matrix products, arithmetic and copies ran while one was open for 23% of the time, Pallas kernels for 0%

profile of v8, /device:TPU:251, one launch (start us, length us, event | category | flops | bytes accessed | tf_op | source)
XLA Modules:
  0.0 80.9 jit_solution(12494024403393462645)
XLA Ops:
  0.7 0.7 convert_bitcast_fusion
  1.4 1.1 %fusion.138 = (f32[4,6,128]{2,0,1:T(4,128)S(1)}, f32[4,6,36,128]{3,0,2,1:T(4,128)S(1)}) fusion(f32[4,6,36,128]{3,0,2,1:T(4,128)} %param.19, f32[4,128]{1,0:T(4,128)S(1)} %get-tuple-element.205), kind=kLoop, calls=%fused_computation.295 | loop fusion | flops 218112 | bytes 899072 | tf_op jit(solution)/shard_map/reduce_sum | solution.py:229
  2.9 0.7 collective-permute-start.3
  3.6 1.1 %collective-permute-start.2 = (f32[4,5,36,128]{3,0,2,1:T(4,128)S(1)}, f32[4,5,36,128]{3,0,2,1:T(4,128)S(1)}, u32[]{:S(2)}, u32[]{:S(2)}) collective-permute-start(f32[4,5,36,128]{3,0,2,1:T(4,128)S(1)} %get-tuple-element.203), channel_id=1, source_target_pairs={{0,64},{64,128},{128,192},{192,256},{256,320},{320,384},{384,448},... | collective-permute-start | bytes 1105928 | tf_op jit(solution)/shard_map/ppermute | solution.py:29
  4.8 0.7 slice.691
  5.4 0.7 constant_dynamic-update-slice_fusion.19
  6.3 4.4 %collective-permute-start = (f32[4,7,18,128]{3,0,2,1:T(4,128)S(1)}, f32[4,7,18,128]{3,0,2,1:T(4,128)S(1)}, u32[]{:S(2)}, u32[]{:S(2)}) collective-permute-start(f32[4,7,18,128]{3,0,2,1:T(4,128)S(1)} %get-tuple-element.181), channel_id=1, source_target_pairs={{0,1},{1,2},{2,3},{3,4},{4,5},{5,6},{6,7},{7,8},{8,9},{9,10},{10,1... | collective-permute-start | bytes 774152 | tf_op jit(solution)/shard_map/ppermute | solution.py:29
  10.7 1.9 %collective-permute-start.1 = (f32[4,7,18,128]{3,0,2,1:T(4,128)S(1)}, f32[4,7,18,128]{3,0,2,1:T(4,128)S(1)}, u32[]{:S(2)}, u32[]{:S(2)}) collective-permute-start(f32[4,7,18,128]{3,0,2,1:T(4,128)S(1)} %get-tuple-element.180), channel_id=1, source_target_pairs={{1,0},{2,1},{3,2},{4,3},{5,4},{6,5},{7,6},{8,7},{9,8},{10,9},{11,1... | collective-permute-start | bytes 774152 | tf_op jit(solution)/shard_map/ppermute | solution.py:29
  12.8 0.7 fusion.143
  13.5 0.6 fusion.142
  27.0 0.6 slice.782
  29.0 0.7 and_reduce_fusion
  30.1 0.7 constant_dynamic-update-slice_fusion.18
  30.8 3.9 %maximum_maximum_fusion = f32[4,14,72,128]{3,0,2,1:T(4,128)S(1)} fusion(f32[4,4,36,128]{3,0,2,1:T(4,128)S(1)} %slice_select_fusion.2, f32[4,6,36,128]{3,0,2,1:T(4,128)S(1)} %get-tuple-element.171, f32[4,4,36,128]{3,0,2,1:T(4,128)S(1)} %slice_select_fusion.3), kind=kLoop, calls=%fused_computation | loop fusion | flops 2580480 | bytes 3096576 | tf_op jit(solution)/shard_map/concatenate | solution.py:123
  34.7 1.7 %broadcast_multiply_fusion = (f32[4,6,36,128]{3,0,2,1:T(4,128)S(1)}, f32[4,6,36,128]{3,0,2,1:T(4,128)S(1)}) fusion(f32[4,6,36,128]{3,0,2,1:T(4,128)S(1)} %get-tuple-element.171, f32[4,14,72,128]{3,0,2,1:T(4,128)S(1)} %maximum_maximum_fusion, s32[]{:T(128)S(6)} %select_n.201, s32[]{:T(128)S(6)} %select_n.200, f32[]{:T(128)S(6)} %sub.271, s32[]{:T(128)S(6)} %select_n.198, ...), kind=kLoop, calls=%fused_computation.194 | loop fusion | flops 1769472 | bytes 3096616 | tf_op jit(solution)/shard_map/mul | solution.py:137
  36.5 1.3 %constant_dynamic-update-slice_fusion.17 = f32[4,1,36,128]{3,0,2,1:T(4,128)S(1)} fusion(f32[4,1,36,128]{3,0,2,1:T(4,128)S(1)} %constant_dynamic-update-slice_fusion.18, s32[]{:T(128)} %bitcast.24, f32[4,128]{1,0:T(4,128)S(1)} %slice_bitcast_fusion.2, pred[]{:T(512)} %and_reduce_fusion), kind=kLoop, calls=%fused_computation.247 | loop fusion | flops 512 | bytes 6149 | tf_op jit(solution)/shard_map/scatter | solution.py:200
  38.0 1.7 %collective-permute-start.6 = (f32[4,5,36,128]{3,0,2,1:T(4,128)S(1)}, f32[4,5,36,128]{3,0,2,1:T(4,128)S(1)}, u32[]{:S(2)}, u32[]{:S(2)}) collective-permute-start(f32[4,5,36,128]{3,0,2,1:T(4,128)S(1)} %get-tuple-element.179), channel_id=1, source_target_pairs={{0,64},{64,128},{128,192},{192,256},{256,320},{320,384},{384,448},... | collective-permute-start | bytes 1105928 | tf_op jit(solution)/shard_map/ppermute | solution.py:29
  39.9 0.3 multiply_multiply_fusion.3
  40.2 0.2 fusion.136
  40.4 0.4 slice_multiply_fusion.23
  40.9 0.2 fusion.135
  41.1 0.4 slice_multiply_fusion.19
  41.5 0.2 fusion.134
  41.8 0.4 slice_multiply_fusion.15
  42.4 0.2 fusion.132
  42.6 0.4 slice_multiply_fusion.11
  43.2 0.3 slice_multiply_fusion.7
  43.5 0.2 fusion.130
  43.8 0.3 slice_multiply_fusion.3
  44.3 0.5 fusion.81
  44.9 6.7 %collective-permute-start.4 = (f32[4,6,18,128]{3,0,2,1:T(4,128)S(1)}, f32[4,6,18,128]{3,0,2,1:T(4,128)S(1)}, u32[]{:S(2)}, u32[]{:S(2)}) collective-permute-start(f32[4,6,18,128]{3,0,2,1:T(4,128)S(1)} %get-tuple-element.199), channel_id=1, source_target_pairs={{0,1},{1,2},{2,3},{3,4},{4,5},{5,6},{6,7},{7,8},{8,9},{9,10},{10,1... | collective-permute-start | bytes 663560 | tf_op jit(solution)/shard_map/ppermute | solution.py:29
  51.6 1.9 %collective-permute-start.5 = (f32[4,6,18,128]{3,0,2,1:T(4,128)S(1)}, f32[4,6,18,128]{3,0,2,1:T(4,128)S(1)}, u32[]{:S(2)}, u32[]{:S(2)}) collective-permute-start(f32[4,6,18,128]{3,0,2,1:T(4,128)S(1)} %get-tuple-element.198), channel_id=1, source_target_pairs={{1,0},{2,1},{3,2},{4,3},{5,4},{6,5},{7,6},{8,7},{9,8},{10,9},{11,1... | collective-permute-start | bytes 663560 | tf_op jit(solution)/shard_map/ppermute | solution.py:29
  53.7 2.5 %collective-permute-done.4 = f32[4,6,18,128]{3,0,2,1:T(4,128)S(1)} collective-permute-done((f32[4,6,18,128]{3,0,2,1:T(4,128)S(1)}, f32[4,6,18,128]{3,0,2,1:T(4,128)S(1)}, u32[]{:S(2)}, u32[]{:S(2)}) %collective-permute-start.4) | collective-permute-done | bytes 221216 | tf_op jit(solution)/shard_map/ppermute | solution.py:29
  56.2 7.5 %collective-permute-done.5 = f32[4,6,18,128]{3,0,2,1:T(4,128)S(1)} collective-permute-done((f32[4,6,18,128]{3,0,2,1:T(4,128)S(1)}, f32[4,6,18,128]{3,0,2,1:T(4,128)S(1)}, u32[]{:S(2)}, u32[]{:S(2)}) %collective-permute-start.5) | collective-permute-done | bytes 221216 | tf_op jit(solution)/shard_map/ppermute | solution.py:29
  63.7 4.9 %collective-permute-start.8 = (f32[5,4,128]{2,1,0:T(4,128)S(1)}, f32[5,4,128]{2,1,0:T(4,128)S(1)}, u32[]{:S(2)}, u32[]{:S(2)}) collective-permute-start(f32[5,4,128]{2,1,0:T(4,128)S(1)} %get-tuple-element.190), channel_id=1, source_target_pairs={{0,256},{64,320},{128,384},{192,448},{256,0},{320,64},{384,128},{4... | collective-permute-start | bytes 30728 | tf_op jit(solution)/shard_map/ppermute | solution.py:29
  68.8 0.2 fusion.127
  69.0 0.4 slice_multiply_fusion.10
  69.3 0.2 fusion.126
  69.6 0.3 slice_multiply_fusion.6
  69.9 0.2 fusion.125
  70.1 0.3 slice_multiply_fusion.2
  71.1 0.4 slice_multiply_fusion.22
  71.8 0.4 slice_multiply_fusion.18
  72.4 0.4 slice_multiply_fusion.14
  73.1 0.6 fusion.76
  73.7 3.9 %maximum_maximum_fusion.1 = f32[4,14,72,128]{3,0,2,1:T(4,128)S(1)} fusion(f32[4,4,36,128]{3,0,2,1:T(4,128)S(1)} %slice_select_fusion, f32[4,6,36,128]{3,0,2,1:T(4,128)S(1)} %get-tuple-element.112, f32[4,4,36,128]{3,0,2,1:T(4,128)S(1)} %slice_select_fusion.1), kind=kLoop, calls=%fused_computation.1 | loop fusion | flops 2580480 | bytes 3096576 | tf_op jit(solution)/shard_map/concatenate | solution.py:145
  77.8 0.6 multiply_add_fusion
  78.4 2.5 %fusion.65 = f32[4,6,36,128]{3,0,2,1:T(4,128)} fusion(f32[4,6,36,128]{3,0,2,1:T(4,128)S(1)} %get-tuple-element.171, f32[4,6,36,128]{3,0,2,1:T(4,128)S(1)} %get-tuple-element.113, f32[4,14,72,128]{3,0,2,1:T(4,128)S(1)} %maximum_maximum_fusion.1, s32[]{:T(128)S(6)} %select_n.219, s32[]{:T(128)S(6)} %select_n.218, s32[]{:T(128)S(6)} %select_n.216, ...), kind=kLoop, calls=%fused_computation.119 | loop fusion | flops 1769472 | bytes 3543080 | tf_op jit(solution)/shard_map/mul | solution.py:314
  (96 shorter events, 4.4 us)
Async XLA Ops:
  0.6 2.0 %copy-start.1 = (f32[4,128]{1,0:T(4,128)S(1)}, f32[4,128]{1,0:T(4,128)}, u32[]{:S(2)}) copy-start(f32[4,128]{1,0:T(4,128)} %param.20) | copy-start | bytes 6148
  2.5 10.3 %copy-start = (s32[4]{0:T(128)S(1)}, s32[4]{0:T(128)}, u32[]{:S(2)}) copy-start(s32[4]{0:T(128)} %param.24) | copy-start | bytes 52
  2.5 11.0 %copy-start.2 = (f32[2]{0:T(128)S(1)}, f32[2]{0:T(128)}, u32[]{:S(2)}) copy-start(f32[2]{0:T(128)} %param.25) | copy-start | bytes 28
  2.6 26.4 %copy-start.5 = (s32[4]{0:T(128)S(1)}, s32[4]{0:T(128)}, u32[]{:S(2)}) copy-start(s32[4]{0:T(128)} %constant.296.clone.1) | copy-start | bytes 52
  2.9 26.8 %collective-permute-start.3 = (f32[4,5,36,128]{3,0,2,1:T(4,128)S(1)}, f32[4,5,36,128]{3,0,2,1:T(4,128)S(1)}, u32[]{:S(2)}, u32[]{:S(2)}) collective-permute-start(f32[4,5,36,128]{3,0,2,1:T(4,128)S(1)} %get-tuple-element.202), channel_id=1, source_target_pairs={{0,448},{64,0},{128,64},{192,128},{256,192},{320,256},{384,320},{4... | collective-permute-start | bytes 1105928 | tf_op jit(solution)/shard_map/ppermute | solution.py:29
  3.6 26.2 %collective-permute-start.2 = (f32[4,5,36,128]{3,0,2,1:T(4,128)S(1)}, f32[4,5,36,128]{3,0,2,1:T(4,128)S(1)}, u32[]{:S(2)}, u32[]{:S(2)}) collective-permute-start(f32[4,5,36,128]{3,0,2,1:T(4,128)S(1)} %get-tuple-element.203), channel_id=1, source_target_pairs={{0,64},{64,128},{128,192},{192,256},{256,320},{320,384},{384,448},... | collective-permute-start | bytes 1105928 | tf_op jit(solution)/shard_map/ppermute | solution.py:29
  6.3 23.6 %collective-permute-start = (f32[4,7,18,128]{3,0,2,1:T(4,128)S(1)}, f32[4,7,18,128]{3,0,2,1:T(4,128)S(1)}, u32[]{:S(2)}, u32[]{:S(2)}) collective-permute-start(f32[4,7,18,128]{3,0,2,1:T(4,128)S(1)} %get-tuple-element.181), channel_id=1, source_target_pairs={{0,1},{1,2},{2,3},{3,4},{4,5},{5,6},{6,7},{7,8},{8,9},{9,10},{10,1... | collective-permute-start | bytes 774152 | tf_op jit(solution)/shard_map/ppermute | solution.py:29
  10.7 19.2 %collective-permute-start.1 = (f32[4,7,18,128]{3,0,2,1:T(4,128)S(1)}, f32[4,7,18,128]{3,0,2,1:T(4,128)S(1)}, u32[]{:S(2)}, u32[]{:S(2)}) collective-permute-start(f32[4,7,18,128]{3,0,2,1:T(4,128)S(1)} %get-tuple-element.180), channel_id=1, source_target_pairs={{1,0},{2,1},{3,2},{4,3},{5,4},{6,5},{7,6},{8,7},{9,8},{10,9},{11,1... | collective-permute-start | bytes 774152 | tf_op jit(solution)/shard_map/ppermute | solution.py:29
  37.9 15.6 %collective-permute-start.7 = (f32[4,5,36,128]{3,0,2,1:T(4,128)S(1)}, f32[4,5,36,128]{3,0,2,1:T(4,128)S(1)}, u32[]{:S(2)}, u32[]{:S(2)}) collective-permute-start(f32[4,5,36,128]{3,0,2,1:T(4,128)S(1)} %get-tuple-element.178), channel_id=1, source_target_pairs={{0,448},{64,0},{128,64},{192,128},{256,192},{320,256},{384,320},{4... | collective-permute-start | bytes 1105928 | tf_op jit(solution)/shard_map/ppermute | solution.py:29
  38.0 15.6 %collective-permute-start.6 = (f32[4,5,36,128]{3,0,2,1:T(4,128)S(1)}, f32[4,5,36,128]{3,0,2,1:T(4,128)S(1)}, u32[]{:S(2)}, u32[]{:S(2)}) collective-permute-start(f32[4,5,36,128]{3,0,2,1:T(4,128)S(1)} %get-tuple-element.179), channel_id=1, source_target_pairs={{0,64},{64,128},{128,192},{192,256},{256,320},{320,384},{384,448},... | collective-permute-start | bytes 1105928 | tf_op jit(solution)/shard_map/ppermute | solution.py:29
  44.9 11.3 %collective-permute-start.4 = (f32[4,6,18,128]{3,0,2,1:T(4,128)S(1)}, f32[4,6,18,128]{3,0,2,1:T(4,128)S(1)}, u32[]{:S(2)}, u32[]{:S(2)}) collective-permute-start(f32[4,6,18,128]{3,0,2,1:T(4,128)S(1)} %get-tuple-element.199), channel_id=1, source_target_pairs={{0,1},{1,2},{2,3},{3,4},{4,5},{5,6},{6,7},{7,8},{8,9},{9,10},{10,1... | collective-permute-start | bytes 663560 | tf_op jit(solution)/shard_map/ppermute | solution.py:29
  51.6 12.0 %collective-permute-start.5 = (f32[4,6,18,128]{3,0,2,1:T(4,128)S(1)}, f32[4,6,18,128]{3,0,2,1:T(4,128)S(1)}, u32[]{:S(2)}, u32[]{:S(2)}) collective-permute-start(f32[4,6,18,128]{3,0,2,1:T(4,128)S(1)} %get-tuple-element.198), channel_id=1, source_target_pairs={{1,0},{2,1},{3,2},{4,3},{5,4},{6,5},{7,6},{8,7},{9,8},{10,9},{11,1... | collective-permute-start | bytes 663560 | tf_op jit(solution)/shard_map/ppermute | solution.py:29
  63.7 14.0 %collective-permute-start.8 = (f32[5,4,128]{2,1,0:T(4,128)S(1)}, f32[5,4,128]{2,1,0:T(4,128)S(1)}, u32[]{:S(2)}, u32[]{:S(2)}) collective-permute-start(f32[5,4,128]{2,1,0:T(4,128)S(1)} %get-tuple-element.190), channel_id=1, source_target_pairs={{0,256},{64,320},{128,384},{192,448},{256,0},{320,64},{384,128},{4... | collective-permute-start | bytes 30728 | tf_op jit(solution)/shard_map/ppermute | solution.py:29
  73.7 4.1 %copy-start.3 = (s32[4,128]{1,0:T(4,128)S(1)}, s32[4,128]{1,0:T(4,128)}, u32[]{:S(2)}) copy-start(s32[4,128]{1,0:T(4,128)} %param.22) | copy-start | bytes 6148
  73.7 4.1 %copy-start.4 = (f32[4,128]{1,0:T(4,128)S(1)}, f32[4,128]{1,0:T(4,128)}, u32[]{:S(2)}) copy-start(f32[4,128]{1,0:T(4,128)} %param.23) | copy-start | bytes 6148

commit v9 on v3

--- a/solution.py
+++ b/solution.py
@@ -208,6 +208,7 @@
     freq_total = lax.axis_size("freq")
     slot = jnp.zeros((tile_rows, 1, dir_count, tile_cols), jnp.float32)
     slot = slot.at[:, 0, 0, :].set(partial_value)
+    gated, slot, below, above = lax.optimization_barrier((masked, slot, below, above))
 
     def tagged_halo(side):
         pieces = []
@@ -217,7 +218,7 @@
             take = min(freq_count, need)
             lo = freq_count - take if side < 0 else 0
             piece = jnp.concatenate(
-                [lax.slice_in_dim(masked, lo, lo + take, axis=1), slot], axis=1
+                [lax.slice_in_dim(gated, lo, lo + take, axis=1), slot], axis=1
             )
             got = from_neighbour(piece, "freq", -side * distance, True)
             source = freq_index + side * distance
@@ -231,19 +232,6 @@
 
     low = tagged_halo(-1)
     high = tagged_halo(+1)
-    low_bins = [p[1] for p in reversed(low)]
-    high_bins = [p[1] for p in high]
-    known = {0: partial_value}
-    for offset, _, value in low + high:
-        known[offset] = value
-    orbital = jnp.sqrt(gathered_sum(known, freq_index, freq_total, partial_value))
-    full_step = SUBSTEPS * sub_step
-    damping = 1.0 + full_step * canopy * veg_field * orbital
-
-    extended = jnp.concatenate(low_bins + [masked] + high_bins, axis=1)
-    change = source_change(extended, quad_offsets, quad_weights, freq_count)
-    increment = (masked + full_step * change) / damping[:, None, None, :] - masked
-
     geo_index = lax.axis_index("geo")
     geo_count = lax.axis_size("geo")
 
@@ -267,6 +255,23 @@
         sines[:half],
         True,
     )
+    arrays = [(p[1], p[2]) for p in low + high]
+    north, arrays = lax.optimization_barrier((north, arrays))
+    tagged = [(p[0],) + tuple(a) for p, a in zip(low + high, arrays)]
+    low, high = tagged[: len(low)], tagged[len(low) :]
+    low_bins = [p[1] for p in reversed(low)]
+    high_bins = [p[1] for p in high]
+    known = {0: partial_value}
+    for offset, _, value in low + high:
+        known[offset] = value
+    orbital = jnp.sqrt(gathered_sum(known, freq_index, freq_total, partial_value))
+    full_step = SUBSTEPS * sub_step
+    damping = 1.0 + full_step * canopy * veg_field * orbital
+
+    extended = jnp.concatenate(low_bins + [masked] + high_bins, axis=1)
+    change = source_change(extended, quad_offsets, quad_weights, freq_count)
+    increment = (masked + full_step * change) / damping[:, None, None, :] - masked
+
     s_off = [k + 1 for k in range(len(above))]
     a_spec, a_speed, a_wet = unpack(above, s_off)
     south = propagate(

time: 79 us -> 79.4 us (level)
  the two profiles are of different devices: /device:TPU:2 before, /device:TPU:242 now
where the time goes in v9:
time: 79.4 us; the launch traced here: 78.8 us
  starting transfers between devices  26.1 us (33%)
  other arithmetic  20.1 us (25%)
  between operations  15.5 us (20%)
  waiting for transfers between devices  8.81 us (11%)
  local copies, waits for them, and re-layouts  8.3 us (10%)
    ppermute x9, starting transfers between devices, from_neighbour(): return lax.ppermute(block, axis, pairs)  26.1 us
    ppermute x9, waiting for transfers between devices, from_neighbour(): return lax.ppermute(block, axis, pairs)  8.81 us
    mul x16, other arithmetic, propagate(): east_flux = east_speed[lo:hi] * spectrum  7.76 us
    slice x16, local copies, waits for them, and re-layouts, east_west(): behind = jnp.concatenate([zeros, east_flux[..., :-1]], axis=-1)  3.96 us
    mul x1, other arithmetic, source_change(): coupling * (centre * centre * (coef_plus * upper + coef_minus * lower) -...  3.88 us
    mul x1, other arithmetic, body(): return (wet_four * (moved + increment), orbital)  3.14 us
  transfers between devices with their start and end apart: 9, of which 3 were waited for; matrix products, arithmetic and copies ran while one was open for 25% of the time, Pallas kernels for 0%

profile of v9, /device:TPU:242, one launch (start us, length us, event | category | flops | bytes accessed | tf_op | source)
XLA Modules:
  0.0 78.8 jit_solution(16423868637643517735)
XLA Ops:
  0.7 0.7 convert_bitcast_fusion
  1.4 0.6 slice.672
  1.9 1.1 %fusion.165 = (f32[4,6,128]{2,0,1:T(4,128)S(1)}, f32[4,6,36,128]{3,0,2,1:T(4,128)S(1)}) fusion(f32[4,6,36,128]{3,0,2,1:T(4,128)} %param.13, f32[4,128]{1,0:T(4,128)S(1)} %get-tuple-element.175), kind=kLoop, calls=%fused_computation.334 | loop fusion | flops 218112 | bytes 899072 | tf_op jit(solution)/shard_map/reduce_sum | solution.py:205
  3.1 0.7 constant_dynamic-update-slice_fusion.24
  3.9 4.8 %collective-permute-start = (f32[4,7,18,128]{3,0,2,1:T(4,128)S(1)}, f32[4,7,18,128]{3,0,2,1:T(4,128)S(1)}, u32[]{:S(2)}, u32[]{:S(2)}) collective-permute-start(f32[4,7,18,128]{3,0,2,1:T(4,128)S(1)} %get-tuple-element.157), channel_id=1, source_target_pairs={{0,2},{1,3},{2,4},{3,5},{4,6},{5,7},{6,8},{7,9},{8,10},{9,11},{10,... | collective-permute-start | bytes 774152 | tf_op jit(solution)/shard_map/ppermute | solution.py:29
  8.7 3.5 %collective-permute-start.1 = (f32[4,7,18,128]{3,0,2,1:T(4,128)S(1)}, f32[4,7,18,128]{3,0,2,1:T(4,128)S(1)}, u32[]{:S(2)}, u32[]{:S(2)}) collective-permute-start(f32[4,7,18,128]{3,0,2,1:T(4,128)S(1)} %get-tuple-element.157), channel_id=1, source_target_pairs={{0,1},{1,2},{2,3},{3,4},{4,5},{5,6},{6,7},{7,8},{8,9},{9,10},{10,1... | collective-permute-start | bytes 774152 | tf_op jit(solution)/shard_map/ppermute | solution.py:29
  12.2 2.4 %collective-permute-start.2 = (f32[4,7,18,128]{3,0,2,1:T(4,128)S(1)}, f32[4,7,18,128]{3,0,2,1:T(4,128)S(1)}, u32[]{:S(2)}, u32[]{:S(2)}) collective-permute-start(f32[4,7,18,128]{3,0,2,1:T(4,128)S(1)} %get-tuple-element.156), channel_id=1, source_target_pairs={{1,0},{2,1},{3,2},{4,3},{5,4},{6,5},{7,6},{8,7},{9,8},{10,9},{11,1... | collective-permute-start | bytes 774152 | tf_op jit(solution)/shard_map/ppermute | solution.py:29
  14.6 3.1 %collective-permute-start.3 = (f32[4,7,18,128]{3,0,2,1:T(4,128)S(1)}, f32[4,7,18,128]{3,0,2,1:T(4,128)S(1)}, u32[]{:S(2)}, u32[]{:S(2)}) collective-permute-start(f32[4,7,18,128]{3,0,2,1:T(4,128)S(1)} %get-tuple-element.156), channel_id=1, source_target_pairs={{2,0},{3,1},{4,2},{5,3},{6,4},{7,5},{8,6},{9,7},{10,8},{11,9},{12,... | collective-permute-start | bytes 774152 | tf_op jit(solution)/shard_map/ppermute | solution.py:29
  17.9 0.6 fusion.167
  18.6 0.6 fusion.166
  33.6 3.3 %collective-permute-done.3 = f32[4,7,18,128]{3,0,2,1:T(4,128)S(1)} collective-permute-done((f32[4,7,18,128]{3,0,2,1:T(4,128)S(1)}, f32[4,7,18,128]{3,0,2,1:T(4,128)S(1)}, u32[]{:S(2)}, u32[]{:S(2)}) %collective-permute-start.3) | collective-permute-done | bytes 258080 | tf_op jit(solution)/shard_map/ppermute | solution.py:29
  37.2 0.4 copy-done
  37.7 1.7 %collective-permute-start.6 = (f32[4,7,36,128]{3,0,2,1:T(4,128)S(1)}, f32[4,7,36,128]{3,0,2,1:T(4,128)S(1)}, u32[]{:S(2)}, u32[]{:S(2)}) collective-permute-start(f32[4,7,36,128]{3,0,2,1:T(4,128)S(1)} %constant_dynamic-update-slice_fusion), channel_id=1, source_target_pairs={{0,448},{64,0},{128,64},{192,128},{256,192},{320,256},{384,320},{4... | collective-permute-start | bytes 1548296 | tf_op jit(solution)/shard_map/ppermute | solution.py:29
  39.4 0.2 add_multiply_fusion.4
  39.6 0.4 fusion.94
  40.1 0.3 fusion.150
  40.4 0.7 slice_multiply_fusion.11
  41.1 0.3 fusion.149
  41.5 0.7 slice_multiply_fusion.9
  42.4 0.3 fusion.148
  42.7 0.7 slice_multiply_fusion.7
  43.6 0.3 fusion.147
  43.9 0.5 slice_multiply_fusion.28
  44.6 0.4 slice_multiply_fusion.26
  45.3 0.4 slice_multiply_fusion.24
  46.0 0.4 slice_multiply_fusion.22
  46.7 0.7 slice-done
  47.5 0.4 fusion.96
  47.9 0.3 fusion.154
  48.2 0.6 slice_multiply_fusion.5
  48.8 0.3 fusion.153
  49.2 0.6 slice_multiply_fusion.3
  49.9 0.3 fusion.152
  50.2 0.6 slice_multiply_fusion.1
  50.9 0.3 fusion.151
  51.2 0.3 slice_multiply_fusion.20
  51.8 0.5 slice_multiply_fusion.18
  52.5 0.3 slice_multiply_fusion.16
  53.1 0.3 slice_multiply_fusion.14
  53.7 3.4 %collective-permute-start.5 = (f32[4,3,36,128]{3,0,2,1:T(4,128)S(1)}, f32[4,3,36,128]{3,0,2,1:T(4,128)S(1)}, u32[]{:S(2)}, u32[]{:S(2)}) collective-permute-start(f32[4,3,36,128]{3,0,2,1:T(4,128)S(1)} %get-tuple-element.151), channel_id=1, source_target_pairs={{0,128},{64,192},{128,256},{192,320},{256,384},{320,448},{384,0},{... | collective-permute-start | bytes 663560 | tf_op jit(solution)/shard_map/ppermute | solution.py:29
  57.1 2.4 %collective-permute-start.7 = (f32[4,3,36,128]{3,0,2,1:T(4,128)S(1)}, f32[4,3,36,128]{3,0,2,1:T(4,128)S(1)}, u32[]{:S(2)}, u32[]{:S(2)}) collective-permute-start(f32[4,3,36,128]{3,0,2,1:T(4,128)S(1)} %get-tuple-element.150), channel_id=1, source_target_pairs={{0,384},{64,448},{128,0},{192,64},{256,128},{320,192},{384,256},{4... | collective-permute-start | bytes 663560 | tf_op jit(solution)/shard_map/ppermute | solution.py:29
  59.6 0.5 fusion.106
  60.1 2.7 %collective-permute-done.5 = f32[4,3,36,128]{3,0,2,1:T(4,128)S(1)} collective-permute-done((f32[4,3,36,128]{3,0,2,1:T(4,128)S(1)}, f32[4,3,36,128]{3,0,2,1:T(4,128)S(1)}, u32[]{:S(2)}, u32[]{:S(2)}) %collective-permute-start.5) | collective-permute-done | bytes 221216 | tf_op jit(solution)/shard_map/ppermute | solution.py:29
  62.8 2.8 %collective-permute-done.7 = f32[4,3,36,128]{3,0,2,1:T(4,128)S(1)} collective-permute-done((f32[4,3,36,128]{3,0,2,1:T(4,128)S(1)}, f32[4,3,36,128]{3,0,2,1:T(4,128)S(1)}, u32[]{:S(2)}, u32[]{:S(2)}) %collective-permute-start.7) | collective-permute-done | bytes 221216 | tf_op jit(solution)/shard_map/ppermute | solution.py:29
  66.1 4.7 %collective-permute-start.8 = (f32[5,4,128]{2,1,0:T(4,128)S(1)}, f32[5,4,128]{2,1,0:T(4,128)S(1)}, u32[]{:S(2)}, u32[]{:S(2)}) collective-permute-start(f32[5,4,128]{2,1,0:T(4,128)S(1)} %get-tuple-element.162), channel_id=1, source_target_pairs={{0,256},{64,320},{128,384},{192,448},{256,0},{320,64},{384,128},{4... | collective-permute-start | bytes 30728 | tf_op jit(solution)/shard_map/ppermute | solution.py:29
  71.0 3.9 %subtract_multiply_fusion = f32[4,14,36,128]{3,0,2,1:T(4,128)S(1)} fusion(s32[]{:T(128)S(6)} %select_n.255, s32[]{:T(128)S(6)} %select_n.254, f32[4,22,36,128]{3,0,2,1:T(4,128)S(1)} %constant_dynamic-update-slice_fusion.2, s32[]{:T(128)S(6)} %select_n.252, s32[]{:T(128)S(6)} %select_n.251, s32[]{:T(128)S(6)} %select_n.250, s32[]{:T(128)S(6)} %select_n.248, ...), kind=kLoop, calls=%fused_computation.28 | loop fusion | flops 5677056 | bytes 3981352 | tf_op jit(solution)/shard_map/mul | solution.py:138
  75.1 0.6 multiply_add_fusion
  75.7 3.1 %fusion.93 = f32[4,6,36,128]{3,0,2,1:T(4,128)} fusion(f32[4,6,36,128]{3,0,2,1:T(4,128)S(1)} %get-tuple-element.55, f32[4,6,18,128]{3,0,2,1:T(4,128)S(1)} %get-tuple-element.169, f32[4,6,18,128]{3,0,2,1:T(4,128)S(1)} %get-tuple-element.57, f32[4,14,36,128]{3,0,2,1:T(4,128)S(1)} %subtract_multiply_fusion, s32[]{:T(128)S(6)} %select_n.263, s32[]{:T(128)S(6)} %select_n.262, ...), kind=kLoop, calls=%fused_computation.192 | loop fusion | flops 2211840 | bytes 2805800 | tf_op jit(solution)/shard_map/mul | solution.py:286
  (106 shorter events, 4.5 us)
Async XLA Ops:
  0.6 2.5 %copy-start.3 = (f32[4,128]{1,0:T(4,128)S(1)}, f32[4,128]{1,0:T(4,128)}, u32[]{:S(2)}) copy-start(f32[4,128]{1,0:T(4,128)} %param.14) | copy-start | bytes 6148
  0.6 17.3 %copy-start.2 = (s32[4]{0:T(128)S(1)}, s32[4]{0:T(128)}, u32[]{:S(2)}) copy-start(s32[4]{0:T(128)} %param.18) | copy-start | bytes 52
  0.7 17.9 %copy-start.4 = (f32[2]{0:T(128)S(1)}, f32[2]{0:T(128)}, u32[]{:S(2)}) copy-start(f32[2]{0:T(128)} %param.19) | copy-start | bytes 28
  3.9 29.7 %collective-permute-start = (f32[4,7,18,128]{3,0,2,1:T(4,128)S(1)}, f32[4,7,18,128]{3,0,2,1:T(4,128)S(1)}, u32[]{:S(2)}, u32[]{:S(2)}) collective-permute-start(f32[4,7,18,128]{3,0,2,1:T(4,128)S(1)} %get-tuple-element.157), channel_id=1, source_target_pairs={{0,2},{1,3},{2,4},{3,5},{4,6},{5,7},{6,8},{7,9},{8,10},{9,11},{10,... | collective-permute-start | bytes 774152 | tf_op jit(solution)/shard_map/ppermute | solution.py:29
  8.7 24.8 %collective-permute-start.1 = (f32[4,7,18,128]{3,0,2,1:T(4,128)S(1)}, f32[4,7,18,128]{3,0,2,1:T(4,128)S(1)}, u32[]{:S(2)}, u32[]{:S(2)}) collective-permute-start(f32[4,7,18,128]{3,0,2,1:T(4,128)S(1)} %get-tuple-element.157), channel_id=1, source_target_pairs={{0,1},{1,2},{2,3},{3,4},{4,5},{5,6},{6,7},{7,8},{8,9},{9,10},{10,1... | collective-permute-start | bytes 774152 | tf_op jit(solution)/shard_map/ppermute | solution.py:29
  12.2 21.4 %collective-permute-start.2 = (f32[4,7,18,128]{3,0,2,1:T(4,128)S(1)}, f32[4,7,18,128]{3,0,2,1:T(4,128)S(1)}, u32[]{:S(2)}, u32[]{:S(2)}) collective-permute-start(f32[4,7,18,128]{3,0,2,1:T(4,128)S(1)} %get-tuple-element.156), channel_id=1, source_target_pairs={{1,0},{2,1},{3,2},{4,3},{5,4},{6,5},{7,6},{8,7},{9,8},{10,9},{11,1... | collective-permute-start | bytes 774152 | tf_op jit(solution)/shard_map/ppermute | solution.py:29
  14.6 22.3 %collective-permute-start.3 = (f32[4,7,18,128]{3,0,2,1:T(4,128)S(1)}, f32[4,7,18,128]{3,0,2,1:T(4,128)S(1)}, u32[]{:S(2)}, u32[]{:S(2)}) collective-permute-start(f32[4,7,18,128]{3,0,2,1:T(4,128)S(1)} %get-tuple-element.156), channel_id=1, source_target_pairs={{2,0},{3,1},{4,2},{5,3},{6,4},{7,5},{8,6},{9,7},{10,8},{11,9},{12,... | collective-permute-start | bytes 774152 | tf_op jit(solution)/shard_map/ppermute | solution.py:29
  33.6 3.6 %copy-start.1 = (f32[4,7,18,128]{3,0,2,1:T(4,128)}, f32[4,7,18,128]{3,0,2,1:T(4,128)S(1)}, u32[]{:S(2)}) copy-start(f32[4,7,18,128]{3,0,2,1:T(4,128)S(1)} %collective-permute-done.2) | copy-start | bytes 774148
  36.9 0.7 copy-start
  37.6 28.0 %collective-permute-start.4 = (f32[4,7,36,128]{3,0,2,1:T(4,128)S(1)}, f32[4,7,36,128]{3,0,2,1:T(4,128)S(1)}, u32[]{:S(2)}, u32[]{:S(2)}) collective-permute-start(f32[4,7,36,128]{3,0,2,1:T(4,128)S(1)} %constant_dynamic-update-slice_fusion), channel_id=1, source_target_pairs={{0,64},{64,128},{128,192},{192,256},{256,320},{320,384},{384,448},... | collective-permute-start | bytes 1548296 | tf_op jit(solution)/shard_map/ppermute | solution.py:29
  37.7 28.1 %collective-permute-start.6 = (f32[4,7,36,128]{3,0,2,1:T(4,128)S(1)}, f32[4,7,36,128]{3,0,2,1:T(4,128)S(1)}, u32[]{:S(2)}, u32[]{:S(2)}) collective-permute-start(f32[4,7,36,128]{3,0,2,1:T(4,128)S(1)} %constant_dynamic-update-slice_fusion), channel_id=1, source_target_pairs={{0,448},{64,0},{128,64},{192,128},{256,192},{320,256},{384,320},{4... | collective-permute-start | bytes 1548296 | tf_op jit(solution)/shard_map/ppermute | solution.py:29
  46.4 0.9 %slice-start = ((f32[4,7,18,128]{3,0,2,1:T(4,128)}), f32[4,6,18,128]{3,0,2,1:T(4,128)S(1)}, s32[]{:S(2)}) async-start(f32[4,7,18,128]{3,0,2,1:T(4,128)} %copy-done), calls=%async_computation | async-start | bytes 442368 | tf_op jit(solution)/shard_map/slice | solution.py:243
  46.4 1.0 %slice-start.1 = ((f32[4,7,18,128]{3,0,2,1:T(4,128)}), f32[4,6,18,128]{3,0,2,1:T(4,128)S(1)}, s32[]{:S(2)}) async-start(f32[4,7,18,128]{3,0,2,1:T(4,128)} %copy-done.1), calls=%async_computation.1 | async-start | bytes 442368 | tf_op jit(solution)/shard_map/slice | solution.py:243
  53.7 9.1 %collective-permute-start.5 = (f32[4,3,36,128]{3,0,2,1:T(4,128)S(1)}, f32[4,3,36,128]{3,0,2,1:T(4,128)S(1)}, u32[]{:S(2)}, u32[]{:S(2)}) collective-permute-start(f32[4,3,36,128]{3,0,2,1:T(4,128)S(1)} %get-tuple-element.151), channel_id=1, source_target_pairs={{0,128},{64,192},{128,256},{192,320},{256,384},{320,448},{384,0},{... | collective-permute-start | bytes 663560 | tf_op jit(solution)/shard_map/ppermute | solution.py:29
  57.1 8.5 %collective-permute-start.7 = (f32[4,3,36,128]{3,0,2,1:T(4,128)S(1)}, f32[4,3,36,128]{3,0,2,1:T(4,128)S(1)}, u32[]{:S(2)}, u32[]{:S(2)}) collective-permute-start(f32[4,3,36,128]{3,0,2,1:T(4,128)S(1)} %get-tuple-element.150), channel_id=1, source_target_pairs={{0,384},{64,448},{128,0},{192,64},{256,128},{320,192},{384,256},{4... | collective-permute-start | bytes 663560 | tf_op jit(solution)/shard_map/ppermute | solution.py:29
  66.1 8.8 %collective-permute-start.8 = (f32[5,4,128]{2,1,0:T(4,128)S(1)}, f32[5,4,128]{2,1,0:T(4,128)S(1)}, u32[]{:S(2)}, u32[]{:S(2)}) collective-permute-start(f32[5,4,128]{2,1,0:T(4,128)S(1)} %get-tuple-element.162), channel_id=1, source_target_pairs={{0,256},{64,320},{128,384},{192,448},{256,0},{320,64},{384,128},{4... | collective-permute-start | bytes 30728 | tf_op jit(solution)/shard_map/ppermute | solution.py:29
  71.0 4.1 %copy-start.5 = (s32[4,128]{1,0:T(4,128)S(1)}, s32[4,128]{1,0:T(4,128)}, u32[]{:S(2)}) copy-start(s32[4,128]{1,0:T(4,128)} %param.16) | copy-start | bytes 6148
  71.0 4.1 %copy-start.6 = (f32[4,128]{1,0:T(4,128)S(1)}, f32[4,128]{1,0:T(4,128)}, u32[]{:S(2)}) copy-start(f32[4,128]{1,0:T(4,128)} %param.17) | copy-start | bytes 6148

commit v10 on v9

--- a/solution.py
+++ b/solution.py
@@ -80,6 +80,17 @@
     return glob[0]
 
 
+def full_sum(known, index, count, value):
+    if len(known) < count or count % 2:
+        return butterfly_sum(value, "freq")
+    table = jnp.stack([known[rel] for rel in range(count)])
+    table = jnp.concatenate([table, table], axis=0)
+    glob = lax.dynamic_slice_in_dim(table, (count - index) % count, count, axis=0)
+    while glob.shape[0] > 1:
+        glob = glob[0::2] + glob[1::2]
+    return glob[0]
+
+
 def physics(radian_freq, water_depth, dir_count):
     square = (radian_freq * radian_freq)[None, :, None]
     column = water_depth[:, None, :]
@@ -207,8 +218,12 @@
     freq_index = lax.axis_index("freq")
     freq_total = lax.axis_size("freq")
     slot = jnp.zeros((tile_rows, 1, dir_count, tile_cols), jnp.float32)
-    slot = slot.at[:, 0, 0, :].set(partial_value)
-    gated, slot, below, above = lax.optimization_barrier((masked, slot, below, above))
+    far = freq_total // 2
+    opposite = from_neighbour(partial_value, "freq", far, True)
+    slot = slot.at[:, 0, 0, :].set(partial_value).at[:, 0, 1, :].set(opposite)
+    gated, slot, below, above, opposite = lax.optimization_barrier(
+        (masked, slot, below, above, opposite)
+    )
 
     def tagged_halo(side):
         pieces = []
@@ -224,7 +239,7 @@
             source = freq_index + side * distance
             inside = (source >= 0) & (source < freq_total)
             pieces.append(
-                (distance * side, jnp.where(inside, got[:, :take], 0.0), got[:, take, 0, :])
+                (distance * side, jnp.where(inside, got[:, :take], 0.0), got[:, take, :2, :])
             )
             need -= take
             distance += 1
@@ -261,10 +276,11 @@
     low, high = tagged[: len(low)], tagged[len(low) :]
     low_bins = [p[1] for p in reversed(low)]
     high_bins = [p[1] for p in high]
-    known = {0: partial_value}
+    known = {0: partial_value, far: opposite}
     for offset, _, value in low + high:
-        known[offset] = value
-    orbital = jnp.sqrt(gathered_sum(known, freq_index, freq_total, partial_value))
+        known[offset % freq_total] = value[:, 0]
+        known[(offset + far) % freq_total] = value[:, 1]
+    orbital = jnp.sqrt(full_sum(known, freq_index, freq_total, partial_value))
     full_step = SUBSTEPS * sub_step
     damping = 1.0 + full_step * canopy * veg_field * orbital
 

time: 79.4 us -> 80 us (level)
  the two profiles are of different devices: /device:TPU:242 before, /device:TPU:278 now
where the time goes in v10:
time: 80 us; the launch traced here: 79.4 us
  starting transfers between devices  28.1 us (35%)
  other arithmetic  19.7 us (25%)
  between operations  15.7 us (20%)
  local copies, waits for them, and re-layouts  9.34 us (12%)
  waiting for transfers between devices  6.54 us (8%)
    ppermute x9, starting transfers between devices, from_neighbour(): return lax.ppermute(block, axis, pairs)  28.1 us
    mul x16, other arithmetic, propagate(): east_flux = east_speed[lo:hi] * spectrum  7.58 us
    ppermute x9, waiting for transfers between devices, from_neighbour(): return lax.ppermute(block, axis, pairs)  6.54 us
    slice x16, local copies, waits for them, and re-layouts, east_west(): behind = jnp.concatenate([zeros, east_flux[..., :-1]], axis=-1)  4.14 us
    mul x1, other arithmetic, source_change(): coupling * (centre * centre * (coef_plus * upper + coef_minus * lower) -...  3.77 us
    mul x1, other arithmetic, body(): return (wet_four * (moved + increment), orbital)  3.05 us
  transfers between devices with their start and end apart: 9, of which 2 were waited for; matrix products, arithmetic and copies ran while one was open for 21% of the time, Pallas kernels for 0%

profile of v10, /device:TPU:278, one launch (start us, length us, event | category | flops | bytes accessed | tf_op | source)
XLA Modules:
  0.0 79.4 jit_solution(3537979076707098902)
XLA Ops:
  0.7 0.7 convert_bitcast_fusion
  1.4 0.6 slice.706
  1.9 1.1 %fusion.165 = (f32[4,6,128]{2,0,1:T(4,128)S(1)}, f32[4,6,36,128]{3,0,2,1:T(4,128)S(1)}) fusion(f32[4,6,36,128]{3,0,2,1:T(4,128)} %param.15, f32[4,128]{1,0:T(4,128)S(1)} %get-tuple-element.181), kind=kLoop, calls=%fused_computation.333 | loop fusion | flops 218112 | bytes 899072 | tf_op jit(solution)/shard_map/reduce_sum | solution.py:216
  3.1 0.7 constant_dynamic-update-slice_fusion.23
  3.9 5.7 %collective-permute-start.1 = (f32[4,7,18,128]{3,0,2,1:T(4,128)S(1)}, f32[4,7,18,128]{3,0,2,1:T(4,128)S(1)}, u32[]{:S(2)}, u32[]{:S(2)}) collective-permute-start(f32[4,7,18,128]{3,0,2,1:T(4,128)S(1)} %get-tuple-element.169), channel_id=1, source_target_pairs={{0,2},{1,3},{2,4},{3,5},{4,6},{5,7},{6,8},{7,9},{8,10},{9,11},{10,... | collective-permute-start | bytes 774152 | tf_op jit(solution)/shard_map/ppermute | solution.py:29
  9.6 2.6 %collective-permute-start.2 = (f32[4,7,18,128]{3,0,2,1:T(4,128)S(1)}, f32[4,7,18,128]{3,0,2,1:T(4,128)S(1)}, u32[]{:S(2)}, u32[]{:S(2)}) collective-permute-start(f32[4,7,18,128]{3,0,2,1:T(4,128)S(1)} %get-tuple-element.169), channel_id=1, source_target_pairs={{0,1},{1,2},{2,3},{3,4},{4,5},{5,6},{6,7},{7,8},{8,9},{9,10},{10,1... | collective-permute-start | bytes 774152 | tf_op jit(solution)/shard_map/ppermute | solution.py:29
  12.2 3.3 %collective-permute-start.3 = (f32[4,7,18,128]{3,0,2,1:T(4,128)S(1)}, f32[4,7,18,128]{3,0,2,1:T(4,128)S(1)}, u32[]{:S(2)}, u32[]{:S(2)}) collective-permute-start(f32[4,7,18,128]{3,0,2,1:T(4,128)S(1)} %get-tuple-element.168), channel_id=1, source_target_pairs={{1,0},{2,1},{3,2},{4,3},{5,4},{6,5},{7,6},{8,7},{9,8},{10,9},{11,1... | collective-permute-start | bytes 774152 | tf_op jit(solution)/shard_map/ppermute | solution.py:29
  15.5 4.4 %collective-permute-start.4 = (f32[4,7,18,128]{3,0,2,1:T(4,128)S(1)}, f32[4,7,18,128]{3,0,2,1:T(4,128)S(1)}, u32[]{:S(2)}, u32[]{:S(2)}) collective-permute-start(f32[4,7,18,128]{3,0,2,1:T(4,128)S(1)} %get-tuple-element.168), channel_id=1, source_target_pairs={{2,0},{3,1},{4,2},{5,3},{6,4},{7,5},{8,6},{9,7},{10,8},{11,9},{12,... | collective-permute-start | bytes 774152 | tf_op jit(solution)/shard_map/ppermute | solution.py:29
  20.1 3.3 %collective-permute-start = (f32[4,128]{1,0:T(4,128)S(1)}, f32[4,128]{1,0:T(4,128)S(1)}, u32[]{:S(2)}, u32[]{:S(2)}) collective-permute-start(f32[4,128]{1,0:T(4,128)S(1)} %get-tuple-element.173), channel_id=1, source_target_pairs={{0,256},{64,320},{128,384},{192,448},{256,0},{320,64},{384,128},{4... | collective-permute-start | bytes 6152 | tf_op jit(solution)/shard_map/ppermute | solution.py:29
  23.6 0.6 fusion.167
  24.3 0.6 fusion.166
  39.1 0.7 constant_dynamic-update-slice_fusion.24
  40.1 0.4 copy-done.1
  40.7 1.7 %collective-permute-start.7 = (f32[4,7,36,128]{3,0,2,1:T(4,128)S(1)}, f32[4,7,36,128]{3,0,2,1:T(4,128)S(1)}, u32[]{:S(2)}, u32[]{:S(2)}) collective-permute-start(f32[4,7,36,128]{3,0,2,1:T(4,128)S(1)} %constant_dynamic-update-slice_fusion), channel_id=1, source_target_pairs={{0,448},{64,0},{128,64},{192,128},{256,192},{320,256},{384,320},{4... | collective-permute-start | bytes 1548296 | tf_op jit(solution)/shard_map/ppermute | solution.py:29
  42.6 0.4 fusion.94
  43.1 0.3 fusion.150
  43.4 0.7 slice_multiply_fusion.11
  44.1 0.3 fusion.149
  44.5 0.7 slice_multiply_fusion.9
  45.4 0.3 fusion.148
  45.7 0.7 slice_multiply_fusion.7
  46.6 0.3 fusion.147
  46.9 0.5 slice_multiply_fusion.28
  47.6 0.4 slice_multiply_fusion.26
  48.3 0.4 slice_multiply_fusion.24
  49.0 0.4 slice_multiply_fusion.22
  49.7 0.7 slice-done
  50.5 0.4 fusion.96
  50.9 0.3 fusion.154
  51.2 0.6 slice_multiply_fusion.5
  51.8 0.3 fusion.153
  52.2 0.6 slice_multiply_fusion.3
  52.9 0.3 fusion.152
  53.2 0.6 slice_multiply_fusion.1
  53.9 0.3 fusion.151
  54.2 0.3 slice_multiply_fusion.20
  54.8 0.3 slice_multiply_fusion.18
  55.2 0.4 fusion.162
  55.5 0.3 slice_multiply_fusion.16
  56.1 0.3 slice_multiply_fusion.14
  56.7 5.2 %collective-permute-start.6 = (f32[4,3,36,128]{3,0,2,1:T(4,128)S(1)}, f32[4,3,36,128]{3,0,2,1:T(4,128)S(1)}, u32[]{:S(2)}, u32[]{:S(2)}) collective-permute-start(f32[4,3,36,128]{3,0,2,1:T(4,128)S(1)} %get-tuple-element.163), channel_id=1, source_target_pairs={{0,128},{64,192},{128,256},{192,320},{256,384},{320,448},{384,0},{... | collective-permute-start | bytes 663560 | tf_op jit(solution)/shard_map/ppermute | solution.py:29
  61.9 1.9 %collective-permute-start.8 = (f32[4,3,36,128]{3,0,2,1:T(4,128)S(1)}, f32[4,3,36,128]{3,0,2,1:T(4,128)S(1)}, u32[]{:S(2)}, u32[]{:S(2)}) collective-permute-start(f32[4,3,36,128]{3,0,2,1:T(4,128)S(1)} %get-tuple-element.162), channel_id=1, source_target_pairs={{0,384},{64,448},{128,0},{192,64},{256,128},{320,192},{384,256},{4... | collective-permute-start | bytes 663560 | tf_op jit(solution)/shard_map/ppermute | solution.py:29
  63.8 0.5 fusion.106
  64.4 2.0 %collective-permute-done.6 = f32[4,3,36,128]{3,0,2,1:T(4,128)S(1)} collective-permute-done((f32[4,3,36,128]{3,0,2,1:T(4,128)S(1)}, f32[4,3,36,128]{3,0,2,1:T(4,128)S(1)}, u32[]{:S(2)}, u32[]{:S(2)}) %collective-permute-start.6) | collective-permute-done | bytes 221216 | tf_op jit(solution)/shard_map/ppermute | solution.py:29
  66.4 4.5 %collective-permute-done.8 = f32[4,3,36,128]{3,0,2,1:T(4,128)S(1)} collective-permute-done((f32[4,3,36,128]{3,0,2,1:T(4,128)S(1)}, f32[4,3,36,128]{3,0,2,1:T(4,128)S(1)}, u32[]{:S(2)}, u32[]{:S(2)}) %collective-permute-start.8) | collective-permute-done | bytes 221216 | tf_op jit(solution)/shard_map/ppermute | solution.py:29
  72.0 0.6 multiply_add_fusion
  72.5 3.8 %subtract_multiply_fusion = f32[4,14,36,128]{3,0,2,1:T(4,128)S(1)} fusion(s32[]{:T(128)S(6)} %select_n.255, s32[]{:T(128)S(6)} %select_n.254, f32[4,22,36,128]{3,0,2,1:T(4,128)S(1)} %constant_dynamic-update-slice_fusion.2, s32[]{:T(128)S(6)} %select_n.252, s32[]{:T(128)S(6)} %select_n.251, s32[]{:T(128)S(6)} %select_n.250, s32[]{:T(128)S(6)} %select_n.248, ...), kind=kLoop, calls=%fused_computation.28 | loop fusion | flops 5677056 | bytes 3981352 | tf_op jit(solution)/shard_map/mul | solution.py:149
  76.3 3.1 %fusion.93 = f32[4,6,36,128]{3,0,2,1:T(4,128)} fusion(f32[4,6,36,128]{3,0,2,1:T(4,128)S(1)} %get-tuple-element.67, f32[4,6,18,128]{3,0,2,1:T(4,128)S(1)} %get-tuple-element.175, f32[4,6,18,128]{3,0,2,1:T(4,128)S(1)} %get-tuple-element.69, f32[4,14,36,128]{3,0,2,1:T(4,128)S(1)} %subtract_multiply_fusion, s32[]{:T(128)S(6)} %select_n.263, s32[]{:T(128)S(6)} %select_n.262, ...), kind=kLoop, calls=%fused_computation.192 | loop fusion | flops 2211840 | bytes 2805800 | tf_op jit(solution)/shard_map/mul | solution.py:302
  (108 shorter events, 4.8 us)
Async XLA Ops:
  0.6 2.5 %copy-start.3 = (f32[4,128]{1,0:T(4,128)S(1)}, f32[4,128]{1,0:T(4,128)}, u32[]{:S(2)}) copy-start(f32[4,128]{1,0:T(4,128)} %param.16) | copy-start | bytes 6148
  0.6 23.0 %copy-start.2 = (s32[4]{0:T(128)S(1)}, s32[4]{0:T(128)}, u32[]{:S(2)}) copy-start(s32[4]{0:T(128)} %param.20) | copy-start | bytes 52
  0.7 23.6 %copy-start.4 = (f32[2]{0:T(128)S(1)}, f32[2]{0:T(128)}, u32[]{:S(2)}) copy-start(f32[2]{0:T(128)} %param.21) | copy-start | bytes 28
  3.9 35.9 %collective-permute-start.1 = (f32[4,7,18,128]{3,0,2,1:T(4,128)S(1)}, f32[4,7,18,128]{3,0,2,1:T(4,128)S(1)}, u32[]{:S(2)}, u32[]{:S(2)}) collective-permute-start(f32[4,7,18,128]{3,0,2,1:T(4,128)S(1)} %get-tuple-element.169), channel_id=1, source_target_pairs={{0,2},{1,3},{2,4},{3,5},{4,6},{5,7},{6,8},{7,9},{8,10},{9,11},{10,... | collective-permute-start | bytes 774152 | tf_op jit(solution)/shard_map/ppermute | solution.py:29
  9.6 30.2 %collective-permute-start.2 = (f32[4,7,18,128]{3,0,2,1:T(4,128)S(1)}, f32[4,7,18,128]{3,0,2,1:T(4,128)S(1)}, u32[]{:S(2)}, u32[]{:S(2)}) collective-permute-start(f32[4,7,18,128]{3,0,2,1:T(4,128)S(1)} %get-tuple-element.169), channel_id=1, source_target_pairs={{0,1},{1,2},{2,3},{3,4},{4,5},{5,6},{6,7},{7,8},{8,9},{9,10},{10,1... | collective-permute-start | bytes 774152 | tf_op jit(solution)/shard_map/ppermute | solution.py:29
  12.2 27.6 %collective-permute-start.3 = (f32[4,7,18,128]{3,0,2,1:T(4,128)S(1)}, f32[4,7,18,128]{3,0,2,1:T(4,128)S(1)}, u32[]{:S(2)}, u32[]{:S(2)}) collective-permute-start(f32[4,7,18,128]{3,0,2,1:T(4,128)S(1)} %get-tuple-element.168), channel_id=1, source_target_pairs={{1,0},{2,1},{3,2},{4,3},{5,4},{6,5},{7,6},{8,7},{9,8},{10,9},{11,1... | collective-permute-start | bytes 774152 | tf_op jit(solution)/shard_map/ppermute | solution.py:29
  15.5 24.3 %collective-permute-start.4 = (f32[4,7,18,128]{3,0,2,1:T(4,128)S(1)}, f32[4,7,18,128]{3,0,2,1:T(4,128)S(1)}, u32[]{:S(2)}, u32[]{:S(2)}) collective-permute-start(f32[4,7,18,128]{3,0,2,1:T(4,128)S(1)} %get-tuple-element.168), channel_id=1, source_target_pairs={{2,0},{3,1},{4,2},{5,3},{6,4},{7,5},{8,6},{9,7},{10,8},{11,9},{12,... | collective-permute-start | bytes 774152 | tf_op jit(solution)/shard_map/ppermute | solution.py:29
  20.1 19.1 %collective-permute-start = (f32[4,128]{1,0:T(4,128)S(1)}, f32[4,128]{1,0:T(4,128)S(1)}, u32[]{:S(2)}, u32[]{:S(2)}) collective-permute-start(f32[4,128]{1,0:T(4,128)S(1)} %get-tuple-element.173), channel_id=1, source_target_pairs={{0,256},{64,320},{128,384},{192,448},{256,0},{320,64},{384,128},{4... | collective-permute-start | bytes 6152 | tf_op jit(solution)/shard_map/ppermute | solution.py:29
  39.8 0.7 copy-start.1
  39.9 0.8 copy-start
  40.6 30.4 %collective-permute-start.5 = (f32[4,7,36,128]{3,0,2,1:T(4,128)S(1)}, f32[4,7,36,128]{3,0,2,1:T(4,128)S(1)}, u32[]{:S(2)}, u32[]{:S(2)}) collective-permute-start(f32[4,7,36,128]{3,0,2,1:T(4,128)S(1)} %constant_dynamic-update-slice_fusion), channel_id=1, source_target_pairs={{0,64},{64,128},{128,192},{192,256},{256,320},{320,384},{384,448},... | collective-permute-start | bytes 1548296 | tf_op jit(solution)/shard_map/ppermute | solution.py:29
  40.7 30.5 %collective-permute-start.7 = (f32[4,7,36,128]{3,0,2,1:T(4,128)S(1)}, f32[4,7,36,128]{3,0,2,1:T(4,128)S(1)}, u32[]{:S(2)}, u32[]{:S(2)}) collective-permute-start(f32[4,7,36,128]{3,0,2,1:T(4,128)S(1)} %constant_dynamic-update-slice_fusion), channel_id=1, source_target_pairs={{0,448},{64,0},{128,64},{192,128},{256,192},{320,256},{384,320},{4... | collective-permute-start | bytes 1548296 | tf_op jit(solution)/shard_map/ppermute | solution.py:29
  49.4 0.9 %slice-start = ((f32[4,7,18,128]{3,0,2,1:T(4,128)}), f32[4,6,18,128]{3,0,2,1:T(4,128)S(1)}, s32[]{:S(2)}) async-start(f32[4,7,18,128]{3,0,2,1:T(4,128)} %copy-done), calls=%async_computation | async-start | bytes 442368 | tf_op jit(solution)/shard_map/slice | solution.py:258
  49.4 1.0 %slice-start.1 = ((f32[4,7,18,128]{3,0,2,1:T(4,128)}), f32[4,6,18,128]{3,0,2,1:T(4,128)S(1)}, s32[]{:S(2)}) async-start(f32[4,7,18,128]{3,0,2,1:T(4,128)} %copy-done.1), calls=%async_computation.1 | async-start | bytes 442368 | tf_op jit(solution)/shard_map/slice | solution.py:258
  56.7 9.7 %collective-permute-start.6 = (f32[4,3,36,128]{3,0,2,1:T(4,128)S(1)}, f32[4,3,36,128]{3,0,2,1:T(4,128)S(1)}, u32[]{:S(2)}, u32[]{:S(2)}) collective-permute-start(f32[4,3,36,128]{3,0,2,1:T(4,128)S(1)} %get-tuple-element.163), channel_id=1, source_target_pairs={{0,128},{64,192},{128,256},{192,320},{256,384},{320,448},{384,0},{... | collective-permute-start | bytes 663560 | tf_op jit(solution)/shard_map/ppermute | solution.py:29
  61.9 9.0 %collective-permute-start.8 = (f32[4,3,36,128]{3,0,2,1:T(4,128)S(1)}, f32[4,3,36,128]{3,0,2,1:T(4,128)S(1)}, u32[]{:S(2)}, u32[]{:S(2)}) collective-permute-start(f32[4,3,36,128]{3,0,2,1:T(4,128)S(1)} %get-tuple-element.162), channel_id=1, source_target_pairs={{0,384},{64,448},{128,0},{192,64},{256,128},{320,192},{384,256},{4... | collective-permute-start | bytes 663560 | tf_op jit(solution)/shard_map/ppermute | solution.py:29
  71.3 0.7 copy-start.5
  71.3 0.7 copy-start.6

commit v11 on v10

--- a/solution.py
+++ b/solution.py
@@ -232,14 +232,15 @@
         while need > 0:
             take = min(freq_count, need)
             lo = freq_count - take if side < 0 else 0
-            piece = jnp.concatenate(
-                [lax.slice_in_dim(gated, lo, lo + take, axis=1), slot], axis=1
-            )
-            got = from_neighbour(piece, "freq", -side * distance, True)
+            got = from_neighbour(jnp.concatenate([gated, slot], axis=1), "freq", -side * distance, True)
             source = freq_index + side * distance
             inside = (source >= 0) & (source < freq_total)
             pieces.append(
-                (distance * side, jnp.where(inside, got[:, :take], 0.0), got[:, take, :2, :])
+                (
+                    distance * side,
+                    jnp.where(inside, got[:, lo : lo + take], 0.0),
+                    got[:, freq_count, :2, :],
+                )
             )
             need -= take
             distance += 1

time: 80 us -> 74 us (0.925)
  waiting for transfers between devices: 6.54 us -> 3.24 us
  starting transfers between devices: 28.1 us -> 26.6 us
    ppermute x9, waiting for transfers between devices: 6.54 us -> 3.24 us  [from_neighbour(): return lax.ppermute(block, axis, pairs)]
    ppermute x9, starting transfers between devices: 28.1 us -> 26.6 us  [from_neighbour(): return lax.ppermute(block, axis, pairs)]
  transfers between devices with their start and end apart: 9 -> 9, of which waited for: 2 -> 1; matrix products, arithmetic and copies ran while one was open for 21% -> 22% of each run, Pallas kernels for 0% -> 0%
where the time goes in v11:
time: 74 us; the launch traced here: 73.3 us
  starting transfers between devices  26.6 us (36%)
  other arithmetic  19.9 us (27%)
  between operations  15 us (20%)
  local copies, waits for them, and re-layouts  8.68 us (12%)
  waiting for transfers between devices  3.24 us (4%)
    ppermute x9, starting transfers between devices, from_neighbour(): return lax.ppermute(block, axis, pairs)  26.6 us
    mul x16, other arithmetic, propagate(): east_flux = east_speed[lo:hi] * spectrum  7.77 us
    slice x16, local copies, waits for them, and re-layouts, east_west(): behind = jnp.concatenate([zeros, east_flux[..., :-1]], axis=-1)  3.96 us
    mul x1, other arithmetic, source_change(): coupling * (centre * centre * (coef_plus * upper + coef_minus * lower) -...  3.8 us
    ppermute x9, waiting for transfers between devices, from_neighbour(): return lax.ppermute(block, axis, pairs)  3.24 us
    mul x1, other arithmetic, body(): return (wet_four * (moved + increment), orbital)  3.06 us
  transfers between devices with their start and end apart: 9, of which 1 were waited for; matrix products, arithmetic and copies ran while one was open for 22% of the time, Pallas kernels for 0%

profile of v11, /device:TPU:278, one launch (start us, length us, event | category | flops | bytes accessed | tf_op | source)
XLA Modules:
  0.0 73.3 jit_solution(17275853949998137978)
XLA Ops:
  0.7 0.7 convert_bitcast_fusion
  1.4 0.6 slice.700
  1.9 1.1 %fusion.164 = (f32[4,6,128]{2,0,1:T(4,128)S(1)}, f32[4,6,36,128]{3,0,2,1:T(4,128)S(1)}) fusion(f32[4,6,36,128]{3,0,2,1:T(4,128)} %param.15, f32[4,128]{1,0:T(4,128)S(1)} %get-tuple-element.177), kind=kLoop, calls=%fused_computation.330 | loop fusion | flops 218112 | bytes 899072 | tf_op jit(solution)/shard_map/reduce_sum | solution.py:216
  3.1 0.7 constant_dynamic-update-slice_fusion.23
  3.9 5.7 %collective-permute-start.1 = (f32[4,7,18,128]{3,0,2,1:T(4,128)S(1)}, f32[4,7,18,128]{3,0,2,1:T(4,128)S(1)}, u32[]{:S(2)}, u32[]{:S(2)}) collective-permute-start(f32[4,7,18,128]{3,0,2,1:T(4,128)S(1)} %get-tuple-element.165), channel_id=1, source_target_pairs={{0,2},{1,3},{2,4},{3,5},{4,6},{5,7},{6,8},{7,9},{8,10},{9,11},{10,... | collective-permute-start | bytes 774152 | tf_op jit(solution)/shard_map/ppermute | solution.py:29
  9.6 2.6 %collective-permute-start.2 = (f32[4,7,18,128]{3,0,2,1:T(4,128)S(1)}, f32[4,7,18,128]{3,0,2,1:T(4,128)S(1)}, u32[]{:S(2)}, u32[]{:S(2)}) collective-permute-start(f32[4,7,18,128]{3,0,2,1:T(4,128)S(1)} %get-tuple-element.165), channel_id=1, source_target_pairs={{0,1},{1,2},{2,3},{3,4},{4,5},{5,6},{6,7},{7,8},{8,9},{9,10},{10,1... | collective-permute-start | bytes 774152 | tf_op jit(solution)/shard_map/ppermute | solution.py:29
  12.2 3.3 %collective-permute-start.3 = (f32[4,7,18,128]{3,0,2,1:T(4,128)S(1)}, f32[4,7,18,128]{3,0,2,1:T(4,128)S(1)}, u32[]{:S(2)}, u32[]{:S(2)}) collective-permute-start(f32[4,7,18,128]{3,0,2,1:T(4,128)S(1)} %get-tuple-element.164), channel_id=1, source_target_pairs={{1,0},{2,1},{3,2},{4,3},{5,4},{6,5},{7,6},{8,7},{9,8},{10,9},{11,1... | collective-permute-start | bytes 774152 | tf_op jit(solution)/shard_map/ppermute | solution.py:29
  15.5 4.4 %collective-permute-start.4 = (f32[4,7,18,128]{3,0,2,1:T(4,128)S(1)}, f32[4,7,18,128]{3,0,2,1:T(4,128)S(1)}, u32[]{:S(2)}, u32[]{:S(2)}) collective-permute-start(f32[4,7,18,128]{3,0,2,1:T(4,128)S(1)} %get-tuple-element.164), channel_id=1, source_target_pairs={{2,0},{3,1},{4,2},{5,3},{6,4},{7,5},{8,6},{9,7},{10,8},{11,9},{12,... | collective-permute-start | bytes 774152 | tf_op jit(solution)/shard_map/ppermute | solution.py:29
  20.1 3.3 %collective-permute-start = (f32[4,128]{1,0:T(4,128)S(1)}, f32[4,128]{1,0:T(4,128)S(1)}, u32[]{:S(2)}, u32[]{:S(2)}) collective-permute-start(f32[4,128]{1,0:T(4,128)S(1)} %get-tuple-element.169), channel_id=1, source_target_pairs={{0,256},{64,320},{128,384},{192,448},{256,0},{320,64},{384,128},{4... | collective-permute-start | bytes 6152 | tf_op jit(solution)/shard_map/ppermute | solution.py:29
  23.6 0.6 fusion.166
  24.3 0.6 fusion.165
  38.4 0.7 constant_dynamic-update-slice_fusion.24
  39.4 4.0 %collective-permute-start.6 = (f32[4,7,36,128]{3,0,2,1:T(4,128)S(1)}, f32[4,7,36,128]{3,0,2,1:T(4,128)S(1)}, u32[]{:S(2)}, u32[]{:S(2)}) collective-permute-start(f32[4,7,36,128]{3,0,2,1:T(4,128)S(1)} %constant_dynamic-update-slice_fusion), channel_id=1, source_target_pairs={{0,128},{64,192},{128,256},{192,320},{256,384},{320,448},{384,0},{... | collective-permute-start | bytes 1548296 | tf_op jit(solution)/shard_map/ppermute | solution.py:29
  43.5 1.5 %collective-permute-start.7 = (f32[4,7,36,128]{3,0,2,1:T(4,128)S(1)}, f32[4,7,36,128]{3,0,2,1:T(4,128)S(1)}, u32[]{:S(2)}, u32[]{:S(2)}) collective-permute-start(f32[4,7,36,128]{3,0,2,1:T(4,128)S(1)} %constant_dynamic-update-slice_fusion), channel_id=1, source_target_pairs={{0,448},{64,0},{128,64},{192,128},{256,192},{320,256},{384,320},{4... | collective-permute-start | bytes 1548296 | tf_op jit(solution)/shard_map/ppermute | solution.py:29
  44.9 1.9 %collective-permute-start.8 = (f32[4,7,36,128]{3,0,2,1:T(4,128)S(1)}, f32[4,7,36,128]{3,0,2,1:T(4,128)S(1)}, u32[]{:S(2)}, u32[]{:S(2)}) collective-permute-start(f32[4,7,36,128]{3,0,2,1:T(4,128)S(1)} %constant_dynamic-update-slice_fusion), channel_id=1, source_target_pairs={{0,384},{64,448},{128,0},{192,64},{256,128},{320,192},{384,256},{4... | collective-permute-start | bytes 1548296 | tf_op jit(solution)/shard_map/ppermute | solution.py:29
  46.8 0.2 add_multiply_fusion.4
  47.1 0.4 fusion.94
  47.5 0.3 fusion.150
  47.8 0.7 %slice_multiply_fusion.11 = (f32[11,6,18,128]{3,0,2,1:T(8,128)S(1)}, f32[11,6,18,128]{3,0,2,1:T(8,128)S(1)}) fusion(f32[12,6,18,128]{3,0,2,1:T(8,128)S(1)} %get-tuple-element.163, f32[12,6,18,128]{3,0,2,1:T(8,128)S(1)} %get-tuple-element.127, f32[12,6,18,127]{3,0,2,1:T(8,128)S(1)} %get-tuple-element.117, f32[12,6,18,127]{3,0,2,1:T(8,128)S(1)} %get-tuple-element.116, ...), kind=kLoop, calls=%fused_computation.80 | loop fusion | flops 1368576 | bytes 5580178 | tf_op jit(solution)/shard_map/mul | solution.py:181
  48.6 0.3 fusion.149
  49.0 0.7 %slice_multiply_fusion.9 = (f32[10,6,18,128]{3,0,2,1:T(8,128)S(1)}, f32[10,6,18,128]{3,0,2,1:T(8,128)S(1)}) fusion(f32[12,6,18,128]{3,0,2,1:T(8,128)S(1)} %get-tuple-element.163, f32[11,6,18,128]{3,0,2,1:T(8,128)S(1)} %slice_multiply_fusion.10, f32[11,6,18,127]{3,0,2,1:T(8,128)S(1)} %get-tuple-element.115, f32[11,6,18,127]{3,0,2,1:T(8,128)S(1)} %get-tuple-element.114, ...), kind=kLoop, calls=%fused_computation.70 | loop fusion | flops 1244160 | bytes 5082866 | tf_op jit(solution)/shard_map/mul | solution.py:181
  49.9 0.3 fusion.148
  50.2 0.7 %slice_multiply_fusion.7 = (f32[9,6,18,128]{3,0,2,1:T(8,128)S(1)}, f32[9,6,18,128]{3,0,2,1:T(8,128)S(1)}) fusion(f32[12,6,18,128]{3,0,2,1:T(8,128)S(1)} %get-tuple-element.163, f32[10,6,18,128]{3,0,2,1:T(8,128)S(1)} %slice_multiply_fusion.8, f32[10,6,18,127]{3,0,2,1:T(8,128)S(1)} %get-tuple-element.113, f32[10,6,18,127]{3,0,2,1:T(8,128)S(1)} %get-tuple-element.112, ...), kind=kLoop, calls=%fused_computation.60 | loop fusion | flops 1119744 | bytes 4585554 | tf_op jit(solution)/shard_map/mul | solution.py:181
  51.1 0.3 fusion.147
  51.4 0.5 slice_multiply_fusion.28
  52.1 0.4 slice_multiply_fusion.26
  52.6 0.2 fusion.157
  52.8 0.4 slice_multiply_fusion.24
  53.3 0.2 fusion.156
  53.5 0.4 slice_multiply_fusion.22
  54.2 0.7 slice-done
  54.9 0.4 fusion.96
  55.4 0.3 fusion.154
  55.7 0.6 slice_multiply_fusion.5
  56.2 0.3 fusion.153
  56.7 0.6 slice_multiply_fusion.3
  57.4 0.3 fusion.152
  57.7 0.6 slice_multiply_fusion.1
  58.4 0.3 fusion.151
  58.7 0.3 slice_multiply_fusion.20
  59.2 0.3 slice_multiply_fusion.18
  59.8 0.3 slice_multiply_fusion.16
  60.4 0.5 slice_multiply_fusion.14
  61.1 0.5 fusion.106
  61.6 3.2 %collective-permute-done.8 = f32[4,7,36,128]{3,0,2,1:T(4,128)S(1)} collective-permute-done((f32[4,7,36,128]{3,0,2,1:T(4,128)S(1)}, f32[4,7,36,128]{3,0,2,1:T(4,128)S(1)}, u32[]{:S(2)}, u32[]{:S(2)}) %collective-permute-start.8) | collective-permute-done | bytes 516128 | tf_op jit(solution)/shard_map/ppermute | solution.py:29
  65.9 0.6 multiply_add_fusion
  66.5 3.8 %subtract_multiply_fusion = f32[4,14,36,128]{3,0,2,1:T(4,128)S(1)} fusion(s32[]{:T(128)S(6)} %select_n.255, s32[]{:T(128)S(6)} %select_n.254, f32[4,22,36,128]{3,0,2,1:T(4,128)S(1)} %constant_dynamic-update-slice_fusion.2, s32[]{:T(128)S(6)} %select_n.252, s32[]{:T(128)S(6)} %select_n.251, s32[]{:T(128)S(6)} %select_n.250, s32[]{:T(128)S(6)} %select_n.248, ...), kind=kLoop, calls=%fused_computation.28 | loop fusion | flops 5677056 | bytes 3981352 | tf_op jit(solution)/shard_map/mul | solution.py:149
  70.3 3.1 %fusion.93 = f32[4,6,36,128]{3,0,2,1:T(4,128)} fusion(f32[4,6,36,128]{3,0,2,1:T(4,128)S(1)} %get-tuple-element.67, f32[4,6,18,128]{3,0,2,1:T(4,128)S(1)} %get-tuple-element.171, f32[4,6,18,128]{3,0,2,1:T(4,128)S(1)} %get-tuple-element.69, f32[4,14,36,128]{3,0,2,1:T(4,128)S(1)} %subtract_multiply_fusion, s32[]{:T(128)S(6)} %select_n.263, s32[]{:T(128)S(6)} %select_n.262, ...), kind=kLoop, calls=%fused_computation.192 | loop fusion | flops 2211840 | bytes 2805800 | tf_op jit(solution)/shard_map/mul | solution.py:303
  (106 shorter events, 4.2 us)
Async XLA Ops:
  0.6 2.5 %copy-start.3 = (f32[4,128]{1,0:T(4,128)S(1)}, f32[4,128]{1,0:T(4,128)}, u32[]{:S(2)}) copy-start(f32[4,128]{1,0:T(4,128)} %param.16) | copy-start | bytes 6148
  0.6 23.0 %copy-start.2 = (s32[4]{0:T(128)S(1)}, s32[4]{0:T(128)}, u32[]{:S(2)}) copy-start(s32[4]{0:T(128)} %param.20) | copy-start | bytes 52
  0.7 23.6 %copy-start.4 = (f32[2]{0:T(128)S(1)}, f32[2]{0:T(128)}, u32[]{:S(2)}) copy-start(f32[2]{0:T(128)} %param.21) | copy-start | bytes 28
  3.9 35.2 %collective-permute-start.1 = (f32[4,7,18,128]{3,0,2,1:T(4,128)S(1)}, f32[4,7,18,128]{3,0,2,1:T(4,128)S(1)}, u32[]{:S(2)}, u32[]{:S(2)}) collective-permute-start(f32[4,7,18,128]{3,0,2,1:T(4,128)S(1)} %get-tuple-element.165), channel_id=1, source_target_pairs={{0,2},{1,3},{2,4},{3,5},{4,6},{5,7},{6,8},{7,9},{8,10},{9,11},{10,... | collective-permute-start | bytes 774152 | tf_op jit(solution)/shard_map/ppermute | solution.py:29
  9.6 29.5 %collective-permute-start.2 = (f32[4,7,18,128]{3,0,2,1:T(4,128)S(1)}, f32[4,7,18,128]{3,0,2,1:T(4,128)S(1)}, u32[]{:S(2)}, u32[]{:S(2)}) collective-permute-start(f32[4,7,18,128]{3,0,2,1:T(4,128)S(1)} %get-tuple-element.165), channel_id=1, source_target_pairs={{0,1},{1,2},{2,3},{3,4},{4,5},{5,6},{6,7},{7,8},{8,9},{9,10},{10,1... | collective-permute-start | bytes 774152 | tf_op jit(solution)/shard_map/ppermute | solution.py:29
  12.2 26.9 %collective-permute-start.3 = (f32[4,7,18,128]{3,0,2,1:T(4,128)S(1)}, f32[4,7,18,128]{3,0,2,1:T(4,128)S(1)}, u32[]{:S(2)}, u32[]{:S(2)}) collective-permute-start(f32[4,7,18,128]{3,0,2,1:T(4,128)S(1)} %get-tuple-element.164), channel_id=1, source_target_pairs={{1,0},{2,1},{3,2},{4,3},{5,4},{6,5},{7,6},{8,7},{9,8},{10,9},{11,1... | collective-permute-start | bytes 774152 | tf_op jit(solution)/shard_map/ppermute | solution.py:29
  15.5 23.6 %collective-permute-start.4 = (f32[4,7,18,128]{3,0,2,1:T(4,128)S(1)}, f32[4,7,18,128]{3,0,2,1:T(4,128)S(1)}, u32[]{:S(2)}, u32[]{:S(2)}) collective-permute-start(f32[4,7,18,128]{3,0,2,1:T(4,128)S(1)} %get-tuple-element.164), channel_id=1, source_target_pairs={{2,0},{3,1},{4,2},{5,3},{6,4},{7,5},{8,6},{9,7},{10,8},{11,9},{12,... | collective-permute-start | bytes 774152 | tf_op jit(solution)/shard_map/ppermute | solution.py:29
  20.1 18.4 %collective-permute-start = (f32[4,128]{1,0:T(4,128)S(1)}, f32[4,128]{1,0:T(4,128)S(1)}, u32[]{:S(2)}, u32[]{:S(2)}) collective-permute-start(f32[4,128]{1,0:T(4,128)S(1)} %get-tuple-element.169), channel_id=1, source_target_pairs={{0,256},{64,320},{128,384},{192,448},{256,0},{320,64},{384,128},{4... | collective-permute-start | bytes 6152 | tf_op jit(solution)/shard_map/ppermute | solution.py:29
  39.1 8.0 %copy-start.1 = (f32[4,7,18,128]{3,0,2,1:T(4,128)}, f32[4,7,18,128]{3,0,2,1:T(4,128)S(1)}, u32[]{:S(2)}) copy-start(f32[4,7,18,128]{3,0,2,1:T(4,128)S(1)} %collective-permute-done.3) | copy-start | bytes 774148
  39.1 7.9 %copy-start = (f32[4,7,18,128]{3,0,2,1:T(4,128)}, f32[4,7,18,128]{3,0,2,1:T(4,128)S(1)}, u32[]{:S(2)}) copy-start(f32[4,7,18,128]{3,0,2,1:T(4,128)S(1)} %collective-permute-done.4) | copy-start | bytes 774148
  39.4 22.2 %collective-permute-start.5 = (f32[4,7,36,128]{3,0,2,1:T(4,128)S(1)}, f32[4,7,36,128]{3,0,2,1:T(4,128)S(1)}, u32[]{:S(2)}, u32[]{:S(2)}) collective-permute-start(f32[4,7,36,128]{3,0,2,1:T(4,128)S(1)} %constant_dynamic-update-slice_fusion), channel_id=1, source_target_pairs={{0,64},{64,128},{128,192},{192,256},{256,320},{320,384},{384,448},... | collective-permute-start | bytes 1548296 | tf_op jit(solution)/shard_map/ppermute | solution.py:29
  39.4 25.7 %collective-permute-start.6 = (f32[4,7,36,128]{3,0,2,1:T(4,128)S(1)}, f32[4,7,36,128]{3,0,2,1:T(4,128)S(1)}, u32[]{:S(2)}, u32[]{:S(2)}) collective-permute-start(f32[4,7,36,128]{3,0,2,1:T(4,128)S(1)} %constant_dynamic-update-slice_fusion), channel_id=1, source_target_pairs={{0,128},{64,192},{128,256},{192,320},{256,384},{320,448},{384,0},{... | collective-permute-start | bytes 1548296 | tf_op jit(solution)/shard_map/ppermute | solution.py:29
  43.5 21.4 %collective-permute-start.7 = (f32[4,7,36,128]{3,0,2,1:T(4,128)S(1)}, f32[4,7,36,128]{3,0,2,1:T(4,128)S(1)}, u32[]{:S(2)}, u32[]{:S(2)}) collective-permute-start(f32[4,7,36,128]{3,0,2,1:T(4,128)S(1)} %constant_dynamic-update-slice_fusion), channel_id=1, source_target_pairs={{0,448},{64,0},{128,64},{192,128},{256,192},{320,256},{384,320},{4... | collective-permute-start | bytes 1548296 | tf_op jit(solution)/shard_map/ppermute | solution.py:29
  44.9 19.9 %collective-permute-start.8 = (f32[4,7,36,128]{3,0,2,1:T(4,128)S(1)}, f32[4,7,36,128]{3,0,2,1:T(4,128)S(1)}, u32[]{:S(2)}, u32[]{:S(2)}) collective-permute-start(f32[4,7,36,128]{3,0,2,1:T(4,128)S(1)} %constant_dynamic-update-slice_fusion), channel_id=1, source_target_pairs={{0,384},{64,448},{128,0},{192,64},{256,128},{320,192},{384,256},{4... | collective-permute-start | bytes 1548296 | tf_op jit(solution)/shard_map/ppermute | solution.py:29
  53.9 0.9 %slice-start = ((f32[4,7,18,128]{3,0,2,1:T(4,128)}), f32[4,6,18,128]{3,0,2,1:T(4,128)S(1)}, s32[]{:S(2)}) async-start(f32[4,7,18,128]{3,0,2,1:T(4,128)} %copy-done), calls=%async_computation | async-start | bytes 442368 | tf_op jit(solution)/shard_map/slice | solution.py:259
  53.9 1.0 %slice-start.1 = ((f32[4,7,18,128]{3,0,2,1:T(4,128)}), f32[4,6,18,128]{3,0,2,1:T(4,128)S(1)}, s32[]{:S(2)}) async-start(f32[4,7,18,128]{3,0,2,1:T(4,128)} %copy-done.1), calls=%async_computation.1 | async-start | bytes 442368 | tf_op jit(solution)/shard_map/slice | solution.py:259
  65.2 0.7 copy-start.5
  65.2 0.7 copy-start.6

commit v12 on v11

--- a/solution.py
+++ b/solution.py
@@ -7,6 +7,7 @@
 
 FH = 4
 SUBSTEPS = 8
+SEND_BINS = 6
 
 
 gravity = 9.81
@@ -205,10 +206,14 @@
     half = dir_count // 2
     cosines, sines = angles_of(dir_count)
 
-    fields = jnp.zeros((tile_rows, 1, half, tile_cols), jnp.float32)
-    fields = fields.at[:, 0, 0, :].set(wet_field).at[:, 0, 1, :].set(water_depth)
-    north_msg = jnp.concatenate([masked[:, :, :half], fields], axis=1)
-    south_msg = jnp.concatenate([masked[:, :, half:], fields], axis=1)
+    fields = jnp.stack([wet_field, water_depth], axis=1)
+    flat = freq_count * half
+    north_msg = jnp.concatenate(
+        [masked[:, :, :half].reshape(tile_rows, flat, tile_cols), fields], axis=1
+    )
+    south_msg = jnp.concatenate(
+        [masked[:, :, half:].reshape(tile_rows, flat, tile_cols), fields], axis=1
+    )
     below = halo(north_msg, "geo", 0, SUBSTEPS, -1)
     above = halo(south_msg, "geo", 0, SUBSTEPS, +1)
 
@@ -217,10 +222,9 @@
 
     freq_index = lax.axis_index("freq")
     freq_total = lax.axis_size("freq")
-    slot = jnp.zeros((tile_rows, 1, dir_count, tile_cols), jnp.float32)
     far = freq_total // 2
     opposite = from_neighbour(partial_value, "freq", far, True)
-    slot = slot.at[:, 0, 0, :].set(partial_value).at[:, 0, 1, :].set(opposite)
+    slot = jnp.stack([partial_value, opposite], axis=1)
     gated, slot, below, above, opposite = lax.optimization_barrier(
         (masked, slot, below, above, opposite)
     )
@@ -231,15 +235,25 @@
         need = 2 * FH
         while need > 0:
             take = min(freq_count, need)
-            lo = freq_count - take if side < 0 else 0
-            got = from_neighbour(jnp.concatenate([gated, slot], axis=1), "freq", -side * distance, True)
+            send = min(freq_count, max(take, SEND_BINS))
+            lo = freq_count - send if side < 0 else 0
+            cell = send * dir_count
+            block = lax.slice_in_dim(gated, lo, lo + send, axis=1)
+            got = from_neighbour(
+                jnp.concatenate([block.reshape(tile_rows, cell, tile_cols), slot], axis=1),
+                "freq",
+                -side * distance,
+                True,
+            )
+            first = send - take if side < 0 else 0
             source = freq_index + side * distance
             inside = (source >= 0) & (source < freq_total)
+            bins = got[:, :cell].reshape(tile_rows, send, dir_count, tile_cols)
             pieces.append(
                 (
                     distance * side,
-                    jnp.where(inside, got[:, lo : lo + take], 0.0),
-                    got[:, freq_count, :2, :],
+                    jnp.where(inside, bins[:, first : first + take], 0.0),
+                    got[:, cell:],
                 )
             )
             need -= take
@@ -255,9 +269,9 @@
         spectra, speeds, wets = [], [], []
         for part, offset in zip(parts, offsets):
             valid = (geo_index + offset >= 0) & (geo_index + offset < geo_count)
-            depth = jnp.where(valid, part[:, freq_count, 1, :], 1.0)
-            spectra.append(part[:, :freq_count])
-            wets.append(part[:, freq_count, 0, :])
+            depth = jnp.where(valid, part[:, flat + 1, :], 1.0)
+            spectra.append(part[:, :flat].reshape(tile_rows, freq_count, half, tile_cols))
+            wets.append(part[:, flat, :])
             speeds.append(physics(radian_freq, depth, dir_count)[0])
         return spectra, speeds, wets
 

time: 74 us -> 72.8 us (0.984)
  the two profiles are of different devices: /device:TPU:278 before, /device:TPU:272 now
where the time goes in v12:
time: 72.8 us; the launch traced here: 72.2 us
  starting transfers between devices  29.3 us (40%)
  other arithmetic  20.1 us (28%)
  between operations  15.8 us (22%)
  local copies, waits for them, and re-layouts  6.85 us (9%)
    ppermute x9, starting transfers between devices, from_neighbour(): return lax.ppermute(block, axis, pairs)  29.3 us
    mul x16, other arithmetic, propagate(): east_flux = east_speed[lo:hi] * spectrum  7.76 us
    slice x16, local copies, waits for them, and re-layouts, east_west(): behind = jnp.concatenate([zeros, east_flux[..., :-1]], axis=-1)  3.96 us
    mul x1, other arithmetic, source_change(): coupling * (centre * centre * (coef_plus * upper + coef_minus * lower) -...  3.89 us
    mul x1, other arithmetic, body(): return (wet_four * (moved + increment), orbital)  3.16 us
  transfers between devices with their start and end apart: 9, of which 0 were waited for; matrix products, arithmetic and copies ran while one was open for 22% of the time, Pallas kernels for 0%

profile of v12, /device:TPU:272, one launch (start us, length us, event | category | flops | bytes accessed | tf_op | source)
XLA Modules:
  0.0 72.2 jit_solution(4571036953163668397)
XLA Ops:
  0.7 0.7 convert_bitcast_fusion
  1.4 1.1 %fusion.164 = (f32[4,6,128]{2,0,1:T(4,128)S(1)}, f32[4,6,36,128]{3,0,2,1:T(4,128)S(1)}) fusion(f32[4,6,36,128]{3,0,2,1:T(4,128)} %param.7, f32[4,128]{1,0:T(4,128)S(1)} %get-tuple-element.129), kind=kLoop, calls=%fused_computation.327 | loop fusion | flops 218112 | bytes 899072 | tf_op jit(solution)/shard_map/reduce_sum | solution.py:221
  2.6 5.7 %collective-permute-start.1 = (f32[4,110,128]{2,0,1:T(4,128)S(1)}, f32[4,110,128]{2,0,1:T(4,128)S(1)}, u32[]{:S(2)}, u32[]{:S(2)}) collective-permute-start(f32[4,110,128]{2,0,1:T(4,128)S(1)} %get-tuple-element.119), channel_id=1, source_target_pairs={{0,2},{1,3},{2,4},{3,5},{4,6},{5,7},{6,8},{7,9},{8,10},{9,11},{10,... | collective-permute-start | bytes 675848 | tf_op jit(solution)/shard_map/ppermute | solution.py:30
  8.4 2.6 %collective-permute-start.2 = (f32[4,110,128]{2,0,1:T(4,128)S(1)}, f32[4,110,128]{2,0,1:T(4,128)S(1)}, u32[]{:S(2)}, u32[]{:S(2)}) collective-permute-start(f32[4,110,128]{2,0,1:T(4,128)S(1)} %get-tuple-element.119), channel_id=1, source_target_pairs={{0,1},{1,2},{2,3},{3,4},{4,5},{5,6},{6,7},{7,8},{8,9},{9,10},{10,1... | collective-permute-start | bytes 675848 | tf_op jit(solution)/shard_map/ppermute | solution.py:30
  11.0 3.3 %collective-permute-start.3 = (f32[4,110,128]{2,0,1:T(4,128)S(1)}, f32[4,110,128]{2,0,1:T(4,128)S(1)}, u32[]{:S(2)}, u32[]{:S(2)}) collective-permute-start(f32[4,110,128]{2,0,1:T(4,128)S(1)} %get-tuple-element.118), channel_id=1, source_target_pairs={{1,0},{2,1},{3,2},{4,3},{5,4},{6,5},{7,6},{8,7},{9,8},{10,9},{11,1... | collective-permute-start | bytes 675848 | tf_op jit(solution)/shard_map/ppermute | solution.py:30
  14.2 4.4 %collective-permute-start.4 = (f32[4,110,128]{2,0,1:T(4,128)S(1)}, f32[4,110,128]{2,0,1:T(4,128)S(1)}, u32[]{:S(2)}, u32[]{:S(2)}) collective-permute-start(f32[4,110,128]{2,0,1:T(4,128)S(1)} %get-tuple-element.118), channel_id=1, source_target_pairs={{2,0},{3,1},{4,2},{5,3},{6,4},{7,5},{8,6},{9,7},{10,8},{11,9},{12,... | collective-permute-start | bytes 675848 | tf_op jit(solution)/shard_map/ppermute | solution.py:30
  18.8 4.9 %collective-permute-start = (f32[4,128]{1,0:T(4,128)S(1)}, f32[4,128]{1,0:T(4,128)S(1)}, u32[]{:S(2)}, u32[]{:S(2)}) collective-permute-start(f32[4,128]{1,0:T(4,128)S(1)} %get-tuple-element.121), channel_id=1, source_target_pairs={{0,256},{64,320},{128,384},{192,448},{256,0},{320,64},{384,128},{4... | collective-permute-start | bytes 6152 | tf_op jit(solution)/shard_map/ppermute | solution.py:30
  23.9 0.7 fusion.166
  36.3 0.6 fusion.165
  40.1 2.5 %collective-permute-start.6 = (f32[4,218,128]{2,0,1:T(4,128)S(1)}, f32[4,218,128]{2,0,1:T(4,128)S(1)}, u32[]{:S(2)}, u32[]{:S(2)}) collective-permute-start(f32[4,218,128]{2,0,1:T(4,128)S(1)} %pad_maximum_fusion.4), channel_id=1, source_target_pairs={{0,128},{64,192},{128,256},{192,320},{256,384},{320,448},{384,0},{... | collective-permute-start | bytes 1339400 | tf_op jit(solution)/shard_map/ppermute | solution.py:30
  42.6 2.7 %collective-permute-start.7 = (f32[4,218,128]{2,0,1:T(4,128)S(1)}, f32[4,218,128]{2,0,1:T(4,128)S(1)}, u32[]{:S(2)}, u32[]{:S(2)}) collective-permute-start(f32[4,218,128]{2,0,1:T(4,128)S(1)} %pad_maximum_fusion.4), channel_id=1, source_target_pairs={{0,448},{64,0},{128,64},{192,128},{256,192},{320,256},{384,320},{4... | collective-permute-start | bytes 1339400 | tf_op jit(solution)/shard_map/ppermute | solution.py:30
  45.2 3.3 %collective-permute-start.8 = (f32[4,218,128]{2,0,1:T(4,128)S(1)}, f32[4,218,128]{2,0,1:T(4,128)S(1)}, u32[]{:S(2)}, u32[]{:S(2)}) collective-permute-start(f32[4,218,128]{2,0,1:T(4,128)S(1)} %pad_maximum_fusion.4), channel_id=1, source_target_pairs={{0,384},{64,448},{128,0},{192,64},{256,128},{320,192},{384,256},{4... | collective-permute-start | bytes 1339400 | tf_op jit(solution)/shard_map/ppermute | solution.py:30
  48.6 0.2 add_multiply_fusion.4
  48.8 0.4 fusion.94
  49.3 0.3 fusion.150
  49.6 0.7 %slice_multiply_fusion.11 = (f32[11,6,18,128]{3,0,2,1:T(8,128)S(1)}, f32[11,6,18,128]{3,0,2,1:T(8,128)S(1)}) fusion(f32[12,6,18,128]{3,0,2,1:T(8,128)S(1)} %get-tuple-element.115, f32[12,6,18,128]{3,0,2,1:T(8,128)S(1)} %get-tuple-element.79, f32[12,6,18,127]{3,0,2,1:T(8,128)S(1)} %get-tuple-element.69, f32[12,6,18,127]{3,0,2,1:T(8,128)S(1)} %get-tuple-element.68, ...), kind=kLoop, calls=%fused_computation.80 | loop fusion | flops 1368576 | bytes 5580178 | tf_op jit(solution)/shard_map/mul | solution.py:182
  50.3 0.3 fusion.149
  50.8 0.7 %slice_multiply_fusion.9 = (f32[10,6,18,128]{3,0,2,1:T(8,128)S(1)}, f32[10,6,18,128]{3,0,2,1:T(8,128)S(1)}) fusion(f32[12,6,18,128]{3,0,2,1:T(8,128)S(1)} %get-tuple-element.115, f32[11,6,18,128]{3,0,2,1:T(8,128)S(1)} %slice_multiply_fusion.10, f32[11,6,18,127]{3,0,2,1:T(8,128)S(1)} %get-tuple-element.67, f32[11,6,18,127]{3,0,2,1:T(8,128)S(1)} %get-tuple-element.66, ...), kind=kLoop, calls=%fused_computation.70 | loop fusion | flops 1244160 | bytes 5082866 | tf_op jit(solution)/shard_map/mul | solution.py:182
  51.6 0.3 fusion.148
  51.9 0.7 %slice_multiply_fusion.7 = (f32[9,6,18,128]{3,0,2,1:T(8,128)S(1)}, f32[9,6,18,128]{3,0,2,1:T(8,128)S(1)}) fusion(f32[12,6,18,128]{3,0,2,1:T(8,128)S(1)} %get-tuple-element.115, f32[10,6,18,128]{3,0,2,1:T(8,128)S(1)} %slice_multiply_fusion.8, f32[10,6,18,127]{3,0,2,1:T(8,128)S(1)} %get-tuple-element.65, f32[10,6,18,127]{3,0,2,1:T(8,128)S(1)} %get-tuple-element.64, ...), kind=kLoop, calls=%fused_computation.60 | loop fusion | flops 1119744 | bytes 4585554 | tf_op jit(solution)/shard_map/mul | solution.py:182
  52.8 0.3 fusion.147
  53.1 0.5 slice_multiply_fusion.28
  53.7 0.2 fusion.158
  53.9 0.4 slice_multiply_fusion.26
  54.3 0.2 fusion.157
  54.5 0.4 slice_multiply_fusion.24
  55.0 0.2 fusion.156
  55.2 0.4 slice_multiply_fusion.22
  55.9 0.7 slice-done
  56.7 0.4 fusion.96
  57.1 0.3 fusion.154
  57.4 0.6 slice_multiply_fusion.5
  58.0 0.3 fusion.153
  58.4 0.6 slice_multiply_fusion.3
  59.1 0.3 fusion.152
  59.4 0.6 slice_multiply_fusion.1
  60.1 0.3 fusion.151
  60.4 0.3 slice_multiply_fusion.20
  60.8 0.2 fusion.162
  61.0 0.3 slice_multiply_fusion.18
  61.4 0.2 fusion.161
  61.6 0.3 slice_multiply_fusion.16
  61.9 0.2 fusion.160
  62.1 0.5 slice_multiply_fusion.14
  62.8 0.5 fusion.106
  64.5 0.6 multiply_add_fusion
  65.1 3.9 %subtract_multiply_fusion = f32[4,14,36,128]{3,0,2,1:T(4,128)S(1)} fusion(s32[]{:T(128)S(6)} %select_n.235, s32[]{:T(128)S(6)} %select_n.234, f32[4,22,36,128]{3,0,2,1:T(4,128)S(1)} %constant_dynamic-update-slice_fusion, s32[]{:T(128)S(6)} %select_n.232, s32[]{:T(128)S(6)} %select_n.231, s32[]{:T(128)S(6)} %select_n.230, s32[]{:T(128)S(6)} %select_n.228, ...), kind=kLoop, calls=%fused_computation.28 | loop fusion | flops 5677056 | bytes 3981352 | tf_op jit(solution)/shard_map/mul | solution.py:150
  69.0 3.2 %fusion.93 = f32[4,6,36,128]{3,0,2,1:T(4,128)} fusion(f32[4,6,36,128]{3,0,2,1:T(4,128)S(1)} %get-tuple-element.19, f32[4,6,18,128]{3,0,2,1:T(4,128)S(1)} %get-tuple-element.123, f32[4,6,18,128]{3,0,2,1:T(4,128)S(1)} %get-tuple-element.21, f32[4,14,36,128]{3,0,2,1:T(4,128)S(1)} %subtract_multiply_fusion, s32[]{:T(128)S(6)} %select_n.243, s32[]{:T(128)S(6)} %select_n.242, ...), kind=kLoop, calls=%fused_computation.193 | loop fusion | flops 2211840 | bytes 2805800 | tf_op jit(solution)/shard_map/mul | solution.py:317
  (102 shorter events, 3.5 us)
Async XLA Ops:
  0.6 1.9 %copy-start.3 = (f32[4,128]{1,0:T(4,128)S(1)}, f32[4,128]{1,0:T(4,128)}, u32[]{:S(2)}) copy-start(f32[4,128]{1,0:T(4,128)} %param.8) | copy-start | bytes 6148
  0.6 23.2 %copy-start.2 = (s32[4]{0:T(128)S(1)}, s32[4]{0:T(128)}, u32[]{:S(2)}) copy-start(s32[4]{0:T(128)} %param.12) | copy-start | bytes 52
  0.7 35.6 %copy-start.4 = (f32[2]{0:T(128)S(1)}, f32[2]{0:T(128)}, u32[]{:S(2)}) copy-start(f32[2]{0:T(128)} %param.13) | copy-start | bytes 28
  2.6 37.0 %collective-permute-start.1 = (f32[4,110,128]{2,0,1:T(4,128)S(1)}, f32[4,110,128]{2,0,1:T(4,128)S(1)}, u32[]{:S(2)}, u32[]{:S(2)}) collective-permute-start(f32[4,110,128]{2,0,1:T(4,128)S(1)} %get-tuple-element.119), channel_id=1, source_target_pairs={{0,2},{1,3},{2,4},{3,5},{4,6},{5,7},{6,8},{7,9},{8,10},{9,11},{10,... | collective-permute-start | bytes 675848 | tf_op jit(solution)/shard_map/ppermute | solution.py:30
  8.4 31.3 %collective-permute-start.2 = (f32[4,110,128]{2,0,1:T(4,128)S(1)}, f32[4,110,128]{2,0,1:T(4,128)S(1)}, u32[]{:S(2)}, u32[]{:S(2)}) collective-permute-start(f32[4,110,128]{2,0,1:T(4,128)S(1)} %get-tuple-element.119), channel_id=1, source_target_pairs={{0,1},{1,2},{2,3},{3,4},{4,5},{5,6},{6,7},{7,8},{8,9},{9,10},{10,1... | collective-permute-start | bytes 675848 | tf_op jit(solution)/shard_map/ppermute | solution.py:30
  11.0 28.7 %collective-permute-start.3 = (f32[4,110,128]{2,0,1:T(4,128)S(1)}, f32[4,110,128]{2,0,1:T(4,128)S(1)}, u32[]{:S(2)}, u32[]{:S(2)}) collective-permute-start(f32[4,110,128]{2,0,1:T(4,128)S(1)} %get-tuple-element.118), channel_id=1, source_target_pairs={{1,0},{2,1},{3,2},{4,3},{5,4},{6,5},{7,6},{8,7},{9,8},{10,9},{11,1... | collective-permute-start | bytes 675848 | tf_op jit(solution)/shard_map/ppermute | solution.py:30
  14.2 25.5 %collective-permute-start.4 = (f32[4,110,128]{2,0,1:T(4,128)S(1)}, f32[4,110,128]{2,0,1:T(4,128)S(1)}, u32[]{:S(2)}, u32[]{:S(2)}) collective-permute-start(f32[4,110,128]{2,0,1:T(4,128)S(1)} %get-tuple-element.118), channel_id=1, source_target_pairs={{2,0},{3,1},{4,2},{5,3},{6,4},{7,5},{8,6},{9,7},{10,8},{11,9},{12,... | collective-permute-start | bytes 675848 | tf_op jit(solution)/shard_map/ppermute | solution.py:30
  18.8 20.9 %collective-permute-start = (f32[4,128]{1,0:T(4,128)S(1)}, f32[4,128]{1,0:T(4,128)S(1)}, u32[]{:S(2)}, u32[]{:S(2)}) collective-permute-start(f32[4,128]{1,0:T(4,128)S(1)} %get-tuple-element.121), channel_id=1, source_target_pairs={{0,256},{64,320},{128,384},{192,448},{256,0},{320,64},{384,128},{4... | collective-permute-start | bytes 6152 | tf_op jit(solution)/shard_map/ppermute | solution.py:30
  39.7 9.6 %copy-start.1 = (f32[4,110,128]{2,0,1:T(4,128)}, f32[4,110,128]{2,0,1:T(4,128)S(1)}, u32[]{:S(2)}) copy-start(f32[4,110,128]{2,0,1:T(4,128)S(1)} %collective-permute-done.3) | copy-start | bytes 675844
  39.7 9.6 %copy-start = (f32[4,110,128]{2,0,1:T(4,128)}, f32[4,110,128]{2,0,1:T(4,128)S(1)}, u32[]{:S(2)}) copy-start(f32[4,110,128]{2,0,1:T(4,128)S(1)} %collective-permute-done.4) | copy-start | bytes 675844
  40.0 23.5 %collective-permute-start.5 = (f32[4,218,128]{2,0,1:T(4,128)S(1)}, f32[4,218,128]{2,0,1:T(4,128)S(1)}, u32[]{:S(2)}, u32[]{:S(2)}) collective-permute-start(f32[4,218,128]{2,0,1:T(4,128)S(1)} %pad_maximum_fusion.4), channel_id=1, source_target_pairs={{0,64},{64,128},{128,192},{192,256},{256,320},{320,384},{384,448},... | collective-permute-start | bytes 1339400 | tf_op jit(solution)/shard_map/ppermute | solution.py:30
  40.1 23.3 %collective-permute-start.6 = (f32[4,218,128]{2,0,1:T(4,128)S(1)}, f32[4,218,128]{2,0,1:T(4,128)S(1)}, u32[]{:S(2)}, u32[]{:S(2)}) collective-permute-start(f32[4,218,128]{2,0,1:T(4,128)S(1)} %pad_maximum_fusion.4), channel_id=1, source_target_pairs={{0,128},{64,192},{128,256},{192,320},{256,384},{320,448},{384,0},{... | collective-permute-start | bytes 1339400 | tf_op jit(solution)/shard_map/ppermute | solution.py:30
  42.6 21.1 %collective-permute-start.7 = (f32[4,218,128]{2,0,1:T(4,128)S(1)}, f32[4,218,128]{2,0,1:T(4,128)S(1)}, u32[]{:S(2)}, u32[]{:S(2)}) collective-permute-start(f32[4,218,128]{2,0,1:T(4,128)S(1)} %pad_maximum_fusion.4), channel_id=1, source_target_pairs={{0,448},{64,0},{128,64},{192,128},{256,192},{320,256},{384,320},{4... | collective-permute-start | bytes 1339400 | tf_op jit(solution)/shard_map/ppermute | solution.py:30
  45.2 18.1 %collective-permute-start.8 = (f32[4,218,128]{2,0,1:T(4,128)S(1)}, f32[4,218,128]{2,0,1:T(4,128)S(1)}, u32[]{:S(2)}, u32[]{:S(2)}) collective-permute-start(f32[4,218,128]{2,0,1:T(4,128)S(1)} %pad_maximum_fusion.4), channel_id=1, source_target_pairs={{0,384},{64,448},{128,0},{192,64},{256,128},{320,192},{384,256},{4... | collective-permute-start | bytes 1339400 | tf_op jit(solution)/shard_map/ppermute | solution.py:30
  55.6 0.9 %slice-start = ((f32[4,110,128]{2,0,1:T(4,128)}), f32[4,108,128]{2,0,1:T(4,128)S(1)}, s32[]{:S(2)}) async-start(f32[4,110,128]{2,0,1:T(4,128)} %copy-done), calls=%async_computation | async-start | bytes 442368 | tf_op jit(solution)/shard_map/slice | solution.py:273
  55.6 1.0 %slice-start.1 = ((f32[4,110,128]{2,0,1:T(4,128)}), f32[4,108,128]{2,0,1:T(4,128)S(1)}, s32[]{:S(2)}) async-start(f32[4,110,128]{2,0,1:T(4,128)} %copy-done.1), calls=%async_computation.1 | async-start | bytes 442368 | tf_op jit(solution)/shard_map/slice | solution.py:273
  63.8 0.7 copy-start.5
  63.8 0.7 copy-start.6

commit v13 on v12

--- a/solution.py
+++ b/solution.py
@@ -174,8 +174,8 @@
 
 def propagate(spectrum, speed, wet, cosines, sines, northward):
     step_ratio = sub_step / cell_size
-    east_speed = speed[:, :, None, :] * cosines[None, None, :, None]
-    north_speed = speed[:, :, None, :] * sines[None, None, :, None]
+    east_speed = speed[:, :, None, :] * cosines[None, None, :, None] * step_ratio
+    north_speed = speed[:, :, None, :] * sines[None, None, :, None] * step_ratio
     rows = spectrum.shape[0]
     for substep in range(SUBSTEPS):
         lo, hi = (substep, rows) if northward else (0, rows - substep)
@@ -185,11 +185,11 @@
         across = east_west(east_flux, cosines)
         if northward:
             spectrum = wet[lo + 1 : hi, None, None, :] * (
-                spectrum[1:] - step_ratio * (across[1:] + along)
+                spectrum[1:] - (across[1:] + along)
             )
         else:
             spectrum = wet[lo : hi - 1, None, None, :] * (
-                spectrum[:-1] - step_ratio * (across[:-1] + along)
+                spectrum[:-1] - (across[:-1] + along)
             )
     return spectrum
 

time: 72.8 us -> 72.7 us (level)
  no operation moved by 1% of the time
where the time goes in v13:
time: 72.7 us; the launch traced here: 72 us
  starting transfers between devices  29.3 us (40%)
  other arithmetic  20 us (28%)
  between operations  15.8 us (22%)
  local copies, waits for them, and re-layouts  6.85 us (9%)
    ppermute x9, starting transfers between devices, from_neighbour(): return lax.ppermute(block, axis, pairs)  29.3 us
    mul x16, other arithmetic, propagate(): east_flux = east_speed[lo:hi] * spectrum  7.65 us
    slice x16, local copies, waits for them, and re-layouts, east_west(): behind = jnp.concatenate([zeros, east_flux[..., :-1]], axis=-1)  3.96 us
    mul x1, other arithmetic, source_change(): coupling * (centre * centre * (coef_plus * upper + coef_minus * lower) -...  3.89 us
    mul x1, other arithmetic, body(): return (wet_four * (moved + increment), orbital)  3.17 us
  transfers between devices with their start and end apart: 9, of which 0 were waited for; matrix products, arithmetic and copies ran while one was open for 22% of the time, Pallas kernels for 0%

profile of v13, /device:TPU:272, one launch (start us, length us, event | category | flops | bytes accessed | tf_op | source)
XLA Modules:
  0.0 72.0 jit_solution(16089155735007930803)
XLA Ops:
  0.7 0.7 convert_bitcast_fusion
  1.4 1.1 %fusion.148 = (f32[4,6,128]{2,0,1:T(4,128)S(1)}, f32[4,6,36,128]{3,0,2,1:T(4,128)S(1)}) fusion(f32[4,6,36,128]{3,0,2,1:T(4,128)} %param.7, f32[4,128]{1,0:T(4,128)S(1)} %get-tuple-element.129), kind=kLoop, calls=%fused_computation.311 | loop fusion | flops 218112 | bytes 899072 | tf_op jit(solution)/shard_map/reduce_sum | solution.py:221
  2.6 5.7 %collective-permute-start.1 = (f32[4,110,128]{2,0,1:T(4,128)S(1)}, f32[4,110,128]{2,0,1:T(4,128)S(1)}, u32[]{:S(2)}, u32[]{:S(2)}) collective-permute-start(f32[4,110,128]{2,0,1:T(4,128)S(1)} %get-tuple-element.119), channel_id=1, source_target_pairs={{0,2},{1,3},{2,4},{3,5},{4,6},{5,7},{6,8},{7,9},{8,10},{9,11},{10,... | collective-permute-start | bytes 675848 | tf_op jit(solution)/shard_map/ppermute | solution.py:30
  8.4 2.6 %collective-permute-start.2 = (f32[4,110,128]{2,0,1:T(4,128)S(1)}, f32[4,110,128]{2,0,1:T(4,128)S(1)}, u32[]{:S(2)}, u32[]{:S(2)}) collective-permute-start(f32[4,110,128]{2,0,1:T(4,128)S(1)} %get-tuple-element.119), channel_id=1, source_target_pairs={{0,1},{1,2},{2,3},{3,4},{4,5},{5,6},{6,7},{7,8},{8,9},{9,10},{10,1... | collective-permute-start | bytes 675848 | tf_op jit(solution)/shard_map/ppermute | solution.py:30
  11.0 3.3 %collective-permute-start.3 = (f32[4,110,128]{2,0,1:T(4,128)S(1)}, f32[4,110,128]{2,0,1:T(4,128)S(1)}, u32[]{:S(2)}, u32[]{:S(2)}) collective-permute-start(f32[4,110,128]{2,0,1:T(4,128)S(1)} %get-tuple-element.118), channel_id=1, source_target_pairs={{1,0},{2,1},{3,2},{4,3},{5,4},{6,5},{7,6},{8,7},{9,8},{10,9},{11,1... | collective-permute-start | bytes 675848 | tf_op jit(solution)/shard_map/ppermute | solution.py:30
  14.2 4.4 %collective-permute-start.4 = (f32[4,110,128]{2,0,1:T(4,128)S(1)}, f32[4,110,128]{2,0,1:T(4,128)S(1)}, u32[]{:S(2)}, u32[]{:S(2)}) collective-permute-start(f32[4,110,128]{2,0,1:T(4,128)S(1)} %get-tuple-element.118), channel_id=1, source_target_pairs={{2,0},{3,1},{4,2},{5,3},{6,4},{7,5},{8,6},{9,7},{10,8},{11,9},{12,... | collective-permute-start | bytes 675848 | tf_op jit(solution)/shard_map/ppermute | solution.py:30
  18.8 4.9 %collective-permute-start = (f32[4,128]{1,0:T(4,128)S(1)}, f32[4,128]{1,0:T(4,128)S(1)}, u32[]{:S(2)}, u32[]{:S(2)}) collective-permute-start(f32[4,128]{1,0:T(4,128)S(1)} %get-tuple-element.121), channel_id=1, source_target_pairs={{0,256},{64,320},{128,384},{192,448},{256,0},{320,64},{384,128},{4... | collective-permute-start | bytes 6152 | tf_op jit(solution)/shard_map/ppermute | solution.py:30
  23.9 0.7 fusion.150
  36.3 0.6 fusion.149
  40.1 2.5 %collective-permute-start.6 = (f32[4,218,128]{2,0,1:T(4,128)S(1)}, f32[4,218,128]{2,0,1:T(4,128)S(1)}, u32[]{:S(2)}, u32[]{:S(2)}) collective-permute-start(f32[4,218,128]{2,0,1:T(4,128)S(1)} %pad_maximum_fusion.4), channel_id=1, source_target_pairs={{0,128},{64,192},{128,256},{192,320},{256,384},{320,448},{384,0},{... | collective-permute-start | bytes 1339400 | tf_op jit(solution)/shard_map/ppermute | solution.py:30
  42.6 2.7 %collective-permute-start.7 = (f32[4,218,128]{2,0,1:T(4,128)S(1)}, f32[4,218,128]{2,0,1:T(4,128)S(1)}, u32[]{:S(2)}, u32[]{:S(2)}) collective-permute-start(f32[4,218,128]{2,0,1:T(4,128)S(1)} %pad_maximum_fusion.4), channel_id=1, source_target_pairs={{0,448},{64,0},{128,64},{192,128},{256,192},{320,256},{384,320},{4... | collective-permute-start | bytes 1339400 | tf_op jit(solution)/shard_map/ppermute | solution.py:30
  45.2 3.3 %collective-permute-start.8 = (f32[4,218,128]{2,0,1:T(4,128)S(1)}, f32[4,218,128]{2,0,1:T(4,128)S(1)}, u32[]{:S(2)}, u32[]{:S(2)}) collective-permute-start(f32[4,218,128]{2,0,1:T(4,128)S(1)} %pad_maximum_fusion.4), channel_id=1, source_target_pairs={{0,384},{64,448},{128,0},{192,64},{256,128},{320,192},{384,256},{4... | collective-permute-start | bytes 1339400 | tf_op jit(solution)/shard_map/ppermute | solution.py:30
  48.6 0.2 add_multiply_fusion.4
  48.8 0.4 fusion.80
  49.3 0.3 fusion.134
  49.6 0.7 slice_multiply_fusion.11
  50.3 0.3 fusion.133
  50.7 0.7 slice_multiply_fusion.9
  51.6 0.3 fusion.132
  51.9 0.7 slice_multiply_fusion.7
  52.7 0.3 fusion.131
  53.0 0.5 slice_multiply_fusion.28
  53.6 0.2 fusion.142
  53.8 0.4 slice_multiply_fusion.26
  54.3 0.2 fusion.141
  54.5 0.4 slice_multiply_fusion.24
  54.9 0.2 fusion.140
  55.1 0.4 slice_multiply_fusion.22
  55.8 0.7 slice-done
  56.6 0.4 fusion.82
  57.0 0.3 fusion.138
  57.3 0.5 slice_multiply_fusion.5
  57.9 0.3 fusion.137
  58.3 0.5 slice_multiply_fusion.3
  59.0 0.3 fusion.136
  59.3 0.5 slice_multiply_fusion.1
  60.0 0.3 fusion.135
  60.3 0.3 slice_multiply_fusion.20
  60.7 0.2 fusion.146
  60.9 0.3 slice_multiply_fusion.18
  61.2 0.2 fusion.145
  61.4 0.3 slice_multiply_fusion.16
  61.8 0.2 fusion.144
  62.0 0.5 slice_multiply_fusion.14
  62.7 0.5 fusion.90
  64.4 0.6 multiply_add_fusion
  65.0 3.9 %subtract_multiply_fusion = f32[4,14,36,128]{3,0,2,1:T(4,128)S(1)} fusion(s32[]{:T(128)S(6)} %select_n.235, s32[]{:T(128)S(6)} %select_n.234, f32[4,22,36,128]{3,0,2,1:T(4,128)S(1)} %constant_dynamic-update-slice_fusion, s32[]{:T(128)S(6)} %select_n.232, s32[]{:T(128)S(6)} %select_n.231, s32[]{:T(128)S(6)} %select_n.230, s32[]{:T(128)S(6)} %select_n.228, ...), kind=kLoop, calls=%fused_computation.28 | loop fusion | flops 5677056 | bytes 3981352 | tf_op jit(solution)/shard_map/mul | solution.py:150
  68.9 3.2 %fusion.79 = f32[4,6,36,128]{3,0,2,1:T(4,128)} fusion(f32[4,6,36,128]{3,0,2,1:T(4,128)S(1)} %get-tuple-element.19, f32[4,6,18,128]{3,0,2,1:T(4,128)S(1)} %get-tuple-element.123, f32[4,6,18,128]{3,0,2,1:T(4,128)S(1)} %get-tuple-element.21, f32[4,14,36,128]{3,0,2,1:T(4,128)S(1)} %subtract_multiply_fusion, s32[]{:T(128)S(6)} %select_n.243, s32[]{:T(128)S(6)} %select_n.242, ...), kind=kLoop, calls=%fused_computation.179 | loop fusion | flops 2211840 | bytes 2805800 | tf_op jit(solution)/shard_map/mul | solution.py:317
  (102 shorter events, 3.5 us)
Async XLA Ops:
  0.6 1.9 %copy-start.3 = (f32[4,128]{1,0:T(4,128)S(1)}, f32[4,128]{1,0:T(4,128)}, u32[]{:S(2)}) copy-start(f32[4,128]{1,0:T(4,128)} %param.8) | copy-start | bytes 6148
  0.6 23.2 %copy-start.2 = (s32[4]{0:T(128)S(1)}, s32[4]{0:T(128)}, u32[]{:S(2)}) copy-start(s32[4]{0:T(128)} %param.12) | copy-start | bytes 52
  0.7 35.6 %copy-start.4 = (f32[2]{0:T(128)S(1)}, f32[2]{0:T(128)}, u32[]{:S(2)}) copy-start(f32[2]{0:T(128)} %param.13) | copy-start | bytes 28
  2.6 37.0 %collective-permute-start.1 = (f32[4,110,128]{2,0,1:T(4,128)S(1)}, f32[4,110,128]{2,0,1:T(4,128)S(1)}, u32[]{:S(2)}, u32[]{:S(2)}) collective-permute-start(f32[4,110,128]{2,0,1:T(4,128)S(1)} %get-tuple-element.119), channel_id=1, source_target_pairs={{0,2},{1,3},{2,4},{3,5},{4,6},{5,7},{6,8},{7,9},{8,10},{9,11},{10,... | collective-permute-start | bytes 675848 | tf_op jit(solution)/shard_map/ppermute | solution.py:30
  8.4 31.3 %collective-permute-start.2 = (f32[4,110,128]{2,0,1:T(4,128)S(1)}, f32[4,110,128]{2,0,1:T(4,128)S(1)}, u32[]{:S(2)}, u32[]{:S(2)}) collective-permute-start(f32[4,110,128]{2,0,1:T(4,128)S(1)} %get-tuple-element.119), channel_id=1, source_target_pairs={{0,1},{1,2},{2,3},{3,4},{4,5},{5,6},{6,7},{7,8},{8,9},{9,10},{10,1... | collective-permute-start | bytes 675848 | tf_op jit(solution)/shard_map/ppermute | solution.py:30
  11.0 28.7 %collective-permute-start.3 = (f32[4,110,128]{2,0,1:T(4,128)S(1)}, f32[4,110,128]{2,0,1:T(4,128)S(1)}, u32[]{:S(2)}, u32[]{:S(2)}) collective-permute-start(f32[4,110,128]{2,0,1:T(4,128)S(1)} %get-tuple-element.118), channel_id=1, source_target_pairs={{1,0},{2,1},{3,2},{4,3},{5,4},{6,5},{7,6},{8,7},{9,8},{10,9},{11,1... | collective-permute-start | bytes 675848 | tf_op jit(solution)/shard_map/ppermute | solution.py:30
  14.2 25.5 %collective-permute-start.4 = (f32[4,110,128]{2,0,1:T(4,128)S(1)}, f32[4,110,128]{2,0,1:T(4,128)S(1)}, u32[]{:S(2)}, u32[]{:S(2)}) collective-permute-start(f32[4,110,128]{2,0,1:T(4,128)S(1)} %get-tuple-element.118), channel_id=1, source_target_pairs={{2,0},{3,1},{4,2},{5,3},{6,4},{7,5},{8,6},{9,7},{10,8},{11,9},{12,... | collective-permute-start | bytes 675848 | tf_op jit(solution)/shard_map/ppermute | solution.py:30
  18.8 20.9 %collective-permute-start = (f32[4,128]{1,0:T(4,128)S(1)}, f32[4,128]{1,0:T(4,128)S(1)}, u32[]{:S(2)}, u32[]{:S(2)}) collective-permute-start(f32[4,128]{1,0:T(4,128)S(1)} %get-tuple-element.121), channel_id=1, source_target_pairs={{0,256},{64,320},{128,384},{192,448},{256,0},{320,64},{384,128},{4... | collective-permute-start | bytes 6152 | tf_op jit(solution)/shard_map/ppermute | solution.py:30
  39.7 9.6 %copy-start.1 = (f32[4,110,128]{2,0,1:T(4,128)}, f32[4,110,128]{2,0,1:T(4,128)S(1)}, u32[]{:S(2)}) copy-start(f32[4,110,128]{2,0,1:T(4,128)S(1)} %collective-permute-done.3) | copy-start | bytes 675844
  39.7 9.6 %copy-start = (f32[4,110,128]{2,0,1:T(4,128)}, f32[4,110,128]{2,0,1:T(4,128)S(1)}, u32[]{:S(2)}) copy-start(f32[4,110,128]{2,0,1:T(4,128)S(1)} %collective-permute-done.4) | copy-start | bytes 675844
  40.0 23.3 %collective-permute-start.5 = (f32[4,218,128]{2,0,1:T(4,128)S(1)}, f32[4,218,128]{2,0,1:T(4,128)S(1)}, u32[]{:S(2)}, u32[]{:S(2)}) collective-permute-start(f32[4,218,128]{2,0,1:T(4,128)S(1)} %pad_maximum_fusion.4), channel_id=1, source_target_pairs={{0,64},{64,128},{128,192},{192,256},{256,320},{320,384},{384,448},... | collective-permute-start | bytes 1339400 | tf_op jit(solution)/shard_map/ppermute | solution.py:30
  40.1 23.2 %collective-permute-start.6 = (f32[4,218,128]{2,0,1:T(4,128)S(1)}, f32[4,218,128]{2,0,1:T(4,128)S(1)}, u32[]{:S(2)}, u32[]{:S(2)}) collective-permute-start(f32[4,218,128]{2,0,1:T(4,128)S(1)} %pad_maximum_fusion.4), channel_id=1, source_target_pairs={{0,128},{64,192},{128,256},{192,320},{256,384},{320,448},{384,0},{... | collective-permute-start | bytes 1339400 | tf_op jit(solution)/shard_map/ppermute | solution.py:30
  42.6 21.0 %collective-permute-start.7 = (f32[4,218,128]{2,0,1:T(4,128)S(1)}, f32[4,218,128]{2,0,1:T(4,128)S(1)}, u32[]{:S(2)}, u32[]{:S(2)}) collective-permute-start(f32[4,218,128]{2,0,1:T(4,128)S(1)} %pad_maximum_fusion.4), channel_id=1, source_target_pairs={{0,448},{64,0},{128,64},{192,128},{256,192},{320,256},{384,320},{4... | collective-permute-start | bytes 1339400 | tf_op jit(solution)/shard_map/ppermute | solution.py:30
  45.2 18.0 %collective-permute-start.8 = (f32[4,218,128]{2,0,1:T(4,128)S(1)}, f32[4,218,128]{2,0,1:T(4,128)S(1)}, u32[]{:S(2)}, u32[]{:S(2)}) collective-permute-start(f32[4,218,128]{2,0,1:T(4,128)S(1)} %pad_maximum_fusion.4), channel_id=1, source_target_pairs={{0,384},{64,448},{128,0},{192,64},{256,128},{320,192},{384,256},{4... | collective-permute-start | bytes 1339400 | tf_op jit(solution)/shard_map/ppermute | solution.py:30
  55.5 0.9 %slice-start = ((f32[4,110,128]{2,0,1:T(4,128)}), f32[4,108,128]{2,0,1:T(4,128)S(1)}, s32[]{:S(2)}) async-start(f32[4,110,128]{2,0,1:T(4,128)} %copy-done), calls=%async_computation | async-start | bytes 442368 | tf_op jit(solution)/shard_map/slice | solution.py:273
  55.5 1.0 %slice-start.1 = ((f32[4,110,128]{2,0,1:T(4,128)}), f32[4,108,128]{2,0,1:T(4,128)S(1)}, s32[]{:S(2)}) async-start(f32[4,110,128]{2,0,1:T(4,128)} %copy-done.1), calls=%async_computation.1 | async-start | bytes 442368 | tf_op jit(solution)/shard_map/slice | solution.py:273
  63.7 0.7 copy-start.5
  63.7 0.7 copy-start.6

commit v14 on v13

--- a/solution.py
+++ b/solution.py
@@ -301,7 +301,8 @@
 
     extended = jnp.concatenate(low_bins + [masked] + high_bins, axis=1)
     change = source_change(extended, quad_offsets, quad_weights, freq_count)
-    increment = (masked + full_step * change) / damping[:, None, None, :] - masked
+    relief = 1.0 / damping
+    increment = (masked + full_step * change) * relief[:, None, None, :] - masked
 
     s_off = [k + 1 for k in range(len(above))]
     a_spec, a_speed, a_wet = unpack(above, s_off)

time: 72.7 us -> 72.7 us (level)
  no operation moved by 1% of the time
where the time goes in v14:
time: 72.7 us; the launch traced here: 72 us
  starting transfers between devices  29.3 us (40%)
  other arithmetic  20 us (28%)
  between operations  15.8 us (22%)
  local copies, waits for them, and re-layouts  6.85 us (9%)
    ppermute x9, starting transfers between devices, from_neighbour(): return lax.ppermute(block, axis, pairs)  29.3 us
    mul x16, other arithmetic, propagate(): east_flux = east_speed[lo:hi] * spectrum  7.65 us
    slice x16, local copies, waits for them, and re-layouts, east_west(): behind = jnp.concatenate([zeros, east_flux[..., :-1]], axis=-1)  3.96 us
    mul x1, other arithmetic, source_change(): coupling * (centre * centre * (coef_plus * upper + coef_minus * lower) -...  3.89 us
    mul x1, other arithmetic, body(): return (wet_four * (moved + increment), orbital)  3.17 us
  transfers between devices with their start and end apart: 9, of which 0 were waited for; matrix products, arithmetic and copies ran while one was open for 22% of the time, Pallas kernels for 0%

profile of v14, /device:TPU:272, one launch (start us, length us, event | category | flops | bytes accessed | tf_op | source)
XLA Modules:
  0.0 72.0 jit_solution(6214811180809538804)
XLA Ops:
  0.7 0.7 convert_bitcast_fusion
  1.4 1.1 %fusion.147 = (f32[4,6,128]{2,0,1:T(4,128)S(1)}, f32[4,6,36,128]{3,0,2,1:T(4,128)S(1)}) fusion(f32[4,6,36,128]{3,0,2,1:T(4,128)} %param.7, f32[4,128]{1,0:T(4,128)S(1)} %get-tuple-element.129), kind=kLoop, calls=%fused_computation.310 | loop fusion | flops 218112 | bytes 899072 | tf_op jit(solution)/shard_map/reduce_sum | solution.py:221
  2.6 5.7 %collective-permute-start.1 = (f32[4,110,128]{2,0,1:T(4,128)S(1)}, f32[4,110,128]{2,0,1:T(4,128)S(1)}, u32[]{:S(2)}, u32[]{:S(2)}) collective-permute-start(f32[4,110,128]{2,0,1:T(4,128)S(1)} %get-tuple-element.119), channel_id=1, source_target_pairs={{0,2},{1,3},{2,4},{3,5},{4,6},{5,7},{6,8},{7,9},{8,10},{9,11},{10,... | collective-permute-start | bytes 675848 | tf_op jit(solution)/shard_map/ppermute | solution.py:30
  8.4 2.6 %collective-permute-start.2 = (f32[4,110,128]{2,0,1:T(4,128)S(1)}, f32[4,110,128]{2,0,1:T(4,128)S(1)}, u32[]{:S(2)}, u32[]{:S(2)}) collective-permute-start(f32[4,110,128]{2,0,1:T(4,128)S(1)} %get-tuple-element.119), channel_id=1, source_target_pairs={{0,1},{1,2},{2,3},{3,4},{4,5},{5,6},{6,7},{7,8},{8,9},{9,10},{10,1... | collective-permute-start | bytes 675848 | tf_op jit(solution)/shard_map/ppermute | solution.py:30
  11.0 3.3 %collective-permute-start.3 = (f32[4,110,128]{2,0,1:T(4,128)S(1)}, f32[4,110,128]{2,0,1:T(4,128)S(1)}, u32[]{:S(2)}, u32[]{:S(2)}) collective-permute-start(f32[4,110,128]{2,0,1:T(4,128)S(1)} %get-tuple-element.118), channel_id=1, source_target_pairs={{1,0},{2,1},{3,2},{4,3},{5,4},{6,5},{7,6},{8,7},{9,8},{10,9},{11,1... | collective-permute-start | bytes 675848 | tf_op jit(solution)/shard_map/ppermute | solution.py:30
  14.2 4.4 %collective-permute-start.4 = (f32[4,110,128]{2,0,1:T(4,128)S(1)}, f32[4,110,128]{2,0,1:T(4,128)S(1)}, u32[]{:S(2)}, u32[]{:S(2)}) collective-permute-start(f32[4,110,128]{2,0,1:T(4,128)S(1)} %get-tuple-element.118), channel_id=1, source_target_pairs={{2,0},{3,1},{4,2},{5,3},{6,4},{7,5},{8,6},{9,7},{10,8},{11,9},{12,... | collective-permute-start | bytes 675848 | tf_op jit(solution)/shard_map/ppermute | solution.py:30
  18.8 4.9 %collective-permute-start = (f32[4,128]{1,0:T(4,128)S(1)}, f32[4,128]{1,0:T(4,128)S(1)}, u32[]{:S(2)}, u32[]{:S(2)}) collective-permute-start(f32[4,128]{1,0:T(4,128)S(1)} %get-tuple-element.121), channel_id=1, source_target_pairs={{0,256},{64,320},{128,384},{192,448},{256,0},{320,64},{384,128},{4... | collective-permute-start | bytes 6152 | tf_op jit(solution)/shard_map/ppermute | solution.py:30
  23.9 0.7 fusion.149
  36.3 0.6 fusion.148
  40.1 2.5 %collective-permute-start.6 = (f32[4,218,128]{2,0,1:T(4,128)S(1)}, f32[4,218,128]{2,0,1:T(4,128)S(1)}, u32[]{:S(2)}, u32[]{:S(2)}) collective-permute-start(f32[4,218,128]{2,0,1:T(4,128)S(1)} %pad_maximum_fusion.4), channel_id=1, source_target_pairs={{0,128},{64,192},{128,256},{192,320},{256,384},{320,448},{384,0},{... | collective-permute-start | bytes 1339400 | tf_op jit(solution)/shard_map/ppermute | solution.py:30
  42.6 2.7 %collective-permute-start.7 = (f32[4,218,128]{2,0,1:T(4,128)S(1)}, f32[4,218,128]{2,0,1:T(4,128)S(1)}, u32[]{:S(2)}, u32[]{:S(2)}) collective-permute-start(f32[4,218,128]{2,0,1:T(4,128)S(1)} %pad_maximum_fusion.4), channel_id=1, source_target_pairs={{0,448},{64,0},{128,64},{192,128},{256,192},{320,256},{384,320},{4... | collective-permute-start | bytes 1339400 | tf_op jit(solution)/shard_map/ppermute | solution.py:30
  45.2 3.3 %collective-permute-start.8 = (f32[4,218,128]{2,0,1:T(4,128)S(1)}, f32[4,218,128]{2,0,1:T(4,128)S(1)}, u32[]{:S(2)}, u32[]{:S(2)}) collective-permute-start(f32[4,218,128]{2,0,1:T(4,128)S(1)} %pad_maximum_fusion.4), channel_id=1, source_target_pairs={{0,384},{64,448},{128,0},{192,64},{256,128},{320,192},{384,256},{4... | collective-permute-start | bytes 1339400 | tf_op jit(solution)/shard_map/ppermute | solution.py:30
  48.6 0.2 add_multiply_fusion.4
  48.8 0.4 fusion.79
  49.3 0.3 fusion.133
  49.6 0.7 slice_multiply_fusion.11
  50.3 0.3 fusion.132
  50.7 0.7 slice_multiply_fusion.9
  51.6 0.3 fusion.131
  51.9 0.7 slice_multiply_fusion.7
  52.7 0.3 fusion.130
  53.0 0.5 slice_multiply_fusion.28
  53.6 0.2 fusion.141
  53.8 0.4 slice_multiply_fusion.26
  54.3 0.2 fusion.140
  54.5 0.4 slice_multiply_fusion.24
  54.9 0.2 fusion.139
  55.1 0.4 slice_multiply_fusion.22
  55.8 0.7 slice-done
  56.6 0.4 fusion.81
  57.0 0.3 fusion.137
  57.3 0.5 slice_multiply_fusion.5
  57.9 0.3 fusion.136
  58.3 0.5 slice_multiply_fusion.3
  59.0 0.3 fusion.135
  59.3 0.5 slice_multiply_fusion.1
  60.0 0.3 fusion.134
  60.3 0.3 slice_multiply_fusion.20
  60.7 0.2 fusion.145
  60.9 0.3 slice_multiply_fusion.18
  61.2 0.2 fusion.144
  61.4 0.3 slice_multiply_fusion.16
  61.8 0.2 fusion.143
  62.0 0.5 slice_multiply_fusion.14
  62.7 0.5 fusion.89
  64.4 0.6 add_divide_fusion
  65.0 3.9 %subtract_multiply_fusion = f32[4,14,36,128]{3,0,2,1:T(4,128)S(1)} fusion(s32[]{:T(128)S(6)} %select_n.235, s32[]{:T(128)S(6)} %select_n.234, f32[4,22,36,128]{3,0,2,1:T(4,128)S(1)} %constant_dynamic-update-slice_fusion, s32[]{:T(128)S(6)} %select_n.232, s32[]{:T(128)S(6)} %select_n.231, s32[]{:T(128)S(6)} %select_n.230, s32[]{:T(128)S(6)} %select_n.228, ...), kind=kLoop, calls=%fused_computation.28 | loop fusion | flops 5677056 | bytes 3981352 | tf_op jit(solution)/shard_map/mul | solution.py:150
  68.9 3.2 %fusion.78 = f32[4,6,36,128]{3,0,2,1:T(4,128)} fusion(f32[4,6,18,128]{3,0,2,1:T(4,128)S(1)} %get-tuple-element.123, f32[4,6,18,128]{3,0,2,1:T(4,128)S(1)} %get-tuple-element.21, f32[4,6,36,128]{3,0,2,1:T(4,128)S(1)} %get-tuple-element.19, f32[4,14,36,128]{3,0,2,1:T(4,128)S(1)} %subtract_multiply_fusion, s32[]{:T(128)S(6)} %select_n.243, s32[]{:T(128)S(6)} %select_n.242, ...), kind=kLoop, calls=%fused_computation.178 | loop fusion | flops 2211840 | bytes 2805800 | tf_op jit(solution)/shard_map/mul | solution.py:318
  (102 shorter events, 3.5 us)
Async XLA Ops:
  0.6 1.9 %copy-start.3 = (f32[4,128]{1,0:T(4,128)S(1)}, f32[4,128]{1,0:T(4,128)}, u32[]{:S(2)}) copy-start(f32[4,128]{1,0:T(4,128)} %param.8) | copy-start | bytes 6148
  0.6 23.2 %copy-start.2 = (s32[4]{0:T(128)S(1)}, s32[4]{0:T(128)}, u32[]{:S(2)}) copy-start(s32[4]{0:T(128)} %param.12) | copy-start | bytes 52
  0.7 35.6 %copy-start.4 = (f32[2]{0:T(128)S(1)}, f32[2]{0:T(128)}, u32[]{:S(2)}) copy-start(f32[2]{0:T(128)} %param.13) | copy-start | bytes 28
  2.6 37.0 %collective-permute-start.1 = (f32[4,110,128]{2,0,1:T(4,128)S(1)}, f32[4,110,128]{2,0,1:T(4,128)S(1)}, u32[]{:S(2)}, u32[]{:S(2)}) collective-permute-start(f32[4,110,128]{2,0,1:T(4,128)S(1)} %get-tuple-element.119), channel_id=1, source_target_pairs={{0,2},{1,3},{2,4},{3,5},{4,6},{5,7},{6,8},{7,9},{8,10},{9,11},{10,... | collective-permute-start | bytes 675848 | tf_op jit(solution)/shard_map/ppermute | solution.py:30
  8.4 31.3 %collective-permute-start.2 = (f32[4,110,128]{2,0,1:T(4,128)S(1)}, f32[4,110,128]{2,0,1:T(4,128)S(1)}, u32[]{:S(2)}, u32[]{:S(2)}) collective-permute-start(f32[4,110,128]{2,0,1:T(4,128)S(1)} %get-tuple-element.119), channel_id=1, source_target_pairs={{0,1},{1,2},{2,3},{3,4},{4,5},{5,6},{6,7},{7,8},{8,9},{9,10},{10,1... | collective-permute-start | bytes 675848 | tf_op jit(solution)/shard_map/ppermute | solution.py:30
  11.0 28.7 %collective-permute-start.3 = (f32[4,110,128]{2,0,1:T(4,128)S(1)}, f32[4,110,128]{2,0,1:T(4,128)S(1)}, u32[]{:S(2)}, u32[]{:S(2)}) collective-permute-start(f32[4,110,128]{2,0,1:T(4,128)S(1)} %get-tuple-element.118), channel_id=1, source_target_pairs={{1,0},{2,1},{3,2},{4,3},{5,4},{6,5},{7,6},{8,7},{9,8},{10,9},{11,1... | collective-permute-start | bytes 675848 | tf_op jit(solution)/shard_map/ppermute | solution.py:30
  14.2 25.5 %collective-permute-start.4 = (f32[4,110,128]{2,0,1:T(4,128)S(1)}, f32[4,110,128]{2,0,1:T(4,128)S(1)}, u32[]{:S(2)}, u32[]{:S(2)}) collective-permute-start(f32[4,110,128]{2,0,1:T(4,128)S(1)} %get-tuple-element.118), channel_id=1, source_target_pairs={{2,0},{3,1},{4,2},{5,3},{6,4},{7,5},{8,6},{9,7},{10,8},{11,9},{12,... | collective-permute-start | bytes 675848 | tf_op jit(solution)/shard_map/ppermute | solution.py:30
  18.8 20.9 %collective-permute-start = (f32[4,128]{1,0:T(4,128)S(1)}, f32[4,128]{1,0:T(4,128)S(1)}, u32[]{:S(2)}, u32[]{:S(2)}) collective-permute-start(f32[4,128]{1,0:T(4,128)S(1)} %get-tuple-element.121), channel_id=1, source_target_pairs={{0,256},{64,320},{128,384},{192,448},{256,0},{320,64},{384,128},{4... | collective-permute-start | bytes 6152 | tf_op jit(solution)/shard_map/ppermute | solution.py:30
  39.7 9.6 %copy-start.1 = (f32[4,110,128]{2,0,1:T(4,128)}, f32[4,110,128]{2,0,1:T(4,128)S(1)}, u32[]{:S(2)}) copy-start(f32[4,110,128]{2,0,1:T(4,128)S(1)} %collective-permute-done.3) | copy-start | bytes 675844
  39.7 9.6 %copy-start = (f32[4,110,128]{2,0,1:T(4,128)}, f32[4,110,128]{2,0,1:T(4,128)S(1)}, u32[]{:S(2)}) copy-start(f32[4,110,128]{2,0,1:T(4,128)S(1)} %collective-permute-done.4) | copy-start | bytes 675844
  40.0 23.3 %collective-permute-start.5 = (f32[4,218,128]{2,0,1:T(4,128)S(1)}, f32[4,218,128]{2,0,1:T(4,128)S(1)}, u32[]{:S(2)}, u32[]{:S(2)}) collective-permute-start(f32[4,218,128]{2,0,1:T(4,128)S(1)} %pad_maximum_fusion.4), channel_id=1, source_target_pairs={{0,64},{64,128},{128,192},{192,256},{256,320},{320,384},{384,448},... | collective-permute-start | bytes 1339400 | tf_op jit(solution)/shard_map/ppermute | solution.py:30
  40.1 23.2 %collective-permute-start.6 = (f32[4,218,128]{2,0,1:T(4,128)S(1)}, f32[4,218,128]{2,0,1:T(4,128)S(1)}, u32[]{:S(2)}, u32[]{:S(2)}) collective-permute-start(f32[4,218,128]{2,0,1:T(4,128)S(1)} %pad_maximum_fusion.4), channel_id=1, source_target_pairs={{0,128},{64,192},{128,256},{192,320},{256,384},{320,448},{384,0},{... | collective-permute-start | bytes 1339400 | tf_op jit(solution)/shard_map/ppermute | solution.py:30
  42.6 21.0 %collective-permute-start.7 = (f32[4,218,128]{2,0,1:T(4,128)S(1)}, f32[4,218,128]{2,0,1:T(4,128)S(1)}, u32[]{:S(2)}, u32[]{:S(2)}) collective-permute-start(f32[4,218,128]{2,0,1:T(4,128)S(1)} %pad_maximum_fusion.4), channel_id=1, source_target_pairs={{0,448},{64,0},{128,64},{192,128},{256,192},{320,256},{384,320},{4... | collective-permute-start | bytes 1339400 | tf_op jit(solution)/shard_map/ppermute | solution.py:30
  45.2 18.0 %collective-permute-start.8 = (f32[4,218,128]{2,0,1:T(4,128)S(1)}, f32[4,218,128]{2,0,1:T(4,128)S(1)}, u32[]{:S(2)}, u32[]{:S(2)}) collective-permute-start(f32[4,218,128]{2,0,1:T(4,128)S(1)} %pad_maximum_fusion.4), channel_id=1, source_target_pairs={{0,384},{64,448},{128,0},{192,64},{256,128},{320,192},{384,256},{4... | collective-permute-start | bytes 1339400 | tf_op jit(solution)/shard_map/ppermute | solution.py:30
  55.5 0.9 %slice-start = ((f32[4,110,128]{2,0,1:T(4,128)}), f32[4,108,128]{2,0,1:T(4,128)S(1)}, s32[]{:S(2)}) async-start(f32[4,110,128]{2,0,1:T(4,128)} %copy-done), calls=%async_computation | async-start | bytes 442368 | tf_op jit(solution)/shard_map/slice | solution.py:273
  55.5 1.0 %slice-start.1 = ((f32[4,110,128]{2,0,1:T(4,128)}), f32[4,108,128]{2,0,1:T(4,128)S(1)}, s32[]{:S(2)}) async-start(f32[4,110,128]{2,0,1:T(4,128)} %copy-done.1), calls=%async_computation.1 | async-start | bytes 442368 | tf_op jit(solution)/shard_map/slice | solution.py:273
  63.7 0.7 copy-start.5
  63.7 0.7 copy-start.6

commit v15 on v13

--- a/solution.py
+++ b/solution.py
@@ -2,6 +2,7 @@
 
 import jax
 import jax.numpy as jnp
+import numpy as np
 from jax import lax
 from jax.sharding import PartitionSpec as P
 
@@ -172,7 +173,23 @@
     return jnp.where(east_going, east_flux - behind, ahead - east_flux)
 
 
-def propagate(spectrum, speed, wet, cosines, sines, northward):
+def upwind_across(east_flux, east_static):
+    parts = []
+    start = 0
+    for stop in range(1, len(east_static) + 1):
+        if stop < len(east_static) and east_static[stop] == east_static[start]:
+            continue
+        flux = east_flux[:, :, start:stop]
+        zeros = jnp.zeros_like(flux[..., :1])
+        if east_static[start]:
+            parts.append(flux - jnp.concatenate([zeros, flux[..., :-1]], axis=-1))
+        else:
+            parts.append(jnp.concatenate([flux[..., 1:], zeros], axis=-1) - flux)
+        start = stop
+    return jnp.concatenate(parts, axis=2) if len(parts) > 1 else parts[0]
+
+
+def propagate(spectrum, speed, wet, cosines, sines, northward, east_static):
     step_ratio = sub_step / cell_size
     east_speed = speed[:, :, None, :] * cosines[None, None, :, None] * step_ratio
     north_speed = speed[:, :, None, :] * sines[None, None, :, None] * step_ratio
@@ -182,7 +199,7 @@
         east_flux = east_speed[lo:hi] * spectrum
         north_flux = north_speed[lo:hi] * spectrum
         along = north_flux[1:] - north_flux[:-1]
-        across = east_west(east_flux, cosines)
+        across = upwind_across(east_flux, east_static)
         if northward:
             spectrum = wet[lo + 1 : hi, None, None, :] * (
                 spectrum[1:] - (across[1:] + along)
@@ -205,6 +222,7 @@
     radian_freq = 2.0 * math.pi * base_freq * jnp.power(freq_ratio, bin_index)
     half = dir_count // 2
     cosines, sines = angles_of(dir_count)
+    east_static = np.cos((np.arange(dir_count) + 0.5) * (2.0 * math.pi / dir_count)) > 0.0
 
     fields = jnp.stack([wet_field, water_depth], axis=1)
     flat = freq_count * half
@@ -284,6 +302,7 @@
         cosines[:half],
         sines[:half],
         True,
+        east_static[:half],
     )
     arrays = [(p[1], p[2]) for p in low + high]
     north, arrays = lax.optimization_barrier((north, arrays))
@@ -312,6 +331,7 @@
         cosines[half:],
         sines[half:],
         False,
+        east_static[half:],
     )
     moved = jnp.concatenate([north, south], axis=2)
     return (wet_four * (moved + increment), orbital)

time: 72.7 us -> 71.3 us (0.981)
  the two profiles are of different devices: /device:TPU:272 before, /device:TPU:278 now
where the time goes in v15:
time: 71.3 us; the launch traced here: 70.7 us
  starting transfers between devices  26.6 us (37%)
  other arithmetic  19 us (27%)
  between operations  16.2 us (23%)
  local copies, waits for them, and re-layouts  5.32 us (7%)
  waiting for transfers between devices  3.54 us (5%)
    ppermute x9, starting transfers between devices, from_neighbour(): return lax.ppermute(block, axis, pairs)  26.6 us
    mul x16, other arithmetic, propagate(): east_flux = east_speed[lo:hi] * spectrum  4.37 us
    mul x1, other arithmetic, source_change(): coupling * (centre * centre * (coef_plus * upper + coef_minus * lower) -...  4.01 us
    ppermute x9, waiting for transfers between devices, from_neighbour(): return lax.ppermute(block, axis, pairs)  3.54 us
    mul x1, other arithmetic, body(): return (wet_four * (moved + increment), orbital)  3.1 us
  transfers between devices with their start and end apart: 9, of which 1 were waited for; matrix products, arithmetic and copies ran while one was open for 18% of the time, Pallas kernels for 0%

profile of v15, /device:TPU:278, one launch (start us, length us, event | category | flops | bytes accessed | tf_op | source)
XLA Modules:
  0.0 70.7 jit_solution(1320109649420659508)
XLA Ops:
  0.7 0.7 convert_bitcast_fusion
  1.4 1.1 %fusion.132 = (f32[4,6,128]{2,0,1:T(4,128)S(1)}, f32[4,6,36,128]{3,0,2,1:T(4,128)S(1)}) fusion(f32[4,6,36,128]{3,0,2,1:T(4,128)} %param.7, f32[4,128]{1,0:T(4,128)S(1)} %get-tuple-element.161), kind=kLoop, calls=%fused_computation.309 | loop fusion | flops 218112 | bytes 899072 | tf_op jit(solution)/shard_map/reduce_sum | solution.py:239
  2.6 5.7 %collective-permute-start.1 = (f32[4,110,128]{2,0,1:T(4,128)S(1)}, f32[4,110,128]{2,0,1:T(4,128)S(1)}, u32[]{:S(2)}, u32[]{:S(2)}) collective-permute-start(f32[4,110,128]{2,0,1:T(4,128)S(1)} %get-tuple-element.151), channel_id=1, source_target_pairs={{0,2},{1,3},{2,4},{3,5},{4,6},{5,7},{6,8},{7,9},{8,10},{9,11},{10,... | collective-permute-start | bytes 675848 | tf_op jit(solution)/shard_map/ppermute | solution.py:31
  8.4 2.6 %collective-permute-start.2 = (f32[4,110,128]{2,0,1:T(4,128)S(1)}, f32[4,110,128]{2,0,1:T(4,128)S(1)}, u32[]{:S(2)}, u32[]{:S(2)}) collective-permute-start(f32[4,110,128]{2,0,1:T(4,128)S(1)} %get-tuple-element.151), channel_id=1, source_target_pairs={{0,1},{1,2},{2,3},{3,4},{4,5},{5,6},{6,7},{7,8},{8,9},{9,10},{10,1... | collective-permute-start | bytes 675848 | tf_op jit(solution)/shard_map/ppermute | solution.py:31
  11.0 3.3 %collective-permute-start.3 = (f32[4,110,128]{2,0,1:T(4,128)S(1)}, f32[4,110,128]{2,0,1:T(4,128)S(1)}, u32[]{:S(2)}, u32[]{:S(2)}) collective-permute-start(f32[4,110,128]{2,0,1:T(4,128)S(1)} %get-tuple-element.150), channel_id=1, source_target_pairs={{1,0},{2,1},{3,2},{4,3},{5,4},{6,5},{7,6},{8,7},{9,8},{10,9},{11,1... | collective-permute-start | bytes 675848 | tf_op jit(solution)/shard_map/ppermute | solution.py:31
  14.2 4.4 %collective-permute-start.4 = (f32[4,110,128]{2,0,1:T(4,128)S(1)}, f32[4,110,128]{2,0,1:T(4,128)S(1)}, u32[]{:S(2)}, u32[]{:S(2)}) collective-permute-start(f32[4,110,128]{2,0,1:T(4,128)S(1)} %get-tuple-element.150), channel_id=1, source_target_pairs={{2,0},{3,1},{4,2},{5,3},{6,4},{7,5},{8,6},{9,7},{10,8},{11,9},{12,... | collective-permute-start | bytes 675848 | tf_op jit(solution)/shard_map/ppermute | solution.py:31
  18.8 3.3 %collective-permute-start = (f32[4,128]{1,0:T(4,128)S(1)}, f32[4,128]{1,0:T(4,128)S(1)}, u32[]{:S(2)}, u32[]{:S(2)}) collective-permute-start(f32[4,128]{1,0:T(4,128)S(1)} %get-tuple-element.153), channel_id=1, source_target_pairs={{0,256},{64,320},{128,384},{192,448},{256,0},{320,64},{384,128},{4... | collective-permute-start | bytes 6152 | tf_op jit(solution)/shard_map/ppermute | solution.py:31
  22.2 0.7 fusion.134
  34.9 0.7 fusion.133
  38.7 4.0 %collective-permute-start.6 = (f32[4,218,128]{2,0,1:T(4,128)S(1)}, f32[4,218,128]{2,0,1:T(4,128)S(1)}, u32[]{:S(2)}, u32[]{:S(2)}) collective-permute-start(f32[4,218,128]{2,0,1:T(4,128)S(1)} %pad_maximum_fusion.10), channel_id=1, source_target_pairs={{0,128},{64,192},{128,256},{192,320},{256,384},{320,448},{384,0},{... | collective-permute-start | bytes 1339400 | tf_op jit(solution)/shard_map/ppermute | solution.py:31
  42.7 1.5 %collective-permute-start.7 = (f32[4,218,128]{2,0,1:T(4,128)S(1)}, f32[4,218,128]{2,0,1:T(4,128)S(1)}, u32[]{:S(2)}, u32[]{:S(2)}) collective-permute-start(f32[4,218,128]{2,0,1:T(4,128)S(1)} %pad_maximum_fusion.10), channel_id=1, source_target_pairs={{0,448},{64,0},{128,64},{192,128},{256,192},{320,256},{384,320},{4... | collective-permute-start | bytes 1339400 | tf_op jit(solution)/shard_map/ppermute | solution.py:31
  44.2 1.9 %collective-permute-start.8 = (f32[4,218,128]{2,0,1:T(4,128)S(1)}, f32[4,218,128]{2,0,1:T(4,128)S(1)}, u32[]{:S(2)}, u32[]{:S(2)}) collective-permute-start(f32[4,218,128]{2,0,1:T(4,128)S(1)} %pad_maximum_fusion.10), channel_id=1, source_target_pairs={{0,384},{64,448},{128,0},{192,64},{256,128},{320,192},{384,256},{4... | collective-permute-start | bytes 1339400 | tf_op jit(solution)/shard_map/ppermute | solution.py:31
  46.1 0.2 add_multiply_fusion.4
  46.3 0.4 fusion.66
  46.8 0.2 fusion.118
  47.0 0.2 slice_subtract_fusion.29
  47.2 0.4 slice_multiply_fusion.11
  47.6 0.2 fusion.117
  47.9 0.2 slice_subtract_fusion.27
  48.1 0.4 slice_multiply_fusion.9
  48.6 0.2 fusion.116
  48.8 0.2 slice_subtract_fusion.25
  49.0 0.4 slice_multiply_fusion.7
  49.6 0.2 fusion.115
  49.7 0.2 slice_subtract_fusion.23
  49.9 0.3 slice_multiply_fusion.28
  50.5 0.2 slice_multiply_fusion.26
  51.1 0.2 slice_multiply_fusion.24
  51.7 0.2 slice_multiply_fusion.22
  52.1 0.7 %slice-done = f32[4,108,128]{2,0,1:T(4,128)S(1)} async-done(((f32[4,110,128]{2,0,1:T(4,128)}), f32[4,108,128]{2,0,1:T(4,128)S(1)}, s32[]{:S(2)}) %slice-start) | async-done | bytes 221208 | tf_op jit(solution)/shard_map/slice | solution.py:291
  52.9 0.4 fusion.68
  53.4 0.2 fusion.122
  53.6 0.2 slice_subtract_fusion.17
  53.8 0.3 slice_multiply_fusion.5
  54.0 0.2 fusion.121
  54.3 0.2 slice_subtract_fusion.15
  54.5 0.3 slice_multiply_fusion.3
  54.9 0.2 fusion.120
  55.1 0.2 slice_subtract_fusion.13
  55.3 0.3 slice_multiply_fusion.1
  55.7 0.2 fusion.119
  55.9 0.2 slice_subtract_fusion.11
  58.1 0.3 fusion.75
  58.3 3.5 %collective-permute-done.8 = f32[4,218,128]{2,0,1:T(4,128)S(1)} collective-permute-done((f32[4,218,128]{2,0,1:T(4,128)S(1)}, f32[4,218,128]{2,0,1:T(4,128)S(1)}, u32[]{:S(2)}, u32[]{:S(2)}) %collective-permute-start.8) | collective-permute-done | bytes 446496 | tf_op jit(solution)/shard_map/ppermute | solution.py:31
  62.8 0.2 copy-done.5
  63.0 0.6 multiply_add_fusion
  63.6 4.0 %subtract_multiply_fusion = f32[4,14,36,128]{3,0,2,1:T(4,128)S(1)} fusion(s32[]{:T(128)S(6)} %select_n.163, s32[]{:T(128)S(6)} %select_n.162, f32[4,22,36,128]{3,0,2,1:T(4,128)S(1)} %constant_dynamic-update-slice_fusion, s32[]{:T(128)S(6)} %select_n.160, s32[]{:T(128)S(6)} %select_n.159, s32[]{:T(128)S(6)} %select_n.158, s32[]{:T(128)S(6)} %select_n.156, ...), kind=kLoop, calls=%fused_computation.28 | loop fusion | flops 5677056 | bytes 3981352 | tf_op jit(solution)/shard_map/mul | solution.py:151
  67.6 3.1 %fusion.65 = f32[4,6,36,128]{3,0,2,1:T(4,128)} fusion(f32[4,6,36,128]{3,0,2,1:T(4,128)S(1)} %get-tuple-element.19, f32[4,6,18,128]{3,0,2,1:T(4,128)S(1)} %get-tuple-element.155, f32[4,6,18,128]{3,0,2,1:T(4,128)S(1)} %get-tuple-element.21, f32[4,14,36,128]{3,0,2,1:T(4,128)S(1)} %subtract_multiply_fusion, s32[]{:T(128)S(6)} %select_n.171, s32[]{:T(128)S(6)} %select_n.170, ...), kind=kLoop, calls=%fused_computation.167 | loop fusion | flops 2211840 | bytes 2805800 | tf_op jit(solution)/shard_map/mul | solution.py:337
  (117 shorter events, 5.4 us)
Async XLA Ops:
  0.6 1.9 %copy-start.3 = (f32[4,128]{1,0:T(4,128)S(1)}, f32[4,128]{1,0:T(4,128)}, u32[]{:S(2)}) copy-start(f32[4,128]{1,0:T(4,128)} %param.8) | copy-start | bytes 6148
  0.6 21.6 %copy-start.2 = (s32[4]{0:T(128)S(1)}, s32[4]{0:T(128)}, u32[]{:S(2)}) copy-start(s32[4]{0:T(128)} %param.12) | copy-start | bytes 52
  0.7 34.2 %copy-start.4 = (f32[2]{0:T(128)S(1)}, f32[2]{0:T(128)}, u32[]{:S(2)}) copy-start(f32[2]{0:T(128)} %param.13) | copy-start | bytes 28
  2.6 35.6 %collective-permute-start.1 = (f32[4,110,128]{2,0,1:T(4,128)S(1)}, f32[4,110,128]{2,0,1:T(4,128)S(1)}, u32[]{:S(2)}, u32[]{:S(2)}) collective-permute-start(f32[4,110,128]{2,0,1:T(4,128)S(1)} %get-tuple-element.151), channel_id=1, source_target_pairs={{0,2},{1,3},{2,4},{3,5},{4,6},{5,7},{6,8},{7,9},{8,10},{9,11},{10,... | collective-permute-start | bytes 675848 | tf_op jit(solution)/shard_map/ppermute | solution.py:31
  8.4 29.9 %collective-permute-start.2 = (f32[4,110,128]{2,0,1:T(4,128)S(1)}, f32[4,110,128]{2,0,1:T(4,128)S(1)}, u32[]{:S(2)}, u32[]{:S(2)}) collective-permute-start(f32[4,110,128]{2,0,1:T(4,128)S(1)} %get-tuple-element.151), channel_id=1, source_target_pairs={{0,1},{1,2},{2,3},{3,4},{4,5},{5,6},{6,7},{7,8},{8,9},{9,10},{10,1... | collective-permute-start | bytes 675848 | tf_op jit(solution)/shard_map/ppermute | solution.py:31
  11.0 27.4 %collective-permute-start.3 = (f32[4,110,128]{2,0,1:T(4,128)S(1)}, f32[4,110,128]{2,0,1:T(4,128)S(1)}, u32[]{:S(2)}, u32[]{:S(2)}) collective-permute-start(f32[4,110,128]{2,0,1:T(4,128)S(1)} %get-tuple-element.150), channel_id=1, source_target_pairs={{1,0},{2,1},{3,2},{4,3},{5,4},{6,5},{7,6},{8,7},{9,8},{10,9},{11,1... | collective-permute-start | bytes 675848 | tf_op jit(solution)/shard_map/ppermute | solution.py:31
  14.2 24.1 %collective-permute-start.4 = (f32[4,110,128]{2,0,1:T(4,128)S(1)}, f32[4,110,128]{2,0,1:T(4,128)S(1)}, u32[]{:S(2)}, u32[]{:S(2)}) collective-permute-start(f32[4,110,128]{2,0,1:T(4,128)S(1)} %get-tuple-element.150), channel_id=1, source_target_pairs={{2,0},{3,1},{4,2},{5,3},{6,4},{7,5},{8,6},{9,7},{10,8},{11,9},{12,... | collective-permute-start | bytes 675848 | tf_op jit(solution)/shard_map/ppermute | solution.py:31
  18.8 19.5 %collective-permute-start = (f32[4,128]{1,0:T(4,128)S(1)}, f32[4,128]{1,0:T(4,128)S(1)}, u32[]{:S(2)}, u32[]{:S(2)}) collective-permute-start(f32[4,128]{1,0:T(4,128)S(1)} %get-tuple-element.153), channel_id=1, source_target_pairs={{0,256},{64,320},{128,384},{192,448},{256,0},{320,64},{384,128},{4... | collective-permute-start | bytes 6152 | tf_op jit(solution)/shard_map/ppermute | solution.py:31
  38.3 8.5 %copy-start.1 = (f32[4,110,128]{2,0,1:T(4,128)}, f32[4,110,128]{2,0,1:T(4,128)S(1)}, u32[]{:S(2)}) copy-start(f32[4,110,128]{2,0,1:T(4,128)S(1)} %collective-permute-done.3) | copy-start | bytes 675844
  38.3 8.4 %copy-start = (f32[4,110,128]{2,0,1:T(4,128)}, f32[4,110,128]{2,0,1:T(4,128)S(1)}, u32[]{:S(2)}) copy-start(f32[4,110,128]{2,0,1:T(4,128)S(1)} %collective-permute-done.4) | copy-start | bytes 675844
  38.7 23.3 %collective-permute-start.5 = (f32[4,218,128]{2,0,1:T(4,128)S(1)}, f32[4,218,128]{2,0,1:T(4,128)S(1)}, u32[]{:S(2)}, u32[]{:S(2)}) collective-permute-start(f32[4,218,128]{2,0,1:T(4,128)S(1)} %pad_maximum_fusion.10), channel_id=1, source_target_pairs={{0,64},{64,128},{128,192},{192,256},{256,320},{320,384},{384,448},... | collective-permute-start | bytes 1339400 | tf_op jit(solution)/shard_map/ppermute | solution.py:31
  38.7 23.2 %collective-permute-start.6 = (f32[4,218,128]{2,0,1:T(4,128)S(1)}, f32[4,218,128]{2,0,1:T(4,128)S(1)}, u32[]{:S(2)}, u32[]{:S(2)}) collective-permute-start(f32[4,218,128]{2,0,1:T(4,128)S(1)} %pad_maximum_fusion.10), channel_id=1, source_target_pairs={{0,128},{64,192},{128,256},{192,320},{256,384},{320,448},{384,0},{... | collective-permute-start | bytes 1339400 | tf_op jit(solution)/shard_map/ppermute | solution.py:31
  42.7 19.5 %collective-permute-start.7 = (f32[4,218,128]{2,0,1:T(4,128)S(1)}, f32[4,218,128]{2,0,1:T(4,128)S(1)}, u32[]{:S(2)}, u32[]{:S(2)}) collective-permute-start(f32[4,218,128]{2,0,1:T(4,128)S(1)} %pad_maximum_fusion.10), channel_id=1, source_target_pairs={{0,448},{64,0},{128,64},{192,128},{256,192},{320,256},{384,320},{4... | collective-permute-start | bytes 1339400 | tf_op jit(solution)/shard_map/ppermute | solution.py:31
  44.2 17.7 %collective-permute-start.8 = (f32[4,218,128]{2,0,1:T(4,128)S(1)}, f32[4,218,128]{2,0,1:T(4,128)S(1)}, u32[]{:S(2)}, u32[]{:S(2)}) collective-permute-start(f32[4,218,128]{2,0,1:T(4,128)S(1)} %pad_maximum_fusion.10), channel_id=1, source_target_pairs={{0,384},{64,448},{128,0},{192,64},{256,128},{320,192},{384,256},{4... | collective-permute-start | bytes 1339400 | tf_op jit(solution)/shard_map/ppermute | solution.py:31
  51.9 0.9 %slice-start = ((f32[4,110,128]{2,0,1:T(4,128)}), f32[4,108,128]{2,0,1:T(4,128)S(1)}, s32[]{:S(2)}) async-start(f32[4,110,128]{2,0,1:T(4,128)} %copy-done), calls=%async_computation | async-start | bytes 442368 | tf_op jit(solution)/shard_map/slice | solution.py:291
  51.9 1.0 %slice-start.1 = ((f32[4,110,128]{2,0,1:T(4,128)}), f32[4,108,128]{2,0,1:T(4,128)S(1)}, s32[]{:S(2)}) async-start(f32[4,110,128]{2,0,1:T(4,128)} %copy-done.1), calls=%async_computation.1 | async-start | bytes 442368 | tf_op jit(solution)/shard_map/slice | solution.py:291
  62.3 0.7 copy-start.5
  62.3 0.7 copy-start.6
